TPU v7x, 128 devices: a whole 4x4x4 slice. The times are simulated.
128 devices in a mesh: tm: 32 (over x, z_hi, y), qband: 4 (over z_lo, core).
Axes of the slice: x: 4, y: 4, z: 4 (z_hi: 2, z_lo: 2; z = z_hi * 2 + z_lo), core: 2. Of those that a mesh axis runs over, the one named last changes fastest.
Arguments:
- frames: bfloat16 [128, 1024, 1024], P(('tm', 'qband')), may hold values from -8 to 8
- lag_list: int32 [16], replicated, may hold values from 1 to 64, as said below
- band_index: int32 [1024, 1], P(('tm', 'qband')), may hold values from 0 to 63
- decay_rates: float32 [64, 1024], P('tm', 'qband'), may hold values from 0.002 to 1
Outputs:
- structure: float32 [16, 1024, 1024], P(None, ('tm', 'qband'))
- weights: float32 [64, 1024], P('tm', 'qband')
Inputs may be any that keep to these rules, and one draw needn't show every extreme that they name: `lag_list`: 16 different lags, the largest exactly 64. `band_index`: every band has at least one row.
All inputs are finite; a program needn't handle non-finite values.
Results may differ from a plain program's by a relative error of at most 0.0018.
Values may be sent and summed in bfloat16 or wider, within the bound.
No kernel may reach another device: no remote copies, remote signals or barrier semaphores. Data moves between devices by JAX's collectives and lax.ppermute only.
A program may use at most 128 MiB of HBM per device.

v0:
```python
import math

import jax
import jax.numpy as jnp
from jax import lax
from jax.sharding import PartitionSpec as P

BINS = 1024
ITERS = 64


def dft_table(length):
    positions = jnp.arange(length, dtype=jnp.int32)
    phase_index = positions[:, None] * positions[None, :] % length
    folded = jnp.minimum(phase_index, length - phase_index)
    sign_factor = jnp.where(phase_index * 2 > length, -1.0, 1.0).astype(jnp.float32)
    angles = folded.astype(jnp.float32) * (2.0 * math.pi / length)
    factor = 1.0 / math.sqrt(length)
    return jnp.concatenate(
        [jnp.cos(angles) * factor, -sign_factor * jnp.sin(angles) * factor], axis=1
    ).astype(jnp.bfloat16)


def structure_block(spectrum_block, lag_list):
    frames_all = spectrum_block.shape[2]
    padded = jnp.concatenate([spectrum_block, jnp.zeros_like(spectrum_block)], axis=2)
    time_index = jnp.arange(frames_all, dtype=jnp.int32)

    def one_lag(lag_value):
        shifted = lax.dynamic_slice_in_dim(padded, lag_value, frames_all, 2)
        difference = shifted.astype(jnp.float32) - spectrum_block.astype(jnp.float32)
        squared = difference[0] * difference[0] + difference[1] * difference[1]
        in_range = (time_index < frames_all - lag_value).astype(jnp.float32)
        summed = jnp.sum(squared * in_range[None, :, None], axis=1)
        return summed / (frames_all - lag_value).astype(jnp.float32)

    return lax.map(one_lag, lag_list)


def kernel_panel(decay_rates, lag_list):
    lag_values = lag_list.astype(jnp.float32)
    return (1.0 - jnp.exp(-decay_rates[:, None, :] * lag_values[None, :, None])) / BINS


def descend(kernel, target, step_size, weights, combine):
    partial_value = jnp.einsum("blk,bk->bl", kernel, weights, precision=lax.Precision.HIGHEST)
    residual = combine(partial_value) - target
    gradient = jnp.einsum("blk,bl->bk", kernel, residual, precision=lax.Precision.HIGHEST)
    return jnp.maximum(weights - step_size[:, None] * gradient, 0.0)


def on_device(frames, lag_list, band_index, decay_rates):
    frames_dev, pixels = (frames.shape[0], frames.shape[1])
    table = dft_table(pixels)
    row_transform = jnp.einsum("xk,tyx->kty", table, frames, preferred_element_type=jnp.float32)
    row_transform = row_transform.reshape(2, pixels, frames_dev, pixels).astype(jnp.bfloat16)
    products = jnp.einsum("ckty,yj->cktj", row_transform, table, preferred_element_type=jnp.float32)
    spec_real = products[0, :, :, :pixels] - products[1, :, :, pixels:]
    spec_imag = products[0, :, :, pixels:] + products[1, :, :, :pixels]
    spectrum = jnp.stack([spec_real, spec_imag]).astype(jnp.bfloat16)
    structure = structure_block(
        lax.all_to_all(spectrum, ("tm", "qband"), split_axis=1, concat_axis=2, tiled=True), lag_list
    )
    bands_dev = decay_rates.shape[0]
    bands_total = bands_dev * lax.axis_size("tm")
    row_sums = jnp.sum(structure, axis=2)
    band_ids = jnp.arange(bands_total, dtype=jnp.int32)
    one_hot = (band_index[:, 0][None, :] == band_ids[:, None]).astype(jnp.float32)
    partial_totals = jnp.dot(one_hot, row_sums.T, precision=lax.Precision.HIGHEST)
    partial_counts = jnp.sum(one_hot, axis=1)
    totals, counts = lax.psum((partial_totals, partial_counts), ("tm", "qband"))
    band_mean = totals / (counts[:, None] * pixels)
    target = lax.dynamic_slice_in_dim(band_mean, lax.axis_index("tm") * bands_dev, bands_dev, 0)
    columns = decay_rates.shape[1]
    kernel = kernel_panel(decay_rates, lag_list)
    norm_part = jnp.sum(kernel * kernel, axis=(1, 2))
    step_size = 1.0 / lax.psum(norm_part, "qband")

    def combine_bins(partial_value):
        return lax.psum(partial_value, "qband")

    def iterate(counter, weights):
        return descend(kernel, target, step_size, weights, combine_bins)

    weights = lax.fori_loop(0, ITERS, iterate, jnp.zeros((bands_dev, columns), jnp.float32))
    return (structure, weights)


def solution(mesh):
    placed = (P(("tm", "qband"), None, None), P(), P(("tm", "qband"), None), P("tm", "qband"))
    return jax.shard_map(
        on_device,
        mesh=mesh,
        in_specs=placed,
        out_specs=(P(None, ("tm", "qband"), None), P("tm", "qband")),
        check_vma=False,
    )
```

profile of v0, /device:TPU:1, one launch (start us, length us, event | category | flops | bytes accessed | tf_op | source)
XLA Modules:
  0.0 888.4 jit_solution(16568552919354214911)
XLA Ops:
  0.6 18.3 %multiply_convert_fusion = (bf16[1024,1024]{1,0:T(8,128)(2,1)S(1)}, bf16[1024,1024]{1,0:T(8,128)(2,1)S(1)}) fusion(), kind=kLoop, calls=%fused_computation.49 | loop fusion | flops 26214400 | bytes 4194304 | tf_op jit(solution)/shard_map/convert.3
  29.7 22.7 %convolution_bitcast_fusion = f32[2,1024,1,2048]{3,1,0,2:T(8,128)} fusion(bf16[1024,1024]{1,0:T(8,128)(2,1)} %copy-done.3, bf16[1024,1024]{1,0:T(8,128)(2,1)} %copy-done.4, bf16[2,1024,1024]{2,1,0:T(8,128)(2,1)} %bitcast.66, bf16[1,1024,1024]{2,1,0:T(8,128)(2,1)S(1)} %copy-done), kind=kOutput, calls=%fused_computation.32 | convolution fusion | flops 12895387648 | bytes 27262976 | tf_op jit(solution)/shard_map/ckty,yj->cktj/dot_general | solution.py:57
  65.7 11.9 %all-to-all-start = ((bf16[2,1024,1,1024]{3,0,2,1:T(2,128)(2,1)}), bf16[2,1024,1,1024]{3,0,2,1:T(2,128)(2,1)}, u32[]{:S(2)}, u32[]{:S(2)}) async-start(bf16[2,1024,1,1024]{3,0,2,1:T(2,128)(2,1)} %copy.10), calls=%async_computation | async-start | bytes 8388608 | tf_op jit(solution)/shard_map/all_to_all | solution.py:62
  77.9 25.1 %psum.28 = f32[2]{0:T(128)S(1)} all-reduce(f32[2]{0:T(128)S(1)} %multiply_reduce_fusion), channel_id=1, replica_groups=mesh['tm'=32,'qband'=4] {'qband'}, use_global_device_ids=true, to_apply=%region_8.9 | all-reduce | flops 2 | bytes 16 | tf_op jit(solution)/shard_map/psum | solution.py:77
  103.1 27.1 %all-to-all-done = bf16[2,1024,1,1024]{3,0,2,1:T(2,128)(2,1)} async-done(((bf16[2,1024,1,1024]{3,0,2,1:T(2,128)(2,1)}), bf16[2,1024,1,1024]{3,0,2,1:T(2,128)(2,1)}, u32[]{:S(2)}, u32[]{:S(2)}) %all-to-all-start) | async-done | bytes 4194336 | tf_op jit(solution)/shard_map/all_to_all | solution.py:62
  139.1 267.7 %while.22 = (s32[]{:T(128)}, f32[16,8,1024]{2,1,0:T(8,128)S(1)}, s32[16]{0:T(128)S(1)}, bf16[2,8,256,1024]{3,2,1,0:T(8,128)(2,1)}, bf16[2,8,128,1024]{3,2,1,0:T(...) while((s32[]{:T(128)}, f32[16,8,1024]{2,1,0:T(8,128)S(1)}, s32[16]{0:T(128)S(1)}, ...), condition=%wide.region_2.3_spmd.clone, body=%wide.region_0.2_spmd.clone.sunk | while | flops 11534599 | bytes 25265328 | solution.py:37
  141.6 8.9 convert_subtract_fusion.2
  158.4 8.9 convert_subtract_fusion.2
  175.1 8.9 convert_subtract_fusion.2
  191.8 8.9 convert_subtract_fusion.2
  208.6 8.9 convert_subtract_fusion.2
  225.3 8.9 convert_subtract_fusion.2
  242.0 8.9 convert_subtract_fusion.2
  258.7 8.9 convert_subtract_fusion.2
  275.5 8.9 convert_subtract_fusion.2
  292.2 8.9 convert_subtract_fusion.2
  308.9 8.9 convert_subtract_fusion.2
  325.7 8.9 convert_subtract_fusion.2
  342.4 8.9 convert_subtract_fusion.2
  359.1 8.9 convert_subtract_fusion.2
  375.9 8.9 convert_subtract_fusion.2
  392.6 8.9 convert_subtract_fusion.2
  407.2 64.3 %all-reduce.1 = (f32[64,16]{1,0:T(8,128)S(1)}, f32[64]{0:T(128)S(1)}) all-reduce(f32[64,16]{1,0:T(8,128)S(1)} %fusion.44, f32[64]{0:T(128)S(1)} %convert_reduce_fusion), channel_id=1, replica_groups=mesh['tm'=32,'qband'=4] {'tm','qband'}, use_global_device_ids=true, to_apply=%region_4.5 | all-reduce | flops 1088 | bytes 8704 | tf_op jit(solution)/shard_map/psum | solution.py:71
  471.6 416.2 %while.23 = (s32[]{:T(128)}, f32[2,256]{1,0:T(2,128)S(1)}, f32[2]{0:T(128)S(1)}, f32[2,16]{1,0:T(2,128)S(1)}, f32[16]{0:T(128)S(1)}, /*index=5*/f32[2,256]{1,0:T(2,128)S(1)}, s32[]{:T(128)}, s32[]{:T(128)}) while((s32[]{:T(128)}, f32[2,256]{1,0:T(2,128)S(1)}, f32[2]{0:T(128)S(1)}, f32[2,16]{1,0:T(2,128)S(1)}, f32[16]{0:T(128)S(1)}, ...), condition=%wide.region_11.12_spmd.clone, body=%wide.region_9.11_spmd.clone.sunk | while | flops 248387 | bytes 19560 | solution.py:85
  (487 shorter events, 533.8 us)
Async XLA Ops:
  0.6 29.1 %copy-start = (bf16[1,1024,1024]{2,1,0:T(8,128)(2,1)S(1)}, bf16[1,1024,1024]{2,1,0:T(8,128)(2,1)}, u32[]{:S(2)}) copy-start(bf16[1,1024,1024]{2,1,0:T(8,128)(2,1)} %param.8) | copy-start | bytes 6291460
  19.0 1.3 copy-start.3
  19.0 2.0 copy-start.4
  65.7 12.0 %copy-start.7 = (f32[2,256]{1,0:T(2,128)S(1)}, f32[2,256]{1,0:T(2,128)}, u32[]{:S(2)}) copy-start(f32[2,256]{1,0:T(2,128)} %param.11) | copy-start | bytes 6148
  65.7 12.0 %copy-start.8 = (s32[16]{0:T(128)S(1)}, s32[16]{0:T(128)}, u32[]{:S(2)}) copy-start(s32[16]{0:T(128)} %param.9) | copy-start | bytes 196
  65.7 37.3 %copy-start.9 = (s32[8,1]{0,1:T(1,128)S(1)}, s32[8,1]{0,1:T(1,128)}, u32[]{:S(2)}) copy-start(s32[8,1]{0,1:T(1,128)} %param.10) | copy-start | bytes 100
  65.7 64.4 %all-to-all-start = ((bf16[2,1024,1,1024]{3,0,2,1:T(2,128)(2,1)}), bf16[2,1024,1,1024]{3,0,2,1:T(2,128)(2,1)}, u32[]{:S(2)}, u32[]{:S(2)}) async-start(bf16[2,1024,1,1024]{3,0,2,1:T(2,128)(2,1)} %copy.10), calls=%async_computation | async-start | bytes 8388608 | tf_op jit(solution)/shard_map/all_to_all | solution.py:62
  134.6 4.5 copy-start.2
  406.8 481.1 %copy-start.5 = (f32[16,8,1024]{2,1,0:T(8,128)}, f32[16,8,1024]{2,1,0:T(8,128)S(1)}, u32[]{:S(2)}) copy-start(f32[16,8,1024]{2,1,0:T(8,128)S(1)} %get-tuple-element.59) | copy-start | bytes 1572868
  406.8 481.6 %copy-start.1 = (bf16[1,1024,1024]{2,1,0:T(8,128)(2,1)S(1)}, bf16[1,1024,1024]{2,1,0:T(8,128)(2,1)}, u32[]{:S(2)}) copy-start(bf16[1,1024,1024]{2,1,0:T(8,128)(2,1)} %param.8) | copy-start | bytes 6291460
  887.8 0.6 copy-start.6
where the time goes:
time: 891 us; the launch traced here: 888 us
  blocking collectives  471 us (53%)
  other arithmetic  250 us (28%)
  matrix products  51.5 us (6%)
  loops' own time  42.4 us (5%)
  local copies, waits for them, and re-layouts  33.7 us (4%)
  waiting for transfers between devices  27.1 us (3%)
  starting transfers between devices  11.9 us (1%)
    psum x64, blocking collectives, combine_bins(): return lax.psum(partial_value, 'qband')  381 us
    sub x16, other arithmetic, one_lag(): shifted.astype(jnp.float32) - spectrum_block.astype(jnp.float32)  142 us
    reduce_sum x16, other arithmetic, one_lag(): summed = jnp.sum(squared * in_range[None, :, None], axis=1)  73.8 us
    psum x1, blocking collectives, on_device(): totals, counts = lax.psum((partial_totals, partial_counts), ('tm', 'qband'))  64.3 us
    another operation x1, loops' own time, structure_block(): return lax.map(one_lag, lag_list)  42.2 us
    all_to_all x1, waiting for transfers between devices, on_device(): lax.all_to_all(spectrum, ('tm', 'qband'), split_axis=1, concat_axis=2, ti...  27.1 us
    psum x1, blocking collectives, on_device(): step_size = 1.0 / lax.psum(norm_part, 'qband')  25.1 us
    another operation x2, other arithmetic  24.9 us
  transfers between devices with their start and end apart: 1, of which 1 were waited for; matrix products, arithmetic and copies ran while one was open for 0% of the time, Pallas kernels for 0%

commit v1 on v0

--- a/solution.py
+++ b/solution.py
@@ -4,6 +4,8 @@
 import jax.numpy as jnp
 from jax import lax
 from jax.sharding import PartitionSpec as P
+from jax.experimental import pallas as pl
+from jax.experimental.pallas import tpu as pltpu
 
 BINS = 1024
 ITERS = 64
@@ -72,18 +74,38 @@
     band_mean = totals / (counts[:, None] * pixels)
     target = lax.dynamic_slice_in_dim(band_mean, lax.axis_index("tm") * bands_dev, bands_dev, 0)
     columns = decay_rates.shape[1]
-    kernel = kernel_panel(decay_rates, lag_list)
-    norm_part = jnp.sum(kernel * kernel, axis=(1, 2))
-    step_size = 1.0 / lax.psum(norm_part, "qband")
+    all_rates = lax.all_gather(decay_rates, "qband", axis=1, tiled=True)
+    kernel = kernel_panel(all_rates, lag_list)
+    step_size = 1.0 / jnp.sum(kernel * kernel, axis=(1, 2))
+    weights = fit_bands(kernel, target, step_size)
+    weights = lax.dynamic_slice_in_dim(weights, lax.axis_index("qband") * columns, columns, 1)
+    return (structure, weights)
 
-    def combine_bins(partial_value):
-        return lax.psum(partial_value, "qband")
 
-    def iterate(counter, weights):
-        return descend(kernel, target, step_size, weights, combine_bins)
+def fit_kernel(k_ref, tgt_ref, step_ref, w_ref):
+    for b in range(k_ref.shape[0]):
+        panel = k_ref[b]
+        tgt = tgt_ref[b][:, 0:1]
+        step = step_ref[b]
 
-    weights = lax.fori_loop(0, ITERS, iterate, jnp.zeros((bands_dev, columns), jnp.float32))
-    return (structure, weights)
+        def body(i, w):
+            predicted = jnp.sum(panel * w, axis=1, keepdims=True)
+            residual = predicted - tgt
+            gradient = jnp.sum(panel * residual, axis=0, keepdims=True)
+            return jnp.maximum(w - step * gradient, 0.0)
+
+        w_ref[b] = lax.fori_loop(0, ITERS, body, jnp.zeros(step.shape, jnp.float32))
+
+
+def fit_bands(kernel, target, step_size):
+    bands, lags, bins = kernel.shape
+    tgt = jnp.broadcast_to(target[:, :, None], (bands, lags, 128))
+    step = jnp.broadcast_to(step_size[:, None, None], (bands, 1, bins))
+    out = pl.pallas_call(
+        fit_kernel,
+        out_shape=jax.ShapeDtypeStruct((bands, 1, bins), jnp.float32),
+    )(kernel, tgt, step)
+    return out[:, 0, :]
 
 
 def solution(mesh):

time: 891 us -> 500 us (0.56)
  blocking collectives: 471 us -> 89.6 us
  matrix products: 51.5 us -> 23 us
  Pallas kernels: 0 us -> 25 us
    psum x65 -> x0, blocking collectives: 406 us -> none  [the longest x64 381 us: combine_bins(): return lax.psum(partial_value, 'qband')]
    dot_general x128 -> x0, matrix products: 28.5 us -> none  [the longest x64 14.6 us: descend(): jnp.einsum('blk,bk->bl', kernel, weights, precision=lax.Precision.HIGHEST)]
    all_gather x0 -> x1, blocking collectives: none -> 25.3 us  [on_device(): all_rates = lax.all_gather(decay_rates, 'qband', axis=1, tiled=True)]
    pallas_call x0 -> x1, Pallas kernels: none -> 25 us  [fit_bands(): pl.pallas_call(fit_kernel, out_shape=jax.ShapeDtypeStruct((bands, 1, bins...]
where the time goes in v1:
time: 500 us; the launch traced here: 499 us
  other arithmetic  245 us (49%)
  blocking collectives  89.6 us (18%)
  loops' own time  42.2 us (8%)
  local copies, waits for them, and re-layouts  35.7 us (7%)
  waiting for transfers between devices  26.3 us (5%)
  Pallas kernels  25 us (5%)
  matrix products  23 us (5%)
  starting transfers between devices  11.9 us (2%)
    sub x16, other arithmetic, one_lag(): shifted.astype(jnp.float32) - spectrum_block.astype(jnp.float32)  142 us
    reduce_sum x16, other arithmetic, one_lag(): summed = jnp.sum(squared * in_range[None, :, None], axis=1)  73.8 us
    psum x1, blocking collectives, on_device(): totals, counts = lax.psum((partial_totals, partial_counts), ('tm', 'qband'))  64.3 us
    another operation x1, loops' own time, structure_block(): return lax.map(one_lag, lag_list)  42.2 us
    all_to_all x1, waiting for transfers between devices, on_device(): lax.all_to_all(spectrum, ('tm', 'qband'), split_axis=1, concat_axis=2, ti...  26.3 us
    all_gather x1, blocking collectives, on_device(): all_rates = lax.all_gather(decay_rates, 'qband', axis=1, tiled=True)  25.3 us
    pallas_call x1, Pallas kernels, fit_bands(): pl.pallas_call(fit_kernel, out_shape=jax.ShapeDtypeStruct((bands, 1, bins...  25 us
    another operation x2, other arithmetic  24.9 us
  transfers between devices with their start and end apart: 1, of which 1 were waited for; matrix products, arithmetic and copies ran while one was open for 0% of the time, Pallas kernels for 0%

profile of v1, /device:TPU:1, one launch (start us, length us, event | category | flops | bytes accessed | tf_op | source)
XLA Modules:
  0.0 499.4 jit_solution(2487173477283972447)
XLA Ops:
  0.6 18.3 %multiply_convert_fusion = (bf16[1024,1024]{1,0:T(8,128)(2,1)S(1)}, bf16[1024,1024]{1,0:T(8,128)(2,1)S(1)}) fusion(), kind=kLoop, calls=%fused_computation.27 | loop fusion | flops 26214400 | bytes 4194304 | tf_op jit(solution)/shard_map/convert.3
  29.7 22.7 %convolution_bitcast_fusion = f32[2,1024,1,2048]{3,1,0,2:T(8,128)} fusion(bf16[1024,1024]{1,0:T(8,128)(2,1)} %copy-done.3, bf16[1024,1024]{1,0:T(8,128)(2,1)} %copy-done.4, bf16[2,1024,1024]{2,1,0:T(8,128)(2,1)} %bitcast.45, bf16[1,1024,1024]{2,1,0:T(8,128)(2,1)S(1)} %copy-done), kind=kOutput, calls=%fused_computation.10 | convolution fusion | flops 12895387648 | bytes 27262976 | tf_op jit(solution)/shard_map/ckty,yj->cktj/dot_general | solution.py:59
  65.7 11.9 %all-to-all-start = ((bf16[2,1024,1,1024]{3,0,2,1:T(2,128)(2,1)}), bf16[2,1024,1,1024]{3,0,2,1:T(2,128)(2,1)}, u32[]{:S(2)}, u32[]{:S(2)}) async-start(bf16[2,1024,1,1024]{3,0,2,1:T(2,128)(2,1)} %copy.10), calls=%async_computation | async-start | bytes 8388608 | tf_op jit(solution)/shard_map/all_to_all | solution.py:64
  77.7 25.3 %all_gather.3 = f32[2,1024]{1,0:T(2,128)S(1)} all-gather(f32[2,256]{1,0:T(2,128)S(1)} %copy-done.6), channel_id=1, replica_groups=mesh['tm'=32,'qband'=4] {'qband'}, dimensions={1}, use_global_device_ids=true | all-gather | bytes 10240 | tf_op jit(solution)/shard_map/all_gather | solution.py:77
  103.8 26.3 %all-to-all-done = bf16[2,1024,1,1024]{3,0,2,1:T(2,128)(2,1)} async-done(((bf16[2,1024,1,1024]{3,0,2,1:T(2,128)(2,1)}), bf16[2,1024,1,1024]{3,0,2,1:T(2,128)(2,1)}, u32[]{:S(2)}, u32[]{:S(2)}) %all-to-all-start) | async-done | bytes 4194336 | tf_op jit(solution)/shard_map/all_to_all | solution.py:64
  139.1 267.7 %while.11 = (s32[]{:T(128)}, f32[16,8,1024]{2,1,0:T(8,128)S(1)}, s32[16]{0:T(128)S(1)}, bf16[2,8,256,1024]{3,2,1,0:T(8,128)(2,1)}, bf16[2,8,128,1024]{3,2,1,0:T(...) while((s32[]{:T(128)}, f32[16,8,1024]{2,1,0:T(8,128)S(1)}, s32[16]{0:T(128)S(1)}, ...), condition=%wide.region_2.3_spmd.clone, body=%wide.region_0.2_spmd.clone.sunk | while | flops 11534599 | bytes 25265328 | solution.py:39
  141.6 8.9 %convert_subtract_fusion.2 = f32[2,8,128,1024]{3,2,1,0:T(8,128)} fusion(bf16[2,8,128,1024]{3,2,1,0:T(8,128)(2,1)} %get-tuple-element.118, bf16[2,8,256,1024]{3,2,1,0:T(8,128)(2,1)} %get-tuple-element.117, s32[]{:T(128)S(6)} %select_n.34), kind=kLoop, calls=%fused_computation.1.clone.1 | loop fusion | flops 6291456 | bytes 16777220 | tf_op jit(solution)/shard_map/while/body/eval_jaxpr/sub | solution.py:33
  158.3 8.9 %convert_subtract_fusion.2 = f32[2,8,128,1024]{3,2,1,0:T(8,128)} fusion(bf16[2,8,128,1024]{3,2,1,0:T(8,128)(2,1)} %get-tuple-element.118, bf16[2,8,256,1024]{3,2,1,0:T(8,128)(2,1)} %get-tuple-element.117, s32[]{:T(128)S(6)} %select_n.34), kind=kLoop, calls=%fused_computation.1.clone.1 | loop fusion | flops 6291456 | bytes 16777220 | tf_op jit(solution)/shard_map/while/body/eval_jaxpr/sub | solution.py:33
  175.1 8.9 %convert_subtract_fusion.2 = f32[2,8,128,1024]{3,2,1,0:T(8,128)} fusion(bf16[2,8,128,1024]{3,2,1,0:T(8,128)(2,1)} %get-tuple-element.118, bf16[2,8,256,1024]{3,2,1,0:T(8,128)(2,1)} %get-tuple-element.117, s32[]{:T(128)S(6)} %select_n.34), kind=kLoop, calls=%fused_computation.1.clone.1 | loop fusion | flops 6291456 | bytes 16777220 | tf_op jit(solution)/shard_map/while/body/eval_jaxpr/sub | solution.py:33
  191.8 8.9 %convert_subtract_fusion.2 = f32[2,8,128,1024]{3,2,1,0:T(8,128)} fusion(bf16[2,8,128,1024]{3,2,1,0:T(8,128)(2,1)} %get-tuple-element.118, bf16[2,8,256,1024]{3,2,1,0:T(8,128)(2,1)} %get-tuple-element.117, s32[]{:T(128)S(6)} %select_n.34), kind=kLoop, calls=%fused_computation.1.clone.1 | loop fusion | flops 6291456 | bytes 16777220 | tf_op jit(solution)/shard_map/while/body/eval_jaxpr/sub | solution.py:33
  208.6 8.9 %convert_subtract_fusion.2 = f32[2,8,128,1024]{3,2,1,0:T(8,128)} fusion(bf16[2,8,128,1024]{3,2,1,0:T(8,128)(2,1)} %get-tuple-element.118, bf16[2,8,256,1024]{3,2,1,0:T(8,128)(2,1)} %get-tuple-element.117, s32[]{:T(128)S(6)} %select_n.34), kind=kLoop, calls=%fused_computation.1.clone.1 | loop fusion | flops 6291456 | bytes 16777220 | tf_op jit(solution)/shard_map/while/body/eval_jaxpr/sub | solution.py:33
  225.3 8.9 %convert_subtract_fusion.2 = f32[2,8,128,1024]{3,2,1,0:T(8,128)} fusion(bf16[2,8,128,1024]{3,2,1,0:T(8,128)(2,1)} %get-tuple-element.118, bf16[2,8,256,1024]{3,2,1,0:T(8,128)(2,1)} %get-tuple-element.117, s32[]{:T(128)S(6)} %select_n.34), kind=kLoop, calls=%fused_computation.1.clone.1 | loop fusion | flops 6291456 | bytes 16777220 | tf_op jit(solution)/shard_map/while/body/eval_jaxpr/sub | solution.py:33
  242.0 8.9 %convert_subtract_fusion.2 = f32[2,8,128,1024]{3,2,1,0:T(8,128)} fusion(bf16[2,8,128,1024]{3,2,1,0:T(8,128)(2,1)} %get-tuple-element.118, bf16[2,8,256,1024]{3,2,1,0:T(8,128)(2,1)} %get-tuple-element.117, s32[]{:T(128)S(6)} %select_n.34), kind=kLoop, calls=%fused_computation.1.clone.1 | loop fusion | flops 6291456 | bytes 16777220 | tf_op jit(solution)/shard_map/while/body/eval_jaxpr/sub | solution.py:33
  258.8 8.9 %convert_subtract_fusion.2 = f32[2,8,128,1024]{3,2,1,0:T(8,128)} fusion(bf16[2,8,128,1024]{3,2,1,0:T(8,128)(2,1)} %get-tuple-element.118, bf16[2,8,256,1024]{3,2,1,0:T(8,128)(2,1)} %get-tuple-element.117, s32[]{:T(128)S(6)} %select_n.34), kind=kLoop, calls=%fused_computation.1.clone.1 | loop fusion | flops 6291456 | bytes 16777220 | tf_op jit(solution)/shard_map/while/body/eval_jaxpr/sub | solution.py:33
  275.5 8.9 %convert_subtract_fusion.2 = f32[2,8,128,1024]{3,2,1,0:T(8,128)} fusion(bf16[2,8,128,1024]{3,2,1,0:T(8,128)(2,1)} %get-tuple-element.118, bf16[2,8,256,1024]{3,2,1,0:T(8,128)(2,1)} %get-tuple-element.117, s32[]{:T(128)S(6)} %select_n.34), kind=kLoop, calls=%fused_computation.1.clone.1 | loop fusion | flops 6291456 | bytes 16777220 | tf_op jit(solution)/shard_map/while/body/eval_jaxpr/sub | solution.py:33
  292.2 8.9 %convert_subtract_fusion.2 = f32[2,8,128,1024]{3,2,1,0:T(8,128)} fusion(bf16[2,8,128,1024]{3,2,1,0:T(8,128)(2,1)} %get-tuple-element.118, bf16[2,8,256,1024]{3,2,1,0:T(8,128)(2,1)} %get-tuple-element.117, s32[]{:T(128)S(6)} %select_n.34), kind=kLoop, calls=%fused_computation.1.clone.1 | loop fusion | flops 6291456 | bytes 16777220 | tf_op jit(solution)/shard_map/while/body/eval_jaxpr/sub | solution.py:33
  309.0 8.9 %convert_subtract_fusion.2 = f32[2,8,128,1024]{3,2,1,0:T(8,128)} fusion(bf16[2,8,128,1024]{3,2,1,0:T(8,128)(2,1)} %get-tuple-element.118, bf16[2,8,256,1024]{3,2,1,0:T(8,128)(2,1)} %get-tuple-element.117, s32[]{:T(128)S(6)} %select_n.34), kind=kLoop, calls=%fused_computation.1.clone.1 | loop fusion | flops 6291456 | bytes 16777220 | tf_op jit(solution)/shard_map/while/body/eval_jaxpr/sub | solution.py:33
  325.7 8.9 %convert_subtract_fusion.2 = f32[2,8,128,1024]{3,2,1,0:T(8,128)} fusion(bf16[2,8,128,1024]{3,2,1,0:T(8,128)(2,1)} %get-tuple-element.118, bf16[2,8,256,1024]{3,2,1,0:T(8,128)(2,1)} %get-tuple-element.117, s32[]{:T(128)S(6)} %select_n.34), kind=kLoop, calls=%fused_computation.1.clone.1 | loop fusion | flops 6291456 | bytes 16777220 | tf_op jit(solution)/shard_map/while/body/eval_jaxpr/sub | solution.py:33
  342.4 8.9 %convert_subtract_fusion.2 = f32[2,8,128,1024]{3,2,1,0:T(8,128)} fusion(bf16[2,8,128,1024]{3,2,1,0:T(8,128)(2,1)} %get-tuple-element.118, bf16[2,8,256,1024]{3,2,1,0:T(8,128)(2,1)} %get-tuple-element.117, s32[]{:T(128)S(6)} %select_n.34), kind=kLoop, calls=%fused_computation.1.clone.1 | loop fusion | flops 6291456 | bytes 16777220 | tf_op jit(solution)/shard_map/while/body/eval_jaxpr/sub | solution.py:33
  359.2 8.9 %convert_subtract_fusion.2 = f32[2,8,128,1024]{3,2,1,0:T(8,128)} fusion(bf16[2,8,128,1024]{3,2,1,0:T(8,128)(2,1)} %get-tuple-element.118, bf16[2,8,256,1024]{3,2,1,0:T(8,128)(2,1)} %get-tuple-element.117, s32[]{:T(128)S(6)} %select_n.34), kind=kLoop, calls=%fused_computation.1.clone.1 | loop fusion | flops 6291456 | bytes 16777220 | tf_op jit(solution)/shard_map/while/body/eval_jaxpr/sub | solution.py:33
  375.9 8.9 %convert_subtract_fusion.2 = f32[2,8,128,1024]{3,2,1,0:T(8,128)} fusion(bf16[2,8,128,1024]{3,2,1,0:T(8,128)(2,1)} %get-tuple-element.118, bf16[2,8,256,1024]{3,2,1,0:T(8,128)(2,1)} %get-tuple-element.117, s32[]{:T(128)S(6)} %select_n.34), kind=kLoop, calls=%fused_computation.1.clone.1 | loop fusion | flops 6291456 | bytes 16777220 | tf_op jit(solution)/shard_map/while/body/eval_jaxpr/sub | solution.py:33
  392.6 8.9 %convert_subtract_fusion.2 = f32[2,8,128,1024]{3,2,1,0:T(8,128)} fusion(bf16[2,8,128,1024]{3,2,1,0:T(8,128)(2,1)} %get-tuple-element.118, bf16[2,8,256,1024]{3,2,1,0:T(8,128)(2,1)} %get-tuple-element.117, s32[]{:T(128)S(6)} %select_n.34), kind=kLoop, calls=%fused_computation.1.clone.1 | loop fusion | flops 6291456 | bytes 16777220 | tf_op jit(solution)/shard_map/while/body/eval_jaxpr/sub | solution.py:33
  407.3 64.3 %all-reduce.1 = (f32[64,16]{1,0:T(8,128)S(1)}, f32[64]{0:T(128)S(1)}) all-reduce(f32[64,16]{1,0:T(8,128)S(1)} %fusion.24, f32[64]{0:T(128)S(1)} %convert_reduce_fusion), channel_id=1, replica_groups=mesh['tm'=32,'qband'=4] {'tm','qband'}, use_global_device_ids=true, to_apply=%region_4.5 | all-reduce | flops 1088 | bytes 8704 | tf_op jit(solution)/shard_map/psum | solution.py:73
  473.1 25.0 %shard_map.59 = f32[2,1,1024]{2,1,0:T(1,128)} custom-call(f32[2,16,1024]{2,1,0:T(8,128)} %get-tuple-element.62.k_ref, f32[2,16,128]{2,1,0:T(8,128)} %broadcast_in_dim.20.tgt_ref, f32[2,1,1024]{2,1,0:T(1,128)} %broadcast_in_dim.21.step_ref), custom_call_target="tpu_custom_call" | custom-call | tf_op jit(solution)/shard_map/pallas_call | solution.py:104
  (104 shorter events, 120.4 us)
Async XLA Ops:
  0.6 29.1 %copy-start = (bf16[1,1024,1024]{2,1,0:T(8,128)(2,1)S(1)}, bf16[1,1024,1024]{2,1,0:T(8,128)(2,1)}, u32[]{:S(2)}) copy-start(bf16[1,1024,1024]{2,1,0:T(8,128)(2,1)} %param.6) | copy-start | bytes 6291460
  19.0 1.3 copy-start.3
  19.0 1.9 copy-start.4
  65.7 12.0 %copy-start.6 = (f32[2,256]{1,0:T(2,128)S(1)}, f32[2,256]{1,0:T(2,128)}, u32[]{:S(2)}) copy-start(f32[2,256]{1,0:T(2,128)} %param.9) | copy-start | bytes 6148
  65.7 37.3 %copy-start.7 = (s32[16]{0:T(128)S(1)}, s32[16]{0:T(128)}, u32[]{:S(2)}) copy-start(s32[16]{0:T(128)} %param.7) | copy-start | bytes 196
  65.7 37.3 %copy-start.8 = (s32[8,1]{0,1:T(1,128)S(1)}, s32[8,1]{0,1:T(1,128)}, u32[]{:S(2)}) copy-start(s32[8,1]{0,1:T(1,128)} %param.8) | copy-start | bytes 100
  65.7 64.4 %all-to-all-start = ((bf16[2,1024,1,1024]{3,0,2,1:T(2,128)(2,1)}), bf16[2,1024,1,1024]{3,0,2,1:T(2,128)(2,1)}, u32[]{:S(2)}, u32[]{:S(2)}) async-start(bf16[2,1024,1,1024]{3,0,2,1:T(2,128)(2,1)} %copy.10), calls=%async_computation | async-start | bytes 8388608 | tf_op jit(solution)/shard_map/all_to_all | solution.py:64
  134.6 4.5 copy-start.2
  406.8 92.5 %copy-start.5 = (f32[16,8,1024]{2,1,0:T(8,128)}, f32[16,8,1024]{2,1,0:T(8,128)S(1)}, u32[]{:S(2)}) copy-start(f32[16,8,1024]{2,1,0:T(8,128)S(1)} %get-tuple-element.32) | copy-start | bytes 1572868
  406.9 92.5 %copy-start.1 = (bf16[1,1024,1024]{2,1,0:T(8,128)(2,1)S(1)}, bf16[1,1024,1024]{2,1,0:T(8,128)(2,1)}, u32[]{:S(2)}) copy-start(bf16[1,1024,1024]{2,1,0:T(8,128)(2,1)} %param.6) | copy-start | bytes 6291460

commit v2 on v1

v2 whole, which is shorter than its diff:
```python
import math

import jax
import jax.numpy as jnp
from jax import lax
from jax.sharding import PartitionSpec as P
from jax.experimental import pallas as pl
from jax.experimental.pallas import tpu as pltpu

BINS = 1024
ITERS = 64


def dft_table(length):
    positions = jnp.arange(length, dtype=jnp.int32)
    phase_index = positions[:, None] * positions[None, :] % length
    folded = jnp.minimum(phase_index, length - phase_index)
    sign_factor = jnp.where(phase_index * 2 > length, -1.0, 1.0).astype(jnp.float32)
    angles = folded.astype(jnp.float32) * (2.0 * math.pi / length)
    factor = 1.0 / math.sqrt(length)
    return jnp.concatenate(
        [jnp.cos(angles) * factor, -sign_factor * jnp.sin(angles) * factor], axis=1
    ).astype(jnp.bfloat16)


def structure_kernel(lags_ref, x_ref, out_ref, x32_ref):
    frames_all = x_ref.shape[0]

    def convert(t, carry):
        x32_ref[t] = x_ref[t].astype(jnp.float32)
        return carry

    lax.fori_loop(0, frames_all, convert, 0)

    def one_lag(l, carry):
        lag = lags_ref[l]
        count = frames_all - lag

        def step(t, acc):
            d = x32_ref[t + lag] - x32_ref[t]
            return acc + d * d

        out_ref[l] = lax.fori_loop(0, count, step, jnp.zeros(x32_ref.shape[1:], jnp.float32))
        return carry

    lax.fori_loop(0, lags_ref.shape[0], one_lag, 0)


def structure_block(spectrum_block, lag_list):
    frames_all, rows, pixels = spectrum_block.shape
    nlag = lag_list.shape[0]
    summed = pl.pallas_call(
        structure_kernel,
        out_shape=jax.ShapeDtypeStruct((nlag, rows, pixels), jnp.float32),
        in_specs=[
            pl.BlockSpec(memory_space=pltpu.SMEM),
            pl.BlockSpec(memory_space=pltpu.VMEM),
        ],
        out_specs=pl.BlockSpec(memory_space=pltpu.VMEM),
        scratch_shapes=[
            pltpu.VMEM((frames_all, rows, pixels), jnp.float32),
        ],
        compiler_params=pltpu.CompilerParams(vmem_limit_bytes=40 * 1024 * 1024),
    )(lag_list, spectrum_block)
    summed = jnp.sum(summed.reshape(nlag, rows // 2, 2, pixels), axis=2)
    return summed / (frames_all - lag_list).astype(jnp.float32)[:, None, None]


def kernel_panel(decay_rates, lag_list):
    lag_values = lag_list.astype(jnp.float32)
    return (1.0 - jnp.exp(-decay_rates[:, None, :] * lag_values[None, :, None])) / BINS


def fit_kernel(k_ref, tgt_ref, step_ref, w_ref):
    for b in range(k_ref.shape[0]):
        panel = k_ref[b]
        tgt = tgt_ref[b][:, 0:1]
        step = step_ref[b]

        def body(i, w):
            predicted = jnp.sum(panel * w, axis=1, keepdims=True)
            residual = predicted - tgt
            gradient = jnp.sum(panel * residual, axis=0, keepdims=True)
            return jnp.maximum(w - step * gradient, 0.0)

        w_ref[b] = lax.fori_loop(0, ITERS, body, jnp.zeros(step.shape, jnp.float32))


def fit_bands(kernel, target, step_size):
    bands, lags, bins = kernel.shape
    tgt = jnp.broadcast_to(target[:, :, None], (bands, lags, 128))
    step = jnp.broadcast_to(step_size[:, None, None], (bands, 1, bins))
    out = pl.pallas_call(
        fit_kernel,
        out_shape=jax.ShapeDtypeStruct((bands, 1, bins), jnp.float32),
    )(kernel, tgt, step)
    return out[:, 0, :]


def on_device(frames, lag_list, band_index, decay_rates):
    pixels = frames.shape[1]
    devices = lax.axis_size(("tm", "qband"))
    table = dft_table(pixels)
    index_all = lax.all_gather(band_index[:, 0].astype(jnp.float32), ("tm", "qband"), axis=0, tiled=True)
    row_transform = jnp.dot(frames[0], table, preferred_element_type=jnp.float32).astype(jnp.bfloat16)
    row_transform = row_transform.reshape(pixels, 2, pixels)
    cos_part = table[:, :pixels]
    sin_part = table[:, pixels:]
    mixing = jnp.stack([table, jnp.concatenate([-sin_part, cos_part], axis=1)])
    spectrum = jnp.einsum("ypk,pyj->kj", row_transform, mixing, preferred_element_type=jnp.float32)
    spectrum = spectrum.astype(jnp.bfloat16).reshape(devices, (pixels // devices) * 2, pixels)
    gathered = lax.all_to_all(spectrum, ("tm", "qband"), 0, 0, tiled=True)
    structure = structure_block(gathered, lag_list)

    bands_dev = decay_rates.shape[0]
    row_sums = jnp.sum(structure, axis=2)
    sums_all = lax.all_gather(row_sums, ("tm", "qband"), axis=1, tiled=True)
    own_bands = (lax.axis_index("tm") * bands_dev + jnp.arange(bands_dev, dtype=jnp.int32)).astype(jnp.float32)
    one_hot = (index_all[None, :] == own_bands[:, None]).astype(jnp.float32)
    totals = jnp.dot(one_hot, sums_all.T, precision=lax.Precision.HIGHEST)
    counts = jnp.sum(one_hot, axis=1)
    target = totals / (counts[:, None] * pixels)

    columns = decay_rates.shape[1]
    all_rates = lax.all_gather(decay_rates, "qband", axis=1, tiled=True)
    kernel = kernel_panel(all_rates, lag_list)
    step_size = 1.0 / jnp.sum(kernel * kernel, axis=(1, 2))
    weights = fit_bands(kernel, target, step_size)
    weights = lax.dynamic_slice_in_dim(weights, lax.axis_index("qband") * columns, columns, 1)
    return (structure, weights)


def solution(mesh):
    placed = (P(("tm", "qband"), None, None), P(), P(("tm", "qband"), None), P("tm", "qband"))
    return jax.shard_map(
        on_device,
        mesh=mesh,
        in_specs=placed,
        out_specs=(P(None, ("tm", "qband"), None), P("tm", "qband")),
        check_vma=False,
    )
```

time: 500 us -> 436 us (0.87)
  blocking collectives: 89.6 us -> 290 us
  other arithmetic: 245 us -> 58.6 us
  loops' own time: 42.2 us -> 0 us
  waiting for transfers between devices: 26.3 us -> 0.01 us
  local copies, waits for them, and re-layouts: 35.7 us -> 11.4 us
  Pallas kernels: 25 us -> 47 us
  matrix products: 23 us -> 15.7 us
    all_gather x0 -> x1, blocking collectives: none -> 176 us  [on_device(): sums_all = lax.all_gather(row_sums, ('tm', 'qband'), axis=1, tiled=True)]
    sub x16 -> x0, other arithmetic: 142 us -> none  [one_lag(): shifted.astype(jnp.float32) - spectrum_block.astype(jnp.float32)]
    unnamed x0 -> x1, blocking collectives: none -> 88.2 us
    reduce_sum x17 -> x2, other arithmetic: 73.9 us -> 2.73 us  [the longest x1 2.54 us: structure_block(): summed = jnp.sum(summed.reshape(nlag, rows // 2, 2, pixels), axis=2)]
    psum x1 -> x0, blocking collectives: 64.3 us -> none  [on_device(): totals, counts = lax.psum((partial_totals, partial_counts), ('tm', 'qband'))]
    another operation x1 -> x0, loops' own time: 42.2 us -> none  [structure_block(): return lax.map(one_lag, lag_list)]
    all_to_all x1, waiting for transfers between devices: 26.3 us -> 0.01 us  [on_device(): gathered = lax.all_to_all(spectrum, ('tm', 'qband'), 0, 0, tiled=True)]
    another operation x3 -> x1, other arithmetic: 25.3 us -> 0.43 us  [on_device(): mixing = jnp.stack([table, jnp.concatenate([-sin_part, cos_part], axis=1)])]
  transfers between devices with their start and end apart: 1 -> 1, of which waited for: 1 -> 0; matrix products, arithmetic and copies ran while one was open for 0% -> 0% of each run, Pallas kernels for 0% -> 0%
where the time goes in v2:
time: 436 us; the launch traced here: 435 us
  blocking collectives  290 us (67%)
  other arithmetic  58.6 us (13%)
  Pallas kernels  47 us (11%)
  matrix products  15.7 us (4%)
  starting transfers between devices  12 us (3%)
  local copies, waits for them, and re-layouts  11.4 us (3%)
    all_gather x1, blocking collectives, on_device(): sums_all = lax.all_gather(row_sums, ('tm', 'qband'), axis=1, tiled=True)  176 us
    unnamed x1, blocking collectives  88.2 us
    all_gather x1, blocking collectives, on_device(): all_rates = lax.all_gather(decay_rates, 'qband', axis=1, tiled=True)  25.3 us
    pallas_call x1, Pallas kernels, fit_bands(): pl.pallas_call(fit_kernel, out_shape=jax.ShapeDtypeStruct((bands, 1, bins...  25 us
    pallas_call x1, Pallas kernels, structure_block(): pl.pallas_call(structure_kernel, out_shape=jax.ShapeDtypeStruct((nlag, ro...  22 us
    slice x1, other arithmetic, on_device(): sin_part = table[:, pixels:]  18.3 us
    concatenate x1, other arithmetic, dft_table(): jnp.concatenate([jnp.cos(angles) * factor, -sign_factor * jnp.sin(angles)...  18.3 us
    neg x1, other arithmetic, on_device(): mixing = jnp.stack([table, jnp.concatenate([-sin_part, cos_part], axis=1)])  17 us
  transfers between devices with their start and end apart: 1, of which 0 were waited for; matrix products, arithmetic and copies ran while one was open for 0% of the time, Pallas kernels for 0%

profile of v2, /device:TPU:1, one launch (start us, length us, event | category | flops | bytes accessed | tf_op | source)
XLA Modules:
  0.0 435.2 jit_solution(8217142702821592825)
XLA Ops:
  0.6 18.3 %multiply_convert_fusion = (bf16[1024,1024]{1,0:T(8,128)(2,1)S(1)}, bf16[1024,1024]{1,0:T(8,128)(2,1)S(1)}) fusion(), kind=kLoop, calls=%fused_computation.19 | loop fusion | flops 26214400 | bytes 4194304 | tf_op jit(solution)/shard_map/slice | solution.py:108
  19.0 17.0 %fusion.22 = bf16[1024,1024]{1,0:T(8,128)(2,1)S(1)} fusion(), kind=kLoop, calls=%fused_computation.27 | loop fusion | flops 27262976 | bytes 2097152 | tf_op jit(solution)/shard_map/neg | solution.py:109
  36.0 18.3 %fusion.23 = (bf16[1,1024,1024]{2,1,0:T(8,128)(2,1)S(1)}, bf16[1,1024,1024]{2,1,0:T(8,128)(2,1)S(1)}) fusion(), kind=kLoop, calls=%fused_computation.28 | loop fusion | flops 26214400 | bytes 4194304 | tf_op jit(solution)/shard_map/concatenate | solution.py:21
  54.3 0.4 maximum_bitcast_fusion
  54.8 4.8 %fusion.18 = bf16[2048,1024]{1,0:T(8,128)(2,1)S(1)} fusion(bf16[1024,1024]{1,0:T(8,128)(2,1)S(1)} %get-tuple-element.8, bf16[1024,1024]{1,0:T(8,128)(2,1)S(1)} %get-tuple-element.9, bf16[1,1024,1024]{2,1,0:T(8,128)(2,1)S(1)} %copy-done), kind=kOutput, calls=%fused_computation.25 | convolution fusion | flops 4305453056 | bytes 10485760 | tf_op jit(solution)/shard_map/dot_general | solution.py:105
  59.6 10.5 %bitcast_convert_fusion = bf16[1024,2048]{1,0:T(8,128)(2,1)} fusion(bf16[1024,2,1024]{0,2,1:T(8,128)(2,1)S(1)} %bitcast.22, bf16[1,1024,2048]{2,1,0:T(8,128)(2,1)S(1)} %maximum_bitcast_fusion, bf16[1,1024,1024]{2,1,0:T(8,128)(2,1)S(1)} %get-tuple-element.10, bf16[1,1024,1024]{2,1,0:T(8,128)(2,1)S(1)} %get-tuple-element.11), kind=kOutput, calls=%fused_computation.6 | convolution fusion | flops 8617197568 | bytes 16777216 | tf_op jit(solution)/shard_map/ypk,pyj->kj/dot_general | solution.py:110
  70.2 7.1 %reshape.67 = bf16[128,16,1024]{2,1,0:T(8,128)(2,1)} reshape(bf16[1024,2048]{1,0:T(8,128)(2,1)} %bitcast_convert_fusion) | data formatting | bytes 8388608 | tf_op jit(solution)/shard_map/reshape | solution.py:111
  77.3 12.0 %all-to-all-start = ((bf16[128,16,1024]{2,1,0:T(8,128)(2,1)}), bf16[128,16,1024]{2,1,0:T(8,128)(2,1)}, u32[]{:S(2)}, u32[]{:S(2)}) async-start(bf16[128,16,1024]{2,1,0:T(8,128)(2,1)} %reshape.67), calls=%async_computation | async-start | bytes 8388608 | tf_op jit(solution)/shard_map/all_to_all | solution.py:112
  89.3 25.3 %all_gather.9 = f32[2,1024]{1,0:T(2,128)S(1)} all-gather(f32[2,256]{1,0:T(2,128)S(1)} %copy-done.2), channel_id=1, replica_groups=mesh['tm'=32,'qband'=4] {'qband'}, dimensions={1}, use_global_device_ids=true | all-gather | bytes 10240 | tf_op jit(solution)/shard_map/all_gather | solution.py:125
  114.6 0.1 bitcast_dynamic-update-slice_fusion
  114.7 88.2 %all-reduce = f32[1024]{0:T(1024)S(1)} all-reduce(f32[1024]{0:T(1024)S(1)} %bitcast_dynamic-update-slice_fusion), channel_id=2, replica_groups=mesh['tm'=32,'qband'=4] {'tm','qband'}, use_global_device_ids=true, to_apply=%add | all-reduce | flops 1024 | bytes 8192
  202.9 0.2 fusion.26
  203.1 0.8 multiply_reduce_fusion
  203.8 22.0 %shard_map.59 = f32[16,16,1024]{2,1,0:T(8,128)S(1)} custom-call(s32[16]{0:T(128)S(1)} %copy-done.1, bf16[128,16,1024]{2,1,0:T(8,128)(2,1)} %all-to-all-done.x_ref), custom_call_target="tpu_custom_call" | custom-call | tf_op jit(solution)/shard_map/pallas_call | solution.py:52
  225.8 1.6 reshape.68
  227.5 2.5 reduce_sum.36
  230.0 0.9 fusion.31
  231.0 176.3 %all_gather.11 = f32[16,1024]{0,1:T(8,128)S(1)} all-gather(f32[16,8]{0,1:T(8,128)S(1)} %copy.7), channel_id=1, replica_groups=mesh['tm'=32,'qband'=4] {'tm','qband'}, dimensions={1}, use_global_device_ids=true | all-gather | bytes 66048 | tf_op jit(solution)/shard_map/all_gather | solution.py:117
  407.3 0.3 convolution_divide_fusion
  407.6 0.7 broadcast_in_dim.14.tgt_ref
  408.3 0.7 broadcast_in_dim.15.step_ref
  409.0 25.0 %shard_map.60 = f32[2,1,1024]{2,1,0:T(1,128)} custom-call(f32[2,16,1024]{2,1,0:T(8,128)} %get-tuple-element.5.k_ref, f32[2,16,128]{2,1,0:T(8,128)} %broadcast_in_dim.14.tgt_ref, f32[2,1,1024]{2,1,0:T(1,128)} %broadcast_in_dim.15.step_ref), custom_call_target="tpu_custom_call" | custom-call | tf_op jit(solution)/shard_map/pallas_call | solution.py:93
  434.0 0.7 constant_dynamic-slice_fusion
  434.6 0.6 copy.10
  (16 shorter events, 0.1 us)
Async XLA Ops:
  0.6 54.1 %copy-start = (bf16[1,1024,1024]{2,1,0:T(8,128)(2,1)S(1)}, bf16[1,1024,1024]{2,1,0:T(8,128)(2,1)}, u32[]{:S(2)}) copy-start(bf16[1,1024,1024]{2,1,0:T(8,128)(2,1)} %param.4) | copy-start | bytes 6291460
  77.3 12.0 %copy-start.2 = (f32[2,256]{1,0:T(2,128)S(1)}, f32[2,256]{1,0:T(2,128)}, u32[]{:S(2)}) copy-start(f32[2,256]{1,0:T(2,128)} %param.7) | copy-start | bytes 6148
  77.3 37.3 %copy-start.3 = (s32[8,1]{0,1:T(1,128)S(1)}, s32[8,1]{0,1:T(1,128)}, u32[]{:S(2)}) copy-start(s32[8,1]{0,1:T(1,128)} %param.6) | copy-start | bytes 100
  77.3 125.8 %copy-start.1 = (s32[16]{0:T(128)S(1)}, s32[16]{0:T(128)}, u32[]{:S(2)}) copy-start(s32[16]{0:T(128)} %lags_ref.1) | copy-start | bytes 196
  77.3 126.6 %all-to-all-start = ((bf16[128,16,1024]{2,1,0:T(8,128)(2,1)}), bf16[128,16,1024]{2,1,0:T(8,128)(2,1)}, u32[]{:S(2)}, u32[]{:S(2)}) async-start(bf16[128,16,1024]{2,1,0:T(8,128)(2,1)} %reshape.67), calls=%async_computation | async-start | bytes 8388608 | tf_op jit(solution)/shard_map/all_to_all | solution.py:112

commit v3 on v2

--- a/solution.py
+++ b/solution.py
@@ -101,7 +101,6 @@
     pixels = frames.shape[1]
     devices = lax.axis_size(("tm", "qband"))
     table = dft_table(pixels)
-    index_all = lax.all_gather(band_index[:, 0].astype(jnp.float32), ("tm", "qband"), axis=0, tiled=True)
     row_transform = jnp.dot(frames[0], table, preferred_element_type=jnp.float32).astype(jnp.bfloat16)
     row_transform = row_transform.reshape(pixels, 2, pixels)
     cos_part = table[:, :pixels]
@@ -113,20 +112,31 @@
     structure = structure_block(gathered, lag_list)
 
     bands_dev = decay_rates.shape[0]
+    bands_total = bands_dev * lax.axis_size("tm")
     row_sums = jnp.sum(structure, axis=2)
-    sums_all = lax.all_gather(row_sums, ("tm", "qband"), axis=1, tiled=True)
-    own_bands = (lax.axis_index("tm") * bands_dev + jnp.arange(bands_dev, dtype=jnp.int32)).astype(jnp.float32)
-    one_hot = (index_all[None, :] == own_bands[:, None]).astype(jnp.float32)
-    totals = jnp.dot(one_hot, sums_all.T, precision=lax.Precision.HIGHEST)
-    counts = jnp.sum(one_hot, axis=1)
-    target = totals / (counts[:, None] * pixels)
+    band_ids = jnp.arange(bands_total, dtype=jnp.int32)
+    one_hot = (band_index[:, 0][None, :] == band_ids[:, None]).astype(jnp.float32)
+    partial_totals = jnp.dot(one_hot, row_sums.T, precision=lax.Precision.HIGHEST)
+    partial_counts = jnp.sum(one_hot, axis=1, keepdims=True)
+    partial = jnp.concatenate([partial_totals, partial_counts], axis=1)
+    per_dest = jnp.broadcast_to(
+        partial.reshape(bands_total // bands_dev, 1, bands_dev, -1),
+        (bands_total // bands_dev, devices // (bands_total // bands_dev), bands_dev, partial.shape[1]),
+    ).reshape(devices, bands_dev, partial.shape[1])
+    received = lax.all_to_all(per_dest, ("tm", "qband"), 0, 0, tiled=True)
+    own = jnp.sum(received, axis=0)
+    nlag = lag_list.shape[0]
+    target = own[:, :nlag] / (own[:, nlag:] * pixels)
 
     columns = decay_rates.shape[1]
-    all_rates = lax.all_gather(decay_rates, "qband", axis=1, tiled=True)
+    ring = lax.axis_size("qband")
+    pieces = [decay_rates] + [
+        lax.ppermute(decay_rates, "qband", [(j, (j + s) % ring) for j in range(ring)]) for s in range(1, ring)
+    ]
+    all_rates = jnp.concatenate(pieces, axis=1)
     kernel = kernel_panel(all_rates, lag_list)
     step_size = 1.0 / jnp.sum(kernel * kernel, axis=(1, 2))
-    weights = fit_bands(kernel, target, step_size)
-    weights = lax.dynamic_slice_in_dim(weights, lax.axis_index("qband") * columns, columns, 1)
+    weights = fit_bands(kernel, target, step_size)[:, :columns]
     return (structure, weights)
 
 

time: 436 us -> 215 us (0.49)
  blocking collectives: 290 us -> 0 us
  waiting for transfers between devices: 0.01 us -> 59 us
  starting transfers between devices: 12 us -> 20.3 us
    all_gather x2 -> x0, blocking collectives: 202 us -> none  [the longest x1 176 us: on_device(): sums_all = lax.all_gather(row_sums, ('tm', 'qband'), axis=1, tiled=True)]
    unnamed x1 -> x0, blocking collectives: 88.2 us -> none
    all_to_all x1, waiting for transfers between devices: 0.01 us -> 27.4 us  [on_device(): gathered = lax.all_to_all(spectrum, ('tm', 'qband'), 0, 0, tiled=True)]
    ppermute x0 -> x3, waiting for transfers between devices: none -> 21.5 us  [on_device(): lax.ppermute(decay_rates, 'qband', [(j, (j + s) % ring) for j in range(ri...]
    all_to_all x0 -> x1, waiting for transfers between devices: none -> 10.2 us  [on_device(): received = lax.all_to_all(per_dest, ('tm', 'qband'), 0, 0, tiled=True)]
    all_to_all x0 -> x1, starting transfers between devices: none -> 5.79 us  [on_device(): received = lax.all_to_all(per_dest, ('tm', 'qband'), 0, 0, tiled=True)]
  transfers between devices with their start and end apart: 1 -> 5, of which waited for: 0 -> 4; matrix products, arithmetic and copies ran while one was open for 0% -> 0% of each run, Pallas kernels for 0% -> 0%
where the time goes in v3:
time: 215 us; the launch traced here: 216 us
  waiting for transfers between devices  59 us (27%)
  other arithmetic  58.7 us (27%)
  Pallas kernels  49.1 us (23%)
  starting transfers between devices  20.3 us (9%)
  matrix products  15.6 us (7%)
  local copies, waits for them, and re-layouts  12.5 us (6%)
    all_to_all x1, waiting for transfers between devices, on_device(): gathered = lax.all_to_all(spectrum, ('tm', 'qband'), 0, 0, tiled=True)  27.4 us
    pallas_call x1, Pallas kernels, fit_bands(): pl.pallas_call(fit_kernel, out_shape=jax.ShapeDtypeStruct((bands, 1, bins...  25 us
    pallas_call x1, Pallas kernels, structure_block(): pl.pallas_call(structure_kernel, out_shape=jax.ShapeDtypeStruct((nlag, ro...  24.1 us
    ppermute x3, waiting for transfers between devices, on_device(): lax.ppermute(decay_rates, 'qband', [(j, (j + s) % ring) for j in range(ri...  21.5 us
    slice x1, other arithmetic, on_device(): sin_part = table[:, pixels:]  18.3 us
    concatenate x1, other arithmetic, dft_table(): jnp.concatenate([jnp.cos(angles) * factor, -sign_factor * jnp.sin(angles)...  18.3 us
    neg x1, other arithmetic, on_device(): mixing = jnp.stack([table, jnp.concatenate([-sin_part, cos_part], axis=1)])  17 us
    all_to_all x1, starting transfers between devices, on_device(): gathered = lax.all_to_all(spectrum, ('tm', 'qband'), 0, 0, tiled=True)  12 us
  transfers between devices with their start and end apart: 5, of which 4 were waited for; matrix products, arithmetic and copies ran while one was open for 0% of the time, Pallas kernels for 0%

profile of v3, /device:TPU:1, one launch (start us, length us, event | category | flops | bytes accessed | tf_op | source)
XLA Modules:
  0.0 215.9 jit_solution(8511630080183101927)
XLA Ops:
  0.6 18.3 %multiply_convert_fusion = (bf16[1024,1024]{1,0:T(8,128)(2,1)S(1)}, bf16[1024,1024]{1,0:T(8,128)(2,1)S(1)}) fusion(), kind=kLoop, calls=%fused_computation.19 | loop fusion | flops 26214400 | bytes 4194304 | tf_op jit(solution)/shard_map/slice | solution.py:107
  19.0 17.0 %fusion.22 = bf16[1024,1024]{1,0:T(8,128)(2,1)S(1)} fusion(), kind=kLoop, calls=%fused_computation.27 | loop fusion | flops 27262976 | bytes 2097152 | tf_op jit(solution)/shard_map/neg | solution.py:108
  36.0 18.3 %fusion.23 = (bf16[1,1024,1024]{2,1,0:T(8,128)(2,1)S(1)}, bf16[1,1024,1024]{2,1,0:T(8,128)(2,1)S(1)}) fusion(), kind=kLoop, calls=%fused_computation.28 | loop fusion | flops 26214400 | bytes 4194304 | tf_op jit(solution)/shard_map/concatenate | solution.py:21
  54.8 4.8 %fusion.18 = bf16[2048,1024]{1,0:T(8,128)(2,1)S(1)} fusion(bf16[1024,1024]{1,0:T(8,128)(2,1)S(1)} %get-tuple-element.8, bf16[1024,1024]{1,0:T(8,128)(2,1)S(1)} %get-tuple-element.9, bf16[1,1024,1024]{2,1,0:T(8,128)(2,1)S(1)} %copy-done), kind=kOutput, calls=%fused_computation.25 | convolution fusion | flops 4305453056 | bytes 10485760 | tf_op jit(solution)/shard_map/dot_general | solution.py:104
  59.6 10.6 %bitcast_convert_fusion = bf16[1024,2048]{1,0:T(8,128)(2,1)} fusion(bf16[1024,2,1024]{0,2,1:T(8,128)(2,1)S(1)} %bitcast.33, bf16[1,1024,2048]{2,1,0:T(8,128)(2,1)S(1)} %maximum_bitcast_fusion, bf16[1,1024,1024]{2,1,0:T(8,128)(2,1)S(1)} %get-tuple-element.10, bf16[1,1024,1024]{2,1,0:T(8,128)(2,1)S(1)} %get-tuple-element.11), kind=kOutput, calls=%fused_computation.6 | convolution fusion | flops 8617197568 | bytes 16777216 | tf_op jit(solution)/shard_map/ypk,pyj->kj/dot_general | solution.py:109
  70.2 7.1 %reshape.111 = bf16[128,16,1024]{2,1,0:T(8,128)(2,1)} reshape(bf16[1024,2048]{1,0:T(8,128)(2,1)} %bitcast_convert_fusion) | data formatting | bytes 8388608 | tf_op jit(solution)/shard_map/reshape | solution.py:110
  77.3 12.0 %all-to-all-start = ((bf16[128,16,1024]{2,1,0:T(8,128)(2,1)}), bf16[128,16,1024]{2,1,0:T(8,128)(2,1)}, u32[]{:S(2)}, u32[]{:S(2)}) async-start(bf16[128,16,1024]{2,1,0:T(8,128)(2,1)} %reshape.111), calls=%async_computation | async-start | bytes 8388608 | tf_op jit(solution)/shard_map/all_to_all | solution.py:111
  89.2 1.8 collective-permute-start
  91.1 0.7 collective-permute-start.1
  92.5 21.0 %collective-permute-done.1 = f32[2,256]{1,0:T(2,128)S(1)} collective-permute-done((f32[2,256]{1,0:T(2,128)S(1)}, f32[2,256]{1,0:T(2,128)S(1)}, u32[]{:S(2)}, u32[]{:S(2)}) %collective-permute-start.1) | collective-permute-done | bytes 2080 | tf_op jit(solution)/shard_map/ppermute | solution.py:134
  113.6 0.8 multiply_reduce_fusion
  114.3 27.4 %all-to-all-done.x_ref = bf16[128,16,1024]{2,1,0:T(8,128)(2,1)} async-done(((bf16[128,16,1024]{2,1,0:T(8,128)(2,1)}), bf16[128,16,1024]{2,1,0:T(8,128)(2,1)}, u32[]{:S(2)}, u32[]{:S(2)}) %all-to-all-start) | async-done | bytes 4194336 | tf_op jit(solution)/shard_map/all_to_all | solution.py:111
  141.7 24.1 %shard_map.59 = f32[16,16,1024]{2,1,0:T(8,128)S(1)} custom-call(s32[16]{0:T(128)S(1)} %copy-done.1, bf16[128,16,1024]{2,1,0:T(8,128)(2,1)} %all-to-all-done.x_ref), custom_call_target="tpu_custom_call" | custom-call | tf_op jit(solution)/shard_map/pallas_call | solution.py:52
  165.8 1.6 reshape.112
  167.4 2.5 %reduce_sum.45 = f32[16,8,1024]{2,1,0:T(8,128)S(1)} reduce(f32[16,8,2,1024]{3,2,1,0:T(2,128)} %reshape.112, f32[]{:T(128)} %constant.36.clone.1), dimensions={2}, to_apply=%region_0.1 | reduce | flops 131072 | bytes 1572868 | tf_op jit(solution)/shard_map/reduce_sum | solution.py:65
  169.9 0.9 fusion.31
  171.1 0.7 copy.34
  171.9 5.8 %all-to-all-start.1 = ((f32[128,2,17]{2,1,0:T(2,128)}), f32[128,2,17]{2,1,0:T(2,128)S(1)}, u32[]{:S(2)}, u32[]{:S(2)}) async-start(f32[128,2,17]{2,1,0:T(2,128)} %copy.34), calls=%async_computation.1 | async-start | bytes 262144 | tf_op jit(solution)/shard_map/all_to_all | solution.py:126
  177.7 10.2 %all-to-all-done.1 = f32[128,2,17]{2,1,0:T(2,128)S(1)} async-done(((f32[128,2,17]{2,1,0:T(2,128)}), f32[128,2,17]{2,1,0:T(2,128)S(1)}, u32[]{:S(2)}, u32[]{:S(2)}) %all-to-all-start.1) | async-done | bytes 17440 | tf_op jit(solution)/shard_map/all_to_all | solution.py:126
  188.3 0.7 broadcast_in_dim.20.tgt_ref
  188.9 0.7 broadcast_in_dim.21.step_ref
  189.6 25.0 %shard_map.60 = f32[2,1,1024]{2,1,0:T(1,128)} custom-call(f32[2,16,1024]{2,1,0:T(8,128)} %get-tuple-element.5.k_ref, f32[2,16,128]{2,1,0:T(8,128)} %broadcast_in_dim.20.tgt_ref, f32[2,1,1024]{2,1,0:T(1,128)} %broadcast_in_dim.21.step_ref), custom_call_target="tpu_custom_call" | custom-call | tf_op jit(solution)/shard_map/pallas_call | solution.py:93
  214.6 0.7 copy.46
  215.3 0.6 slice.28
  (27 shorter events, 1.9 us)
Async XLA Ops:
  0.6 54.1 %copy-start = (bf16[1,1024,1024]{2,1,0:T(8,128)(2,1)S(1)}, bf16[1,1024,1024]{2,1,0:T(8,128)(2,1)}, u32[]{:S(2)}) copy-start(bf16[1,1024,1024]{2,1,0:T(8,128)(2,1)} %param.4) | copy-start | bytes 6291460
  77.3 12.0 %copy-start.2 = (f32[2,256]{1,0:T(2,128)S(1)}, f32[2,256]{1,0:T(2,128)}, u32[]{:S(2)}) copy-start(f32[2,256]{1,0:T(2,128)} %param.7) | copy-start | bytes 6148
  77.3 14.5 %copy-start.3 = (s32[8,1]{0,1:T(1,128)S(1)}, s32[8,1]{0,1:T(1,128)}, u32[]{:S(2)}) copy-start(s32[8,1]{0,1:T(1,128)} %param.6) | copy-start | bytes 100
  77.3 14.6 %copy-start.1 = (s32[16]{0:T(128)S(1)}, s32[16]{0:T(128)}, u32[]{:S(2)}) copy-start(s32[16]{0:T(128)} %lags_ref.1) | copy-start | bytes 196
  77.3 64.4 %all-to-all-start = ((bf16[128,16,1024]{2,1,0:T(8,128)(2,1)}), bf16[128,16,1024]{2,1,0:T(8,128)(2,1)}, u32[]{:S(2)}, u32[]{:S(2)}) async-start(bf16[128,16,1024]{2,1,0:T(8,128)(2,1)} %reshape.111), calls=%async_computation | async-start | bytes 8388608 | tf_op jit(solution)/shard_map/all_to_all | solution.py:111
  89.2 3.3 %collective-permute-start = (f32[2,256]{1,0:T(2,128)S(1)}, f32[2,256]{1,0:T(2,128)S(1)}, u32[]{:S(2)}, u32[]{:S(2)}) collective-permute-start(f32[2,256]{1,0:T(2,128)S(1)} %copy-done.2), channel_id=1, source_target_pairs={{0,1},{1,2},{2,3},{3,0},{4,5},{5,6},{6,7},{7,4},{8,9},{9,10},{10,1... | collective-permute-start | bytes 6152 | tf_op jit(solution)/shard_map/ppermute | solution.py:134
  91.1 22.5 %collective-permute-start.1 = (f32[2,256]{1,0:T(2,128)S(1)}, f32[2,256]{1,0:T(2,128)S(1)}, u32[]{:S(2)}, u32[]{:S(2)}) collective-permute-start(f32[2,256]{1,0:T(2,128)S(1)} %copy-done.2), channel_id=1, source_target_pairs={{0,2},{1,3},{2,0},{3,1},{4,6},{5,7},{6,4},{7,5},{8,10},{9,11},{10,... | collective-permute-start | bytes 6152 | tf_op jit(solution)/shard_map/ppermute | solution.py:134
  91.8 21.8 %collective-permute-start.2 = (f32[2,256]{1,0:T(2,128)S(1)}, f32[2,256]{1,0:T(2,128)S(1)}, u32[]{:S(2)}, u32[]{:S(2)}) collective-permute-start(f32[2,256]{1,0:T(2,128)S(1)} %copy-done.2), channel_id=1, source_target_pairs={{0,3},{1,0},{2,1},{3,2},{4,7},{5,4},{6,5},{7,6},{8,11},{9,8},{10,9... | collective-permute-start | bytes 6152 | tf_op jit(solution)/shard_map/ppermute | solution.py:134
  171.9 16.0 %all-to-all-start.1 = ((f32[128,2,17]{2,1,0:T(2,128)}), f32[128,2,17]{2,1,0:T(2,128)S(1)}, u32[]{:S(2)}, u32[]{:S(2)}) async-start(f32[128,2,17]{2,1,0:T(2,128)} %copy.34), calls=%async_computation.1 | async-start | bytes 262144 | tf_op jit(solution)/shard_map/all_to_all | solution.py:126

commit v4 on v3

--- a/solution.py
+++ b/solution.py
@@ -25,6 +25,7 @@
 
 def structure_kernel(lags_ref, x_ref, out_ref, x32_ref):
     frames_all = x_ref.shape[0]
+    pixels = out_ref.shape[2]
 
     def convert(t, carry):
         x32_ref[t] = x_ref[t].astype(jnp.float32)
@@ -40,30 +41,29 @@
             d = x32_ref[t + lag] - x32_ref[t]
             return acc + d * d
 
-        out_ref[l] = lax.fori_loop(0, count, step, jnp.zeros(x32_ref.shape[1:], jnp.float32))
+        acc = lax.fori_loop(0, count, step, jnp.zeros(x32_ref.shape[1:], jnp.float32))
+        out_ref[l] = (acc[:, :pixels] + acc[:, pixels:]) / count.astype(jnp.float32)
         return carry
 
     lax.fori_loop(0, lags_ref.shape[0], one_lag, 0)
 
 
 def structure_block(spectrum_block, lag_list):
-    frames_all, rows, pixels = spectrum_block.shape
+    frames_all, rows, width = spectrum_block.shape
     nlag = lag_list.shape[0]
-    summed = pl.pallas_call(
+    return pl.pallas_call(
         structure_kernel,
-        out_shape=jax.ShapeDtypeStruct((nlag, rows, pixels), jnp.float32),
+        out_shape=jax.ShapeDtypeStruct((nlag, rows, width // 2), jnp.float32),
         in_specs=[
             pl.BlockSpec(memory_space=pltpu.SMEM),
             pl.BlockSpec(memory_space=pltpu.VMEM),
         ],
         out_specs=pl.BlockSpec(memory_space=pltpu.VMEM),
         scratch_shapes=[
-            pltpu.VMEM((frames_all, rows, pixels), jnp.float32),
+            pltpu.VMEM((frames_all, rows, width), jnp.float32),
         ],
         compiler_params=pltpu.CompilerParams(vmem_limit_bytes=40 * 1024 * 1024),
     )(lag_list, spectrum_block)
-    summed = jnp.sum(summed.reshape(nlag, rows // 2, 2, pixels), axis=2)
-    return summed / (frames_all - lag_list).astype(jnp.float32)[:, None, None]
 
 
 def kernel_panel(decay_rates, lag_list):
@@ -72,18 +72,17 @@
 
 
 def fit_kernel(k_ref, tgt_ref, step_ref, w_ref):
-    for b in range(k_ref.shape[0]):
-        panel = k_ref[b]
-        tgt = tgt_ref[b][:, 0:1]
-        step = step_ref[b]
+    panel = k_ref[...]
+    tgt = tgt_ref[...][:, :, 0:1]
+    step = step_ref[...]
 
-        def body(i, w):
-            predicted = jnp.sum(panel * w, axis=1, keepdims=True)
-            residual = predicted - tgt
-            gradient = jnp.sum(panel * residual, axis=0, keepdims=True)
-            return jnp.maximum(w - step * gradient, 0.0)
+    def body(i, w):
+        predicted = jnp.sum(panel * w, axis=2, keepdims=True)
+        residual = predicted - tgt
+        gradient = jnp.sum(panel * residual, axis=1, keepdims=True)
+        return jnp.maximum(w - step * gradient, 0.0)
 
-        w_ref[b] = lax.fori_loop(0, ITERS, body, jnp.zeros(step.shape, jnp.float32))
+    w_ref[...] = lax.fori_loop(0, ITERS, body, jnp.zeros(step.shape, jnp.float32))
 
 
 def fit_bands(kernel, target, step_size):
@@ -100,14 +99,14 @@
 def on_device(frames, lag_list, band_index, decay_rates):
     pixels = frames.shape[1]
     devices = lax.axis_size(("tm", "qband"))
-    table = dft_table(pixels)
+    table = lax.optimization_barrier(dft_table(pixels))
     row_transform = jnp.dot(frames[0], table, preferred_element_type=jnp.float32).astype(jnp.bfloat16)
     row_transform = row_transform.reshape(pixels, 2, pixels)
     cos_part = table[:, :pixels]
     sin_part = table[:, pixels:]
     mixing = jnp.stack([table, jnp.concatenate([-sin_part, cos_part], axis=1)])
     spectrum = jnp.einsum("ypk,pyj->kj", row_transform, mixing, preferred_element_type=jnp.float32)
-    spectrum = spectrum.astype(jnp.bfloat16).reshape(devices, (pixels // devices) * 2, pixels)
+    spectrum = spectrum.astype(jnp.bfloat16).reshape(devices, pixels // devices, 2 * pixels)
     gathered = lax.all_to_all(spectrum, ("tm", "qband"), 0, 0, tiled=True)
     structure = structure_block(gathered, lag_list)
 

time: 215 us -> 159 us (0.74)
  other arithmetic: 58.7 us -> 21.8 us
  Pallas kernels: 49.1 us -> 37.4 us
  local copies, waits for them, and re-layouts: 12.5 us -> 3.77 us
    another operation x0 -> x1, other arithmetic: none -> 18.3 us
    slice x1 -> x0, other arithmetic: 18.3 us -> none  [on_device(): sin_part = table[:, pixels:]]
    concatenate x1, other arithmetic: 18.3 us -> 0.43 us  [dft_table(): jnp.concatenate([jnp.cos(angles) * factor, -sign_factor * jnp.sin(angles)...]
    neg x1, other arithmetic: 17 us -> 0.27 us  [on_device(): mixing = jnp.stack([table, jnp.concatenate([-sin_part, cos_part], axis=1)])]
    pallas_call x1, Pallas kernels: 25 us -> 15.3 us  [fit_bands(): pl.pallas_call(fit_kernel, out_shape=jax.ShapeDtypeStruct((bands, 1, bins...]
    reshape x2 -> x0, local copies, waits for them, and re-layouts: 8.69 us -> none  [the longest x1 7.1 us: on_device(): spectrum.astype(jnp.bfloat16)]
    reduce_sum x1 -> x0, other arithmetic: 2.51 us -> none  [structure_block(): summed = jnp.sum(summed.reshape(nlag, rows // 2, 2, pixels), axis=2)]
  transfers between devices with their start and end apart: 5 -> 5, of which waited for: 4 -> 4; matrix products, arithmetic and copies ran while one was open for 0% -> 1% of each run, Pallas kernels for 0% -> 0%
where the time goes in v4:
time: 159 us; the launch traced here: 158 us
  waiting for transfers between devices  59 us (37%)
  Pallas kernels  37.4 us (24%)
  other arithmetic  21.8 us (14%)
  starting transfers between devices  20.3 us (13%)
  matrix products  15.4 us (10%)
  local copies, waits for them, and re-layouts  3.77 us (2%)
    all_to_all x1, waiting for transfers between devices, on_device(): gathered = lax.all_to_all(spectrum, ('tm', 'qband'), 0, 0, tiled=True)  27.3 us
    pallas_call x1, Pallas kernels, structure_block(): pl.pallas_call(structure_kernel, out_shape=jax.ShapeDtypeStruct((nlag, ro...  22.1 us
    ppermute x3, waiting for transfers between devices, on_device(): lax.ppermute(decay_rates, 'qband', [(j, (j + s) % ring) for j in range(ri...  21.5 us
    another operation x1, other arithmetic  18.3 us
    pallas_call x1, Pallas kernels, fit_bands(): pl.pallas_call(fit_kernel, out_shape=jax.ShapeDtypeStruct((bands, 1, bins...  15.3 us
    all_to_all x1, starting transfers between devices, on_device(): gathered = lax.all_to_all(spectrum, ('tm', 'qband'), 0, 0, tiled=True)  11.9 us
    dot_general x1, matrix products, on_device(): jnp.einsum('ypk,pyj->kj', row_transform, mixing, preferred_element_type=j...  10.4 us
    all_to_all x1, waiting for transfers between devices, on_device(): received = lax.all_to_all(per_dest, ('tm', 'qband'), 0, 0, tiled=True)  10.2 us
  transfers between devices with their start and end apart: 5, of which 4 were waited for; matrix products, arithmetic and copies ran while one was open for 1% of the time, Pallas kernels for 0%

profile of v4, /device:TPU:1, one launch (start us, length us, event | category | flops | bytes accessed | tf_op | source)
XLA Modules:
  0.0 158.5 jit_solution(10643271364171928748)
XLA Ops:
  0.6 18.3 %multiply_convert_fusion = (bf16[1024,1024]{1,0:T(8,128)(2,1)S(1)}, bf16[1024,1024]{1,0:T(8,128)(2,1)S(1)}) fusion(), kind=kLoop, calls=%fused_computation.14 | loop fusion | flops 26214400 | bytes 4194304 | tf_op jit(solution)/shard_map/convert.1
  19.0 0.4 pad_maximum_fusion
  19.4 0.3 slice_negate_fusion
  19.7 4.9 %convolution_convert_fusion = bf16[2048,1024]{1,0:T(8,128)(2,1)S(1)} fusion(bf16[1024,2048]{1,0:T(8,128)(2,1)S(1)} %pad_maximum_fusion, bf16[1,1024,1024]{2,1,0:T(8,128)(2,1)S(1)} %copy-done), kind=kOutput, calls=%fused_computation.20 | convolution fusion | flops 4297064448 | bytes 10485760 | tf_op jit(solution)/shard_map/dot_general | solution.py:103
  24.6 0.4 maximum_bitcast_fusion
  25.0 10.4 %fusion.12 = bf16[128,8,2048]{2,1,0:T(8,128)(2,1)} fusion(bf16[1024,2,1024]{0,2,1:T(8,128)(2,1)S(1)} %bitcast.36, bf16[1,1024,2048]{2,1,0:T(8,128)(2,1)S(1)} %maximum_bitcast_fusion, bf16[1,1024,2048]{2,1,0:T(8,128)(2,1)S(1)} %bitcast.30), kind=kOutput, calls=%fused_computation.21 | convolution fusion | flops 8596226048 | bytes 16777216 | tf_op jit(solution)/shard_map/ypk,pyj->kj/dot_general | solution.py:108
  35.4 11.9 %all-to-all-start = ((bf16[128,8,2048]{2,1,0:T(8,128)(2,1)}), bf16[128,8,2048]{2,1,0:T(8,128)(2,1)}, u32[]{:S(2)}, u32[]{:S(2)}) async-start(bf16[128,8,2048]{2,1,0:T(8,128)(2,1)} %fusion.12), calls=%async_computation | async-start | bytes 8388608 | tf_op jit(solution)/shard_map/all_to_all | solution.py:110
  47.3 1.8 %collective-permute-start = (f32[2,256]{1,0:T(2,128)S(1)}, f32[2,256]{1,0:T(2,128)S(1)}, u32[]{:S(2)}, u32[]{:S(2)}) collective-permute-start(f32[2,256]{1,0:T(2,128)S(1)} %copy-done.2), channel_id=1, source_target_pairs={{0,1},{1,2},{2,3},{3,0},{4,5},{5,6},{6,7},{7,4},{8,9},{9,10},{10,1... | collective-permute-start | bytes 6152 | tf_op jit(solution)/shard_map/ppermute | solution.py:133
  49.2 0.7 collective-permute-start.1
  50.2 0.4 collective-permute-done
  50.6 21.0 %collective-permute-done.1 = f32[2,256]{1,0:T(2,128)S(1)} collective-permute-done((f32[2,256]{1,0:T(2,128)S(1)}, f32[2,256]{1,0:T(2,128)S(1)}, u32[]{:S(2)}, u32[]{:S(2)}) %collective-permute-start.1) | collective-permute-done | bytes 2080 | tf_op jit(solution)/shard_map/ppermute | solution.py:133
  71.7 0.8 multiply_reduce_fusion
  72.4 27.3 %all-to-all-done.x_ref = bf16[128,8,2048]{2,1,0:T(8,128)(2,1)} async-done(((bf16[128,8,2048]{2,1,0:T(8,128)(2,1)}), bf16[128,8,2048]{2,1,0:T(8,128)(2,1)}, u32[]{:S(2)}, u32[]{:S(2)}) %all-to-all-start) | async-done | bytes 4194336 | tf_op jit(solution)/shard_map/all_to_all | solution.py:110
  99.8 22.1 %shard_map.59 = f32[16,8,1024]{2,1,0:T(8,128)} custom-call(s32[16]{0:T(128)S(1)} %copy-done.1, bf16[128,8,2048]{2,1,0:T(8,128)(2,1)} %all-to-all-done.x_ref), custom_call_target="tpu_custom_call" | custom-call | tf_op jit(solution)/shard_map/pallas_call | solution.py:54
  121.9 1.1 reduce_sum.36
  123.0 0.2 convolution_bitcast_fusion
  123.4 0.7 copy.34
  124.1 5.8 %all-to-all-start.1 = ((f32[128,2,17]{2,1,0:T(2,128)}), f32[128,2,17]{2,1,0:T(2,128)S(1)}, u32[]{:S(2)}, u32[]{:S(2)}) async-start(f32[128,2,17]{2,1,0:T(2,128)} %copy.34), calls=%async_computation.1 | async-start | bytes 262144 | tf_op jit(solution)/shard_map/all_to_all | solution.py:125
  129.9 10.2 %all-to-all-done.1 = f32[128,2,17]{2,1,0:T(2,128)S(1)} async-done(((f32[128,2,17]{2,1,0:T(2,128)}), f32[128,2,17]{2,1,0:T(2,128)S(1)}, u32[]{:S(2)}, u32[]{:S(2)}) %all-to-all-start.1) | async-done | bytes 17440 | tf_op jit(solution)/shard_map/all_to_all | solution.py:125
  140.5 0.7 broadcast_in_dim.20.tgt_ref
  141.2 0.7 broadcast_in_dim.38.step_ref
  141.8 15.3 %shard_map.60 = f32[2,1,1024]{2,1,0:T(1,128)} custom-call(f32[2,16,1024]{2,1,0:T(8,128)} %get-tuple-element.5.k_ref, f32[2,16,128]{2,1,0:T(8,128)} %broadcast_in_dim.20.tgt_ref, f32[2,1,1024]{2,1,0:T(1,128)} %broadcast_in_dim.38.step_ref), custom_call_target="tpu_custom_call" | custom-call | tf_op jit(solution)/shard_map/pallas_call | solution.py:92
  157.2 0.7 copy.46
  157.9 0.6 slice.22
  (24 shorter events, 0.8 us)
Async XLA Ops:
  0.6 19.1 %copy-start = (bf16[1,1024,1024]{2,1,0:T(8,128)(2,1)S(1)}, bf16[1,1024,1024]{2,1,0:T(8,128)(2,1)}, u32[]{:S(2)}) copy-start(bf16[1,1024,1024]{2,1,0:T(8,128)(2,1)} %param.4) | copy-start | bytes 6291460
  35.4 12.0 %copy-start.2 = (f32[2,256]{1,0:T(2,128)S(1)}, f32[2,256]{1,0:T(2,128)}, u32[]{:S(2)}) copy-start(f32[2,256]{1,0:T(2,128)} %param.7) | copy-start | bytes 6148
  35.4 14.5 %copy-start.3 = (s32[8,1]{0,1:T(1,128)S(1)}, s32[8,1]{0,1:T(1,128)}, u32[]{:S(2)}) copy-start(s32[8,1]{0,1:T(1,128)} %param.6) | copy-start | bytes 100
  35.4 14.8 %copy-start.1 = (s32[16]{0:T(128)S(1)}, s32[16]{0:T(128)}, u32[]{:S(2)}) copy-start(s32[16]{0:T(128)} %lags_ref.1) | copy-start | bytes 196
  35.4 64.4 %all-to-all-start = ((bf16[128,8,2048]{2,1,0:T(8,128)(2,1)}), bf16[128,8,2048]{2,1,0:T(8,128)(2,1)}, u32[]{:S(2)}, u32[]{:S(2)}) async-start(bf16[128,8,2048]{2,1,0:T(8,128)(2,1)} %fusion.12), calls=%async_computation | async-start | bytes 8388608 | tf_op jit(solution)/shard_map/all_to_all | solution.py:110
  47.3 3.3 %collective-permute-start = (f32[2,256]{1,0:T(2,128)S(1)}, f32[2,256]{1,0:T(2,128)S(1)}, u32[]{:S(2)}, u32[]{:S(2)}) collective-permute-start(f32[2,256]{1,0:T(2,128)S(1)} %copy-done.2), channel_id=1, source_target_pairs={{0,1},{1,2},{2,3},{3,0},{4,5},{5,6},{6,7},{7,4},{8,9},{9,10},{10,1... | collective-permute-start | bytes 6152 | tf_op jit(solution)/shard_map/ppermute | solution.py:133
  49.2 22.5 %collective-permute-start.1 = (f32[2,256]{1,0:T(2,128)S(1)}, f32[2,256]{1,0:T(2,128)S(1)}, u32[]{:S(2)}, u32[]{:S(2)}) collective-permute-start(f32[2,256]{1,0:T(2,128)S(1)} %copy-done.2), channel_id=1, source_target_pairs={{0,2},{1,3},{2,0},{3,1},{4,6},{5,7},{6,4},{7,5},{8,10},{9,11},{10,... | collective-permute-start | bytes 6152 | tf_op jit(solution)/shard_map/ppermute | solution.py:133
  49.9 21.8 %collective-permute-start.2 = (f32[2,256]{1,0:T(2,128)S(1)}, f32[2,256]{1,0:T(2,128)S(1)}, u32[]{:S(2)}, u32[]{:S(2)}) collective-permute-start(f32[2,256]{1,0:T(2,128)S(1)} %copy-done.2), channel_id=1, source_target_pairs={{0,3},{1,0},{2,1},{3,2},{4,7},{5,4},{6,5},{7,6},{8,11},{9,8},{10,9... | collective-permute-start | bytes 6152 | tf_op jit(solution)/shard_map/ppermute | solution.py:133
  124.1 16.0 %all-to-all-start.1 = ((f32[128,2,17]{2,1,0:T(2,128)}), f32[128,2,17]{2,1,0:T(2,128)S(1)}, u32[]{:S(2)}, u32[]{:S(2)}) async-start(f32[128,2,17]{2,1,0:T(2,128)} %copy.34), calls=%async_computation.1 | async-start | bytes 262144 | tf_op jit(solution)/shard_map/all_to_all | solution.py:125

commit v5 on v4

--- a/solution.py
+++ b/solution.py
@@ -9,6 +9,7 @@
 
 BINS = 1024
 ITERS = 64
+CHUNKS = 4
 
 
 def dft_table(length):
@@ -104,11 +105,19 @@
     row_transform = row_transform.reshape(pixels, 2, pixels)
     cos_part = table[:, :pixels]
     sin_part = table[:, pixels:]
-    mixing = jnp.stack([table, jnp.concatenate([-sin_part, cos_part], axis=1)])
-    spectrum = jnp.einsum("ypk,pyj->kj", row_transform, mixing, preferred_element_type=jnp.float32)
-    spectrum = spectrum.astype(jnp.bfloat16).reshape(devices, pixels // devices, 2 * pixels)
-    gathered = lax.all_to_all(spectrum, ("tm", "qband"), 0, 0, tiled=True)
-    structure = structure_block(gathered, lag_list)
+    width = pixels // CHUNKS
+    pieces_out = []
+    for k in range(CHUNKS):
+        cols = slice(k * width, (k + 1) * width)
+        mixing = jnp.stack([
+            jnp.concatenate([cos_part[:, cols], sin_part[:, cols]], axis=1),
+            jnp.concatenate([-sin_part[:, cols], cos_part[:, cols]], axis=1),
+        ])
+        spectrum = jnp.einsum("ypk,pyj->kj", row_transform, mixing, preferred_element_type=jnp.float32)
+        spectrum = spectrum.astype(jnp.bfloat16).reshape(devices, pixels // devices, 2 * width)
+        gathered = lax.all_to_all(spectrum, ("tm", "qband"), 0, 0, tiled=True)
+        pieces_out.append(structure_block(gathered, lag_list))
+    structure = jnp.concatenate(pieces_out, axis=2)
 
     bands_dev = decay_rates.shape[0]
     bands_total = bands_dev * lax.axis_size("tm")

time: 159 us -> 221 us (1.39)
  Pallas kernels: 37.4 us -> 68.7 us
  starting transfers between devices: 20.3 us -> 47.7 us
  waiting for transfers between devices: 59 us -> 45.5 us
  matrix products: 15.4 us -> 25.1 us
  other arithmetic: 21.8 us -> 28.7 us
    pallas_call x1 -> x4, Pallas kernels: 22.1 us -> 53.4 us  [structure_block(): pl.pallas_call(structure_kernel, out_shape=jax.ShapeDtypeStruct((nlag, ro...]
    ppermute x3, waiting for transfers between devices: 21.5 us -> 0.47 us  [on_device(): lax.ppermute(decay_rates, 'qband', [(j, (j + s) % ring) for j in range(ri...]
    all_to_all x1 -> x4, starting transfers between devices: 11.9 us -> 26 us  [on_device(): gathered = lax.all_to_all(spectrum, ('tm', 'qband'), 0, 0, tiled=True)]
    all_to_all x1, starting transfers between devices: 5.79 us -> 17.9 us  [on_device(): received = lax.all_to_all(per_dest, ('tm', 'qband'), 0, 0, tiled=True)]
    dot_general x1 -> x4, matrix products: 10.4 us -> 19.9 us  [on_device(): jnp.einsum('ypk,pyj->kj', row_transform, mixing, preferred_element_type=j...]
    all_to_all x1 -> x4, waiting for transfers between devices: 27.3 us -> 35.7 us  [on_device(): gathered = lax.all_to_all(spectrum, ('tm', 'qband'), 0, 0, tiled=True)]
    another operation x2 -> x5, other arithmetic: 18.8 us -> 23.6 us
    slice x0 -> x1, other arithmetic: none -> 2.27 us  [on_device(): sin_part[:, cols]]
  transfers between devices with their start and end apart: 5 -> 8, of which waited for: 4 -> 6; matrix products, arithmetic and copies ran while one was open for 1% -> 11% of each run, Pallas kernels for 0% -> 18%
where the time goes in v5:
time: 221 us; the launch traced here: 222 us
  Pallas kernels  68.7 us (31%)
  starting transfers between devices  47.7 us (22%)
  waiting for transfers between devices  45.5 us (21%)
  other arithmetic  28.7 us (13%)
  matrix products  25.1 us (11%)
  local copies, waits for them, and re-layouts  5.45 us (2%)
    pallas_call x4, Pallas kernels, structure_block(): pl.pallas_call(structure_kernel, out_shape=jax.ShapeDtypeStruct((nlag, ro...  53.4 us
    all_to_all x4, waiting for transfers between devices, on_device(): gathered = lax.all_to_all(spectrum, ('tm', 'qband'), 0, 0, tiled=True)  35.7 us
    all_to_all x4, starting transfers between devices, on_device(): gathered = lax.all_to_all(spectrum, ('tm', 'qband'), 0, 0, tiled=True)  26 us
    dot_general x4, matrix products, on_device(): jnp.einsum('ypk,pyj->kj', row_transform, mixing, preferred_element_type=j...  19.9 us
    another operation x1, other arithmetic  18.3 us
    all_to_all x1, starting transfers between devices, on_device(): received = lax.all_to_all(per_dest, ('tm', 'qband'), 0, 0, tiled=True)  17.9 us
    pallas_call x1, Pallas kernels, fit_bands(): pl.pallas_call(fit_kernel, out_shape=jax.ShapeDtypeStruct((bands, 1, bins...  15.3 us
    all_to_all x1, waiting for transfers between devices, on_device(): received = lax.all_to_all(per_dest, ('tm', 'qband'), 0, 0, tiled=True)  9.34 us
  transfers between devices with their start and end apart: 8, of which 6 were waited for; matrix products, arithmetic and copies ran while one was open for 11% of the time, Pallas kernels for 18%

profile of v5, /device:TPU:1, one launch (start us, length us, event | category | flops | bytes accessed | tf_op | source)
XLA Modules:
  0.0 222.0 jit_solution(4477021347426717414)
XLA Ops:
  0.6 18.3 %multiply_convert_fusion = (bf16[1024,1024]{1,0:T(8,128)(2,1)S(1)}, bf16[1024,1024]{1,0:T(8,128)(2,1)S(1)}) fusion(), kind=kLoop, calls=%fused_computation.8 | loop fusion | flops 26214400 | bytes 4194304 | tf_op jit(solution)/shard_map/convert.1
  19.4 2.3 %fusion.54 = (bf16[1024,256]{1,0:T(8,128)(2,1)}, bf16[1024,256]{1,0:T(8,128)(2,1)}, bf16[1024,256]{1,0:T(8,128)(2,1)}, bf16[1024,256]{1,0:T(8,128)(2,1)}, bf16[1...) fusion(bf16[1024,2048]{1,0:T(8,128)(2,1)S(1)} %pad_maximum_fusion), kind=kLoop, calls=%fused_computation.73 | loop fusion | flops 1048576 | bytes 10485760 | tf_op jit(solution)/shard_map/slice | solution.py:113
  21.7 4.8 %convolution_convert_fusion = bf16[2048,1024]{1,0:T(8,128)(2,1)S(1)} fusion(bf16[1024,2048]{1,0:T(8,128)(2,1)S(1)} %pad_maximum_fusion, bf16[1,1024,1024]{2,1,0:T(8,128)(2,1)S(1)} %copy-done), kind=kOutput, calls=%fused_computation.14 | convolution fusion | flops 4297064448 | bytes 10485760 | tf_op jit(solution)/shard_map/dot_general | solution.py:104
  26.7 1.8 copy-done.4
  28.5 3.3 %fusion.40 = bf16[128,8,512]{2,1,0:T(8,128)(2,1)} fusion(bf16[1024,2,1024]{0,2,1:T(8,128)(2,1)S(1)} %bitcast.66, bf16[1,1024,512]{2,1,0:T(8,128)(2,1)S(1)} %get-tuple-element.21, bf16[1,1024,512]{2,1,0:T(8,128)(2,1)S(1)} %get-tuple-element.20), kind=kOutput, calls=%fused_computation.39 | convolution fusion | flops 2149056512 | bytes 7340032 | tf_op jit(solution)/shard_map/ypk,pyj->kj/dot_general | solution.py:116
  31.8 11.5 %all-to-all-start.3 = ((bf16[128,8,512]{2,1,0:T(8,128)(2,1)}), bf16[128,8,512]{2,1,0:T(8,128)(2,1)S(1)}, u32[]{:S(2)}, u32[]{:S(2)}) async-start(bf16[128,8,512]{2,1,0:T(8,128)(2,1)} %fusion.40), calls=%async_computation.3 | async-start | bytes 2097152 | tf_op jit(solution)/shard_map/all_to_all | solution.py:118
  43.3 1.7 maximum_bitcast_fusion.4
  45.0 5.5 %fusion.37 = bf16[128,8,512]{2,1,0:T(8,128)(2,1)} fusion(bf16[1024,2,1024]{0,2,1:T(8,128)(2,1)} %bitcast.67, bf16[1,1024,512]{2,1,0:T(8,128)(2,1)S(1)} %get-tuple-element.19, bf16[1,1024,512]{2,1,0:T(8,128)(2,1)S(1)} %get-tuple-element.18), kind=kOutput, calls=%fused_computation.38 | convolution fusion | flops 2149056512 | bytes 7340032 | tf_op jit(solution)/shard_map/ypk,pyj->kj/dot_general | solution.py:116
  50.5 12.1 %all-to-all-done.3.x_ref = bf16[128,8,512]{2,1,0:T(8,128)(2,1)S(1)} async-done(((bf16[128,8,512]{2,1,0:T(8,128)(2,1)}), bf16[128,8,512]{2,1,0:T(8,128)(2,1)S(1)}, u32[]{:S(2)}, u32[]{:S(2)}) %all-to-all-start.3) | async-done | bytes 1048608 | tf_op jit(solution)/shard_map/all_to_all | solution.py:118
  62.6 4.8 %all-to-all-start.2 = ((bf16[128,8,512]{2,1,0:T(8,128)(2,1)}), bf16[128,8,512]{2,1,0:T(8,128)(2,1)}, u32[]{:S(2)}, u32[]{:S(2)}) async-start(bf16[128,8,512]{2,1,0:T(8,128)(2,1)} %fusion.37), calls=%async_computation.2 | async-start | bytes 2097152 | tf_op jit(solution)/shard_map/all_to_all | solution.py:118
  69.1 5.5 %fusion.31 = bf16[128,8,512]{2,1,0:T(8,128)(2,1)} fusion(bf16[1024,2,1024]{0,2,1:T(8,128)(2,1)} %bitcast.68, bf16[1,1024,512]{2,1,0:T(8,128)(2,1)S(1)} %get-tuple-element.15, bf16[1,1024,512]{2,1,0:T(8,128)(2,1)S(1)} %get-tuple-element.14), kind=kOutput, calls=%fused_computation.36 | convolution fusion | flops 2149056512 | bytes 7340032 | tf_op jit(solution)/shard_map/ypk,pyj->kj/dot_general | solution.py:116
  74.6 11.9 %all-to-all-done.2.x_ref = bf16[128,8,512]{2,1,0:T(8,128)(2,1)} async-done(((bf16[128,8,512]{2,1,0:T(8,128)(2,1)}), bf16[128,8,512]{2,1,0:T(8,128)(2,1)}, u32[]{:S(2)}, u32[]{:S(2)}) %all-to-all-start.2) | async-done | bytes 1048608 | tf_op jit(solution)/shard_map/all_to_all | solution.py:118
  86.5 5.0 %all-to-all-start = ((bf16[128,8,512]{2,1,0:T(8,128)(2,1)}), bf16[128,8,512]{2,1,0:T(8,128)(2,1)}, u32[]{:S(2)}, u32[]{:S(2)}) async-start(bf16[128,8,512]{2,1,0:T(8,128)(2,1)} %fusion.31), calls=%async_computation | async-start | bytes 2097152 | tf_op jit(solution)/shard_map/all_to_all | solution.py:118
  91.5 1.8 maximum_bitcast_fusion.2
  93.2 5.5 %fusion.34 = bf16[128,8,512]{2,1,0:T(8,128)(2,1)} fusion(bf16[1024,2,1024]{0,2,1:T(8,128)(2,1)} %bitcast.69, bf16[1,1024,512]{2,1,0:T(8,128)(2,1)S(1)} %get-tuple-element.17, bf16[1,1024,512]{2,1,0:T(8,128)(2,1)S(1)} %get-tuple-element.16), kind=kOutput, calls=%fused_computation.37 | convolution fusion | flops 2149056512 | bytes 7340032 | tf_op jit(solution)/shard_map/ypk,pyj->kj/dot_general | solution.py:116
  98.8 11.8 %all-to-all-done.x_ref = bf16[128,8,512]{2,1,0:T(8,128)(2,1)} async-done(((bf16[128,8,512]{2,1,0:T(8,128)(2,1)}), bf16[128,8,512]{2,1,0:T(8,128)(2,1)}, u32[]{:S(2)}, u32[]{:S(2)}) %all-to-all-start) | async-done | bytes 1048608 | tf_op jit(solution)/shard_map/all_to_all | solution.py:118
  110.5 4.8 %all-to-all-start.1 = ((bf16[128,8,512]{2,1,0:T(8,128)(2,1)}), bf16[128,8,512]{2,1,0:T(8,128)(2,1)}, u32[]{:S(2)}, u32[]{:S(2)}) async-start(bf16[128,8,512]{2,1,0:T(8,128)(2,1)} %fusion.34), calls=%async_computation.1 | async-start | bytes 2097152 | tf_op jit(solution)/shard_map/all_to_all | solution.py:118
  120.6 12.8 %shard_map.62 = f32[16,8,256]{2,1,0:T(8,128)S(1)} custom-call(s32[16]{0:T(128)S(1)} %copy-done.1, bf16[128,8,512]{2,1,0:T(8,128)(2,1)S(1)} %all-to-all-done.3.x_ref), custom_call_target="tpu_custom_call" | custom-call | tf_op jit(solution)/shard_map/pallas_call | solution.py:55
  133.5 13.5 %shard_map.61 = f32[16,8,256]{2,1,0:T(8,128)S(1)} custom-call(s32[16]{0:T(128)S(1)} %copy-done.1, bf16[128,8,512]{2,1,0:T(8,128)(2,1)} %all-to-all-done.2.x_ref), custom_call_target="tpu_custom_call" | custom-call | tf_op jit(solution)/shard_map/pallas_call | solution.py:55
  147.1 13.5 %shard_map.59 = f32[16,8,256]{2,1,0:T(8,128)S(1)} custom-call(s32[16]{0:T(128)S(1)} %copy-done.1, bf16[128,8,512]{2,1,0:T(8,128)(2,1)} %all-to-all-done.x_ref), custom_call_target="tpu_custom_call" | custom-call | tf_op jit(solution)/shard_map/pallas_call | solution.py:55
  160.7 13.5 %shard_map.60 = f32[16,8,256]{2,1,0:T(8,128)S(1)} custom-call(s32[16]{0:T(128)S(1)} %copy-done.1, bf16[128,8,512]{2,1,0:T(8,128)(2,1)} %all-to-all-done.1.x_ref), custom_call_target="tpu_custom_call" | custom-call | tf_op jit(solution)/shard_map/pallas_call | solution.py:55
  175.5 17.9 %all-to-all-start.4 = ((f32[128,2,17]{2,1,0:T(2,128)}), f32[128,2,17]{2,1,0:T(2,128)S(1)}, u32[]{:S(2)}, u32[]{:S(2)}) async-start(f32[128,2,17]{2,1,0:T(2,128)} %copy.29), calls=%async_computation.4 | async-start | bytes 262144 | tf_op jit(solution)/shard_map/all_to_all | solution.py:134
  194.3 9.3 %all-to-all-done.4 = f32[128,2,17]{2,1,0:T(2,128)S(1)} async-done(((f32[128,2,17]{2,1,0:T(2,128)}), f32[128,2,17]{2,1,0:T(2,128)S(1)}, u32[]{:S(2)}, u32[]{:S(2)}) %all-to-all-start.4) | async-done | bytes 17440 | tf_op jit(solution)/shard_map/all_to_all | solution.py:134
  205.4 15.3 %shard_map.63 = f32[2,1,1024]{2,1,0:T(1,128)} custom-call(f32[2,16,1024]{2,1,0:T(8,128)} %get-tuple-element.23.k_ref, f32[2,16,128]{2,1,0:T(8,128)} %broadcast_in_dim.20.tgt_ref, f32[2,1,1024]{2,1,0:T(1,128)} %broadcast_in_dim.38.step_ref), custom_call_target="tpu_custom_call" | custom-call | tf_op jit(solution)/shard_map/pallas_call | solution.py:93
  (43 shorter events, 12.9 us)
Async XLA Ops:
  0.6 21.1 %copy-start = (bf16[1,1024,1024]{2,1,0:T(8,128)(2,1)S(1)}, bf16[1,1024,1024]{2,1,0:T(8,128)(2,1)}, u32[]{:S(2)}) copy-start(bf16[1,1024,1024]{2,1,0:T(8,128)(2,1)} %param.4) | copy-start | bytes 6291460
  26.5 1.9 copy-start.4
  31.8 30.8 %all-to-all-start.3 = ((bf16[128,8,512]{2,1,0:T(8,128)(2,1)}), bf16[128,8,512]{2,1,0:T(8,128)(2,1)S(1)}, u32[]{:S(2)}, u32[]{:S(2)}) async-start(bf16[128,8,512]{2,1,0:T(8,128)(2,1)} %fusion.40), calls=%async_computation.3 | async-start | bytes 2097152 | tf_op jit(solution)/shard_map/all_to_all | solution.py:118
  62.6 23.9 %all-to-all-start.2 = ((bf16[128,8,512]{2,1,0:T(8,128)(2,1)}), bf16[128,8,512]{2,1,0:T(8,128)(2,1)}, u32[]{:S(2)}, u32[]{:S(2)}) async-start(bf16[128,8,512]{2,1,0:T(8,128)(2,1)} %fusion.37), calls=%async_computation.2 | async-start | bytes 2097152 | tf_op jit(solution)/shard_map/all_to_all | solution.py:118
  86.5 24.1 %all-to-all-start = ((bf16[128,8,512]{2,1,0:T(8,128)(2,1)}), bf16[128,8,512]{2,1,0:T(8,128)(2,1)}, u32[]{:S(2)}, u32[]{:S(2)}) async-start(bf16[128,8,512]{2,1,0:T(8,128)(2,1)} %fusion.31), calls=%async_computation | async-start | bytes 2097152 | tf_op jit(solution)/shard_map/all_to_all | solution.py:118
  93.2 22.1 %copy-start.2 = (f32[2,256]{1,0:T(2,128)S(1)}, f32[2,256]{1,0:T(2,128)}, u32[]{:S(2)}) copy-start(f32[2,256]{1,0:T(2,128)} %param.7) | copy-start | bytes 6148
  93.2 25.8 %copy-start.3 = (s32[8,1]{0,1:T(1,128)S(1)}, s32[8,1]{0,1:T(1,128)}, u32[]{:S(2)}) copy-start(s32[8,1]{0,1:T(1,128)} %param.6) | copy-start | bytes 100
  93.2 25.9 %copy-start.1 = (s32[16]{0:T(128)S(1)}, s32[16]{0:T(128)}, u32[]{:S(2)}) copy-start(s32[16]{0:T(128)} %lags_ref.7) | copy-start | bytes 196
  110.5 50.2 %all-to-all-start.1 = ((bf16[128,8,512]{2,1,0:T(8,128)(2,1)}), bf16[128,8,512]{2,1,0:T(8,128)(2,1)}, u32[]{:S(2)}, u32[]{:S(2)}) async-start(bf16[128,8,512]{2,1,0:T(8,128)(2,1)} %fusion.34), calls=%async_computation.1 | async-start | bytes 2097152 | tf_op jit(solution)/shard_map/all_to_all | solution.py:118
  115.3 4.0 %collective-permute-start.2 = (f32[2,256]{1,0:T(2,128)S(1)}, f32[2,256]{1,0:T(2,128)S(1)}, u32[]{:S(2)}, u32[]{:S(2)}) collective-permute-start(f32[2,256]{1,0:T(2,128)S(1)} %copy-done.2), channel_id=1, source_target_pairs={{0,3},{1,0},{2,1},{3,2},{4,7},{5,4},{6,5},{7,6},{8,11},{9,8},{10,9... | collective-permute-start | bytes 6152 | tf_op jit(solution)/shard_map/ppermute | solution.py:142
  116.7 2.9 %collective-permute-start.1 = (f32[2,256]{1,0:T(2,128)S(1)}, f32[2,256]{1,0:T(2,128)S(1)}, u32[]{:S(2)}, u32[]{:S(2)}) collective-permute-start(f32[2,256]{1,0:T(2,128)S(1)} %copy-done.2), channel_id=1, source_target_pairs={{0,2},{1,3},{2,0},{3,1},{4,6},{5,7},{6,4},{7,5},{8,10},{9,11},{10,... | collective-permute-start | bytes 6152 | tf_op jit(solution)/shard_map/ppermute | solution.py:142
  117.4 2.4 %collective-permute-start = (f32[2,256]{1,0:T(2,128)S(1)}, f32[2,256]{1,0:T(2,128)S(1)}, u32[]{:S(2)}, u32[]{:S(2)}) collective-permute-start(f32[2,256]{1,0:T(2,128)S(1)} %copy-done.2), channel_id=1, source_target_pairs={{0,1},{1,2},{2,3},{3,0},{4,5},{5,6},{6,7},{7,4},{8,9},{9,10},{10,1... | collective-permute-start | bytes 6152 | tf_op jit(solution)/shard_map/ppermute | solution.py:142
  175.5 28.1 %all-to-all-start.4 = ((f32[128,2,17]{2,1,0:T(2,128)}), f32[128,2,17]{2,1,0:T(2,128)S(1)}, u32[]{:S(2)}, u32[]{:S(2)}) async-start(f32[128,2,17]{2,1,0:T(2,128)} %copy.29), calls=%async_computation.4 | async-start | bytes 262144 | tf_op jit(solution)/shard_map/all_to_all | solution.py:134

commit v6 on v5

--- a/solution.py
+++ b/solution.py
@@ -9,7 +9,8 @@
 
 BINS = 1024
 ITERS = 64
-CHUNKS = 4
+CHUNKS = 1
+UNROLL = 4
 
 
 def dft_table(length):
@@ -42,7 +43,14 @@
             d = x32_ref[t + lag] - x32_ref[t]
             return acc + d * d
 
-        acc = lax.fori_loop(0, count, step, jnp.zeros(x32_ref.shape[1:], jnp.float32))
+        def step_block(i, acc):
+            for u in range(UNROLL):
+                acc = step(i * UNROLL + u, acc)
+            return acc
+
+        blocks = count // UNROLL
+        acc = lax.fori_loop(0, blocks, step_block, jnp.zeros(x32_ref.shape[1:], jnp.float32))
+        acc = lax.fori_loop(blocks * UNROLL, count, step, acc)
         out_ref[l] = (acc[:, :pixels] + acc[:, pixels:]) / count.astype(jnp.float32)
         return carry
 

time: 221 us -> 153 us (0.69)
  Pallas kernels: 68.7 us -> 32.4 us
  starting transfers between devices: 47.7 us -> 20.3 us
  waiting for transfers between devices: 45.5 us -> 59 us
  matrix products: 25.1 us -> 15.4 us
  other arithmetic: 28.7 us -> 21.8 us
    pallas_call x4 -> x1, Pallas kernels: 53.4 us -> 17 us  [structure_block(): pl.pallas_call(structure_kernel, out_shape=jax.ShapeDtypeStruct((nlag, ro...]
    ppermute x3, waiting for transfers between devices: 0.47 us -> 21.5 us  [on_device(): lax.ppermute(decay_rates, 'qband', [(j, (j + s) % ring) for j in range(ri...]
    all_to_all x4 -> x1, starting transfers between devices: 26 us -> 11.9 us  [on_device(): gathered = lax.all_to_all(spectrum, ('tm', 'qband'), 0, 0, tiled=True)]
    all_to_all x1, starting transfers between devices: 17.9 us -> 5.79 us  [on_device(): received = lax.all_to_all(per_dest, ('tm', 'qband'), 0, 0, tiled=True)]
    dot_general x4 -> x1, matrix products: 19.9 us -> 10.4 us  [on_device(): jnp.einsum('ypk,pyj->kj', row_transform, mixing, preferred_element_type=j...]
    all_to_all x4 -> x1, waiting for transfers between devices: 35.7 us -> 27.3 us  [on_device(): gathered = lax.all_to_all(spectrum, ('tm', 'qband'), 0, 0, tiled=True)]
    another operation x4 -> x1, other arithmetic: 5.25 us -> 0.43 us  [on_device(): jnp.stack([jnp.concatenate([cos_part[:, cols], sin_part[:, cols]], axis=1...]
    slice x1 -> x0, other arithmetic: 2.27 us -> none  [on_device(): sin_part[:, cols]]
  transfers between devices with their start and end apart: 8 -> 5, of which waited for: 6 -> 4; matrix products, arithmetic and copies ran while one was open for 11% -> 1% of each run, Pallas kernels for 18% -> 0%
where the time goes in v6:
time: 153 us
  waiting for transfers between devices  59 us (39%)
  Pallas kernels  32.4 us (21%)
  other arithmetic  21.8 us (14%)
  starting transfers between devices  20.3 us (13%)
  matrix products  15.4 us (10%)
  local copies, waits for them, and re-layouts  3.77 us (2%)
    all_to_all x1, waiting for transfers between devices, on_device(): gathered = lax.all_to_all(spectrum, ('tm', 'qband'), 0, 0, tiled=True)  27.3 us
    ppermute x3, waiting for transfers between devices, on_device(): lax.ppermute(decay_rates, 'qband', [(j, (j + s) % ring) for j in range(ri...  21.5 us
    another operation x1, other arithmetic  18.3 us
    pallas_call x1, Pallas kernels, structure_block(): pl.pallas_call(structure_kernel, out_shape=jax.ShapeDtypeStruct((nlag, ro...  17 us
    pallas_call x1, Pallas kernels, fit_bands(): pl.pallas_call(fit_kernel, out_shape=jax.ShapeDtypeStruct((bands, 1, bins...  15.3 us
    all_to_all x1, starting transfers between devices, on_device(): gathered = lax.all_to_all(spectrum, ('tm', 'qband'), 0, 0, tiled=True)  11.9 us
    dot_general x1, matrix products, on_device(): jnp.einsum('ypk,pyj->kj', row_transform, mixing, preferred_element_type=j...  10.4 us
    all_to_all x1, waiting for transfers between devices, on_device(): received = lax.all_to_all(per_dest, ('tm', 'qband'), 0, 0, tiled=True)  10.2 us
  transfers between devices with their start and end apart: 5, of which 4 were waited for; matrix products, arithmetic and copies ran while one was open for 1% of the time, Pallas kernels for 0%

profile of v6, /device:TPU:1, one launch (start us, length us, event | category | flops | bytes accessed | tf_op | source)
XLA Modules:
  0.0 153.4 jit_solution(14217862878901708987)
XLA Ops:
  0.6 18.3 %multiply_convert_fusion = (bf16[1024,1024]{1,0:T(8,128)(2,1)S(1)}, bf16[1024,1024]{1,0:T(8,128)(2,1)S(1)}) fusion(), kind=kLoop, calls=%fused_computation.14 | loop fusion | flops 26214400 | bytes 4194304 | tf_op jit(solution)/shard_map/convert.1
  19.0 0.4 pad_maximum_fusion
  19.4 0.3 slice_negate_fusion
  19.7 4.9 %convolution_convert_fusion = bf16[2048,1024]{1,0:T(8,128)(2,1)S(1)} fusion(bf16[1024,2048]{1,0:T(8,128)(2,1)S(1)} %pad_maximum_fusion, bf16[1,1024,1024]{2,1,0:T(8,128)(2,1)S(1)} %copy-done), kind=kOutput, calls=%fused_computation.20 | convolution fusion | flops 4297064448 | bytes 10485760 | tf_op jit(solution)/shard_map/dot_general | solution.py:112
  24.6 0.4 maximum_bitcast_fusion
  25.0 10.4 %fusion.12 = bf16[128,8,2048]{2,1,0:T(8,128)(2,1)} fusion(bf16[1024,2,1024]{0,2,1:T(8,128)(2,1)S(1)} %bitcast.36, bf16[1,1024,2048]{2,1,0:T(8,128)(2,1)S(1)} %maximum_bitcast_fusion, bf16[1,1024,2048]{2,1,0:T(8,128)(2,1)S(1)} %bitcast.30), kind=kOutput, calls=%fused_computation.21 | convolution fusion | flops 8596226048 | bytes 16777216 | tf_op jit(solution)/shard_map/ypk,pyj->kj/dot_general | solution.py:124
  35.4 11.9 %all-to-all-start = ((bf16[128,8,2048]{2,1,0:T(8,128)(2,1)}), bf16[128,8,2048]{2,1,0:T(8,128)(2,1)}, u32[]{:S(2)}, u32[]{:S(2)}) async-start(bf16[128,8,2048]{2,1,0:T(8,128)(2,1)} %fusion.12), calls=%async_computation | async-start | bytes 8388608 | tf_op jit(solution)/shard_map/all_to_all | solution.py:126
  47.3 1.8 %collective-permute-start = (f32[2,256]{1,0:T(2,128)S(1)}, f32[2,256]{1,0:T(2,128)S(1)}, u32[]{:S(2)}, u32[]{:S(2)}) collective-permute-start(f32[2,256]{1,0:T(2,128)S(1)} %copy-done.2), channel_id=1, source_target_pairs={{0,1},{1,2},{2,3},{3,0},{4,5},{5,6},{6,7},{7,4},{8,9},{9,10},{10,1... | collective-permute-start | bytes 6152 | tf_op jit(solution)/shard_map/ppermute | solution.py:150
  49.2 0.7 collective-permute-start.1
  50.2 0.4 collective-permute-done
  50.6 21.0 %collective-permute-done.1 = f32[2,256]{1,0:T(2,128)S(1)} collective-permute-done((f32[2,256]{1,0:T(2,128)S(1)}, f32[2,256]{1,0:T(2,128)S(1)}, u32[]{:S(2)}, u32[]{:S(2)}) %collective-permute-start.1) | collective-permute-done | bytes 2080 | tf_op jit(solution)/shard_map/ppermute | solution.py:150
  71.7 0.8 multiply_reduce_fusion
  72.4 27.3 %all-to-all-done.x_ref = bf16[128,8,2048]{2,1,0:T(8,128)(2,1)} async-done(((bf16[128,8,2048]{2,1,0:T(8,128)(2,1)}), bf16[128,8,2048]{2,1,0:T(8,128)(2,1)}, u32[]{:S(2)}, u32[]{:S(2)}) %all-to-all-start) | async-done | bytes 4194336 | tf_op jit(solution)/shard_map/all_to_all | solution.py:126
  99.8 17.0 %shard_map.59 = f32[16,8,1024]{2,1,0:T(8,128)} custom-call(s32[16]{0:T(128)S(1)} %copy-done.1, bf16[128,8,2048]{2,1,0:T(8,128)(2,1)} %all-to-all-done.x_ref), custom_call_target="tpu_custom_call" | custom-call | tf_op jit(solution)/shard_map/pallas_call | solution.py:63
  116.8 1.1 reduce_sum.36
  118.0 0.2 convolution_bitcast_fusion
  118.3 0.7 copy.34
  119.1 5.8 %all-to-all-start.1 = ((f32[128,2,17]{2,1,0:T(2,128)}), f32[128,2,17]{2,1,0:T(2,128)S(1)}, u32[]{:S(2)}, u32[]{:S(2)}) async-start(f32[128,2,17]{2,1,0:T(2,128)} %copy.34), calls=%async_computation.1 | async-start | bytes 262144 | tf_op jit(solution)/shard_map/all_to_all | solution.py:142
  124.9 10.2 %all-to-all-done.1 = f32[128,2,17]{2,1,0:T(2,128)S(1)} async-done(((f32[128,2,17]{2,1,0:T(2,128)}), f32[128,2,17]{2,1,0:T(2,128)S(1)}, u32[]{:S(2)}, u32[]{:S(2)}) %all-to-all-start.1) | async-done | bytes 17440 | tf_op jit(solution)/shard_map/all_to_all | solution.py:142
  135.4 0.7 broadcast_in_dim.20.tgt_ref
  136.1 0.7 broadcast_in_dim.38.step_ref
  136.8 15.3 %shard_map.60 = f32[2,1,1024]{2,1,0:T(1,128)} custom-call(f32[2,16,1024]{2,1,0:T(8,128)} %get-tuple-element.5.k_ref, f32[2,16,128]{2,1,0:T(8,128)} %broadcast_in_dim.20.tgt_ref, f32[2,1,1024]{2,1,0:T(1,128)} %broadcast_in_dim.38.step_ref), custom_call_target="tpu_custom_call" | custom-call | tf_op jit(solution)/shard_map/pallas_call | solution.py:101
  152.1 0.7 copy.46
  152.8 0.6 slice.23
  (24 shorter events, 0.8 us)
Async XLA Ops:
  0.6 19.1 %copy-start = (bf16[1,1024,1024]{2,1,0:T(8,128)(2,1)S(1)}, bf16[1,1024,1024]{2,1,0:T(8,128)(2,1)}, u32[]{:S(2)}) copy-start(bf16[1,1024,1024]{2,1,0:T(8,128)(2,1)} %param.4) | copy-start | bytes 6291460
  35.4 12.0 %copy-start.2 = (f32[2,256]{1,0:T(2,128)S(1)}, f32[2,256]{1,0:T(2,128)}, u32[]{:S(2)}) copy-start(f32[2,256]{1,0:T(2,128)} %param.7) | copy-start | bytes 6148
  35.4 14.5 %copy-start.3 = (s32[8,1]{0,1:T(1,128)S(1)}, s32[8,1]{0,1:T(1,128)}, u32[]{:S(2)}) copy-start(s32[8,1]{0,1:T(1,128)} %param.6) | copy-start | bytes 100
  35.4 14.8 %copy-start.1 = (s32[16]{0:T(128)S(1)}, s32[16]{0:T(128)}, u32[]{:S(2)}) copy-start(s32[16]{0:T(128)} %lags_ref.1) | copy-start | bytes 196
  35.4 64.4 %all-to-all-start = ((bf16[128,8,2048]{2,1,0:T(8,128)(2,1)}), bf16[128,8,2048]{2,1,0:T(8,128)(2,1)}, u32[]{:S(2)}, u32[]{:S(2)}) async-start(bf16[128,8,2048]{2,1,0:T(8,128)(2,1)} %fusion.12), calls=%async_computation | async-start | bytes 8388608 | tf_op jit(solution)/shard_map/all_to_all | solution.py:126
  47.3 3.3 %collective-permute-start = (f32[2,256]{1,0:T(2,128)S(1)}, f32[2,256]{1,0:T(2,128)S(1)}, u32[]{:S(2)}, u32[]{:S(2)}) collective-permute-start(f32[2,256]{1,0:T(2,128)S(1)} %copy-done.2), channel_id=1, source_target_pairs={{0,1},{1,2},{2,3},{3,0},{4,5},{5,6},{6,7},{7,4},{8,9},{9,10},{10,1... | collective-permute-start | bytes 6152 | tf_op jit(solution)/shard_map/ppermute | solution.py:150
  49.2 22.5 %collective-permute-start.1 = (f32[2,256]{1,0:T(2,128)S(1)}, f32[2,256]{1,0:T(2,128)S(1)}, u32[]{:S(2)}, u32[]{:S(2)}) collective-permute-start(f32[2,256]{1,0:T(2,128)S(1)} %copy-done.2), channel_id=1, source_target_pairs={{0,2},{1,3},{2,0},{3,1},{4,6},{5,7},{6,4},{7,5},{8,10},{9,11},{10,... | collective-permute-start | bytes 6152 | tf_op jit(solution)/shard_map/ppermute | solution.py:150
  49.9 21.8 %collective-permute-start.2 = (f32[2,256]{1,0:T(2,128)S(1)}, f32[2,256]{1,0:T(2,128)S(1)}, u32[]{:S(2)}, u32[]{:S(2)}) collective-permute-start(f32[2,256]{1,0:T(2,128)S(1)} %copy-done.2), channel_id=1, source_target_pairs={{0,3},{1,0},{2,1},{3,2},{4,7},{5,4},{6,5},{7,6},{8,11},{9,8},{10,9... | collective-permute-start | bytes 6152 | tf_op jit(solution)/shard_map/ppermute | solution.py:150
  119.1 16.0 %all-to-all-start.1 = ((f32[128,2,17]{2,1,0:T(2,128)}), f32[128,2,17]{2,1,0:T(2,128)S(1)}, u32[]{:S(2)}, u32[]{:S(2)}) async-start(f32[128,2,17]{2,1,0:T(2,128)} %copy.34), calls=%async_computation.1 | async-start | bytes 262144 | tf_op jit(solution)/shard_map/all_to_all | solution.py:142

commit v7 on v6

--- a/solution.py
+++ b/solution.py
@@ -10,7 +10,7 @@
 BINS = 1024
 ITERS = 64
 CHUNKS = 1
-UNROLL = 4
+UNROLL = 8
 
 
 def dft_table(length):
@@ -91,7 +91,7 @@
         gradient = jnp.sum(panel * residual, axis=1, keepdims=True)
         return jnp.maximum(w - step * gradient, 0.0)
 
-    w_ref[...] = lax.fori_loop(0, ITERS, body, jnp.zeros(step.shape, jnp.float32))
+    w_ref[...] = lax.fori_loop(0, ITERS, body, jnp.zeros(step.shape, jnp.float32), unroll=4)
 
 
 def fit_bands(kernel, target, step_size):

time: 153 us -> 150 us (0.980)
  Pallas kernels: 32.4 us -> 29 us
    pallas_call x1, Pallas kernels: 15.3 us -> 13.4 us  [fit_bands(): pl.pallas_call(fit_kernel, out_shape=jax.ShapeDtypeStruct((bands, 1, bins...]
where the time goes in v7:
time: 150 us
  waiting for transfers between devices  59 us (39%)
  Pallas kernels  29 us (19%)
  other arithmetic  21.8 us (15%)
  starting transfers between devices  20.3 us (14%)
  matrix products  15.4 us (10%)
  local copies, waits for them, and re-layouts  3.77 us (3%)
    all_to_all x1, waiting for transfers between devices, on_device(): gathered = lax.all_to_all(spectrum, ('tm', 'qband'), 0, 0, tiled=True)  27.3 us
    ppermute x3, waiting for transfers between devices, on_device(): lax.ppermute(decay_rates, 'qband', [(j, (j + s) % ring) for j in range(ri...  21.5 us
    another operation x1, other arithmetic  18.3 us
    pallas_call x1, Pallas kernels, structure_block(): pl.pallas_call(structure_kernel, out_shape=jax.ShapeDtypeStruct((nlag, ro...  15.6 us
    pallas_call x1, Pallas kernels, fit_bands(): pl.pallas_call(fit_kernel, out_shape=jax.ShapeDtypeStruct((bands, 1, bins...  13.4 us
    all_to_all x1, starting transfers between devices, on_device(): gathered = lax.all_to_all(spectrum, ('tm', 'qband'), 0, 0, tiled=True)  11.9 us
    dot_general x1, matrix products, on_device(): jnp.einsum('ypk,pyj->kj', row_transform, mixing, preferred_element_type=j...  10.4 us
    all_to_all x1, waiting for transfers between devices, on_device(): received = lax.all_to_all(per_dest, ('tm', 'qband'), 0, 0, tiled=True)  10.2 us
  transfers between devices with their start and end apart: 5, of which 4 were waited for; matrix products, arithmetic and copies ran while one was open for 1% of the time, Pallas kernels for 0%

profile of v7, /device:TPU:1, one launch (start us, length us, event | category | flops | bytes accessed | tf_op | source)
XLA Modules:
  0.0 150.1 jit_solution(10591127640891859186)
XLA Ops:
  0.6 18.3 %multiply_convert_fusion = (bf16[1024,1024]{1,0:T(8,128)(2,1)S(1)}, bf16[1024,1024]{1,0:T(8,128)(2,1)S(1)}) fusion(), kind=kLoop, calls=%fused_computation.14 | loop fusion | flops 26214400 | bytes 4194304 | tf_op jit(solution)/shard_map/convert.1
  19.0 0.4 pad_maximum_fusion
  19.4 0.3 slice_negate_fusion
  19.7 4.9 %convolution_convert_fusion = bf16[2048,1024]{1,0:T(8,128)(2,1)S(1)} fusion(bf16[1024,2048]{1,0:T(8,128)(2,1)S(1)} %pad_maximum_fusion, bf16[1,1024,1024]{2,1,0:T(8,128)(2,1)S(1)} %copy-done), kind=kOutput, calls=%fused_computation.20 | convolution fusion | flops 4297064448 | bytes 10485760 | tf_op jit(solution)/shard_map/dot_general | solution.py:112
  24.6 0.4 maximum_bitcast_fusion
  25.0 10.4 %fusion.12 = bf16[128,8,2048]{2,1,0:T(8,128)(2,1)} fusion(bf16[1024,2,1024]{0,2,1:T(8,128)(2,1)S(1)} %bitcast.36, bf16[1,1024,2048]{2,1,0:T(8,128)(2,1)S(1)} %maximum_bitcast_fusion, bf16[1,1024,2048]{2,1,0:T(8,128)(2,1)S(1)} %bitcast.30), kind=kOutput, calls=%fused_computation.21 | convolution fusion | flops 8596226048 | bytes 16777216 | tf_op jit(solution)/shard_map/ypk,pyj->kj/dot_general | solution.py:124
  35.4 11.9 %all-to-all-start = ((bf16[128,8,2048]{2,1,0:T(8,128)(2,1)}), bf16[128,8,2048]{2,1,0:T(8,128)(2,1)}, u32[]{:S(2)}, u32[]{:S(2)}) async-start(bf16[128,8,2048]{2,1,0:T(8,128)(2,1)} %fusion.12), calls=%async_computation | async-start | bytes 8388608 | tf_op jit(solution)/shard_map/all_to_all | solution.py:126
  47.3 1.8 %collective-permute-start = (f32[2,256]{1,0:T(2,128)S(1)}, f32[2,256]{1,0:T(2,128)S(1)}, u32[]{:S(2)}, u32[]{:S(2)}) collective-permute-start(f32[2,256]{1,0:T(2,128)S(1)} %copy-done.2), channel_id=1, source_target_pairs={{0,1},{1,2},{2,3},{3,0},{4,5},{5,6},{6,7},{7,4},{8,9},{9,10},{10,1... | collective-permute-start | bytes 6152 | tf_op jit(solution)/shard_map/ppermute | solution.py:150
  49.2 0.7 collective-permute-start.1
  50.2 0.4 collective-permute-done
  50.6 21.0 %collective-permute-done.1 = f32[2,256]{1,0:T(2,128)S(1)} collective-permute-done((f32[2,256]{1,0:T(2,128)S(1)}, f32[2,256]{1,0:T(2,128)S(1)}, u32[]{:S(2)}, u32[]{:S(2)}) %collective-permute-start.1) | collective-permute-done | bytes 2080 | tf_op jit(solution)/shard_map/ppermute | solution.py:150
  71.7 0.8 multiply_reduce_fusion
  72.4 27.3 %all-to-all-done.x_ref = bf16[128,8,2048]{2,1,0:T(8,128)(2,1)} async-done(((bf16[128,8,2048]{2,1,0:T(8,128)(2,1)}), bf16[128,8,2048]{2,1,0:T(8,128)(2,1)}, u32[]{:S(2)}, u32[]{:S(2)}) %all-to-all-start) | async-done | bytes 4194336 | tf_op jit(solution)/shard_map/all_to_all | solution.py:126
  99.8 15.6 %shard_map.59 = f32[16,8,1024]{2,1,0:T(8,128)} custom-call(s32[16]{0:T(128)S(1)} %copy-done.1, bf16[128,8,2048]{2,1,0:T(8,128)(2,1)} %all-to-all-done.x_ref), custom_call_target="tpu_custom_call" | custom-call | tf_op jit(solution)/shard_map/pallas_call | solution.py:63
  115.4 1.1 reduce_sum.36
  116.6 0.2 convolution_bitcast_fusion
  116.9 0.7 copy.34
  117.7 5.8 %all-to-all-start.1 = ((f32[128,2,17]{2,1,0:T(2,128)}), f32[128,2,17]{2,1,0:T(2,128)S(1)}, u32[]{:S(2)}, u32[]{:S(2)}) async-start(f32[128,2,17]{2,1,0:T(2,128)} %copy.34), calls=%async_computation.1 | async-start | bytes 262144 | tf_op jit(solution)/shard_map/all_to_all | solution.py:142
  123.5 10.2 %all-to-all-done.1 = f32[128,2,17]{2,1,0:T(2,128)S(1)} async-done(((f32[128,2,17]{2,1,0:T(2,128)}), f32[128,2,17]{2,1,0:T(2,128)S(1)}, u32[]{:S(2)}, u32[]{:S(2)}) %all-to-all-start.1) | async-done | bytes 17440 | tf_op jit(solution)/shard_map/all_to_all | solution.py:142
  134.1 0.7 broadcast_in_dim.20.tgt_ref
  134.7 0.7 broadcast_in_dim.38.step_ref
  135.4 13.4 %shard_map.60 = f32[2,1,1024]{2,1,0:T(1,128)} custom-call(f32[2,16,1024]{2,1,0:T(8,128)} %get-tuple-element.5.k_ref, f32[2,16,128]{2,1,0:T(8,128)} %broadcast_in_dim.20.tgt_ref, f32[2,1,1024]{2,1,0:T(1,128)} %broadcast_in_dim.38.step_ref), custom_call_target="tpu_custom_call" | custom-call | tf_op jit(solution)/shard_map/pallas_call | solution.py:101
  148.8 0.7 copy.46
  149.5 0.6 slice.23
  (24 shorter events, 0.8 us)
Async XLA Ops:
  0.6 19.1 %copy-start = (bf16[1,1024,1024]{2,1,0:T(8,128)(2,1)S(1)}, bf16[1,1024,1024]{2,1,0:T(8,128)(2,1)}, u32[]{:S(2)}) copy-start(bf16[1,1024,1024]{2,1,0:T(8,128)(2,1)} %param.4) | copy-start | bytes 6291460
  35.4 12.0 %copy-start.2 = (f32[2,256]{1,0:T(2,128)S(1)}, f32[2,256]{1,0:T(2,128)}, u32[]{:S(2)}) copy-start(f32[2,256]{1,0:T(2,128)} %param.7) | copy-start | bytes 6148
  35.4 14.5 %copy-start.3 = (s32[8,1]{0,1:T(1,128)S(1)}, s32[8,1]{0,1:T(1,128)}, u32[]{:S(2)}) copy-start(s32[8,1]{0,1:T(1,128)} %param.6) | copy-start | bytes 100
  35.4 14.8 %copy-start.1 = (s32[16]{0:T(128)S(1)}, s32[16]{0:T(128)}, u32[]{:S(2)}) copy-start(s32[16]{0:T(128)} %lags_ref.1) | copy-start | bytes 196
  35.4 64.4 %all-to-all-start = ((bf16[128,8,2048]{2,1,0:T(8,128)(2,1)}), bf16[128,8,2048]{2,1,0:T(8,128)(2,1)}, u32[]{:S(2)}, u32[]{:S(2)}) async-start(bf16[128,8,2048]{2,1,0:T(8,128)(2,1)} %fusion.12), calls=%async_computation | async-start | bytes 8388608 | tf_op jit(solution)/shard_map/all_to_all | solution.py:126
  47.3 3.3 %collective-permute-start = (f32[2,256]{1,0:T(2,128)S(1)}, f32[2,256]{1,0:T(2,128)S(1)}, u32[]{:S(2)}, u32[]{:S(2)}) collective-permute-start(f32[2,256]{1,0:T(2,128)S(1)} %copy-done.2), channel_id=1, source_target_pairs={{0,1},{1,2},{2,3},{3,0},{4,5},{5,6},{6,7},{7,4},{8,9},{9,10},{10,1... | collective-permute-start | bytes 6152 | tf_op jit(solution)/shard_map/ppermute | solution.py:150
  49.2 22.5 %collective-permute-start.1 = (f32[2,256]{1,0:T(2,128)S(1)}, f32[2,256]{1,0:T(2,128)S(1)}, u32[]{:S(2)}, u32[]{:S(2)}) collective-permute-start(f32[2,256]{1,0:T(2,128)S(1)} %copy-done.2), channel_id=1, source_target_pairs={{0,2},{1,3},{2,0},{3,1},{4,6},{5,7},{6,4},{7,5},{8,10},{9,11},{10,... | collective-permute-start | bytes 6152 | tf_op jit(solution)/shard_map/ppermute | solution.py:150
  49.9 21.8 %collective-permute-start.2 = (f32[2,256]{1,0:T(2,128)S(1)}, f32[2,256]{1,0:T(2,128)S(1)}, u32[]{:S(2)}, u32[]{:S(2)}) collective-permute-start(f32[2,256]{1,0:T(2,128)S(1)} %copy-done.2), channel_id=1, source_target_pairs={{0,3},{1,0},{2,1},{3,2},{4,7},{5,4},{6,5},{7,6},{8,11},{9,8},{10,9... | collective-permute-start | bytes 6152 | tf_op jit(solution)/shard_map/ppermute | solution.py:150
  117.7 16.0 %all-to-all-start.1 = ((f32[128,2,17]{2,1,0:T(2,128)}), f32[128,2,17]{2,1,0:T(2,128)S(1)}, u32[]{:S(2)}, u32[]{:S(2)}) async-start(f32[128,2,17]{2,1,0:T(2,128)} %copy.34), calls=%async_computation.1 | async-start | bytes 262144 | tf_op jit(solution)/shard_map/all_to_all | solution.py:142

commit v8 on v7

--- a/solution.py
+++ b/solution.py
@@ -75,6 +75,29 @@
     )(lag_list, spectrum_block)
 
 
+def table_columns(length, first, count):
+    rows = jnp.arange(length, dtype=jnp.int32)
+    cols = jnp.arange(count, dtype=jnp.int32) + first
+    phase_index = rows[:, None] * cols[None, :] % length
+    folded = jnp.minimum(phase_index, length - phase_index)
+    sign_factor = jnp.where(phase_index * 2 > length, -1.0, 1.0).astype(jnp.float32)
+    angles = folded.astype(jnp.float32) * (2.0 * math.pi / length)
+    factor = 1.0 / math.sqrt(length)
+    return jnp.stack([jnp.cos(angles) * factor, -sign_factor * jnp.sin(angles) * factor]).astype(jnp.bfloat16)
+
+
+def shared_table(length):
+    ring = lax.axis_size("qband")
+    core = lax.axis_index("qband") % 2
+    half = length // 2
+    mine = table_columns(length, core * half, half)
+    other = lax.ppermute(mine, "qband", [(j, j ^ 1) for j in range(ring)])
+    first = jnp.where(core == 0, mine, other)
+    second = jnp.where(core == 0, other, mine)
+    both = jnp.concatenate([first, second], axis=2)
+    return jnp.concatenate([both[0], both[1]], axis=1)
+
+
 def kernel_panel(decay_rates, lag_list):
     lag_values = lag_list.astype(jnp.float32)
     return (1.0 - jnp.exp(-decay_rates[:, None, :] * lag_values[None, :, None])) / BINS
@@ -108,7 +131,7 @@
 def on_device(frames, lag_list, band_index, decay_rates):
     pixels = frames.shape[1]
     devices = lax.axis_size(("tm", "qband"))
-    table = lax.optimization_barrier(dft_table(pixels))
+    table = lax.optimization_barrier(shared_table(pixels))
     row_transform = jnp.dot(frames[0], table, preferred_element_type=jnp.float32).astype(jnp.bfloat16)
     row_transform = row_transform.reshape(pixels, 2, pixels)
     cos_part = table[:, :pixels]

time: 150 us -> 150 us (level)
  other arithmetic: 21.8 us -> 17 us
  waiting for transfers between devices: 59 us -> 63.2 us
    another operation x1 -> x2, other arithmetic: 18.3 us -> 10.9 us
    ppermute x0 -> x1, waiting for transfers between devices: none -> 4.13 us  [shared_table(): other = lax.ppermute(mine, 'qband', [(j, j ^ 1) for j in range(ring)])]
    select_n x0 -> x1, other arithmetic: none -> 2.13 us  [shared_table(): first = jnp.where(core == 0, mine, other)]
  transfers between devices with their start and end apart: 5 -> 6, of which waited for: 4 -> 5; matrix products, arithmetic and copies ran while one was open for 1% -> 1% of each run, Pallas kernels for 0% -> 0%
where the time goes in v8:
time: 150 us
  waiting for transfers between devices  63.2 us (42%)
  Pallas kernels  28.7 us (19%)
  starting transfers between devices  20.7 us (14%)
  other arithmetic  17 us (11%)
  matrix products  15.4 us (10%)
  local copies, waits for them, and re-layouts  3.78 us (3%)
    all_to_all x1, waiting for transfers between devices, on_device(): gathered = lax.all_to_all(spectrum, ('tm', 'qband'), 0, 0, tiled=True)  27.4 us
    ppermute x3, waiting for transfers between devices, on_device(): lax.ppermute(decay_rates, 'qband', [(j, (j + s) % ring) for j in range(ri...  21.5 us
    pallas_call x1, Pallas kernels, structure_block(): pl.pallas_call(structure_kernel, out_shape=jax.ShapeDtypeStruct((nlag, ro...  15.3 us
    pallas_call x1, Pallas kernels, fit_bands(): pl.pallas_call(fit_kernel, out_shape=jax.ShapeDtypeStruct((bands, 1, bins...  13.4 us
    all_to_all x1, starting transfers between devices, on_device(): gathered = lax.all_to_all(spectrum, ('tm', 'qband'), 0, 0, tiled=True)  10.9 us
    dot_general x1, matrix products, on_device(): jnp.einsum('ypk,pyj->kj', row_transform, mixing, preferred_element_type=j...  10.4 us
    all_to_all x1, waiting for transfers between devices, on_device(): received = lax.all_to_all(per_dest, ('tm', 'qband'), 0, 0, tiled=True)  10.2 us
    another operation x1, other arithmetic  9.25 us
  transfers between devices with their start and end apart: 6, of which 5 were waited for; matrix products, arithmetic and copies ran while one was open for 1% of the time, Pallas kernels for 0%

profile of v8, /device:TPU:1, one launch (start us, length us, event | category | flops | bytes accessed | tf_op | source)
XLA Modules:
  0.0 149.5 jit_solution(17006596633183882262)
XLA Ops:
  0.7 9.2 %multiply_convert_fusion.1 = (bf16[1,1024,512]{2,1,0:T(8,128)(2,1)S(1)}, bf16[1,1024,512]{2,1,0:T(8,128)(2,1)S(1)}) fusion(s32[512]{0:T(512)S(1)} %iota_add_fusion), kind=kLoop, calls=%fused_computation.27 | loop fusion | flops 13107200 | bytes 2099200 | tf_op jit(solution)/shard_map/convert
  9.9 1.6 %pad_maximum_fusion.2 = bf16[2,1024,512]{2,1,0:T(8,128)(2,1)} fusion(bf16[1,1024,512]{2,1,0:T(8,128)(2,1)S(1)} %get-tuple-element.11, bf16[1,1024,512]{2,1,0:T(8,128)(2,1)S(1)} %get-tuple-element.10), kind=kLoop, calls=%fused_computation.23 | loop fusion | flops 1048576 | bytes 4194304 | tf_op jit(solution)/shard_map/stack | solution.py:86
  11.6 1.4 collective-permute-start
  13.0 4.1 %collective-permute-done = bf16[2,1024,512]{2,1,0:T(8,128)(2,1)} collective-permute-done((bf16[2,1024,512]{2,1,0:T(8,128)(2,1)}, bf16[2,1024,512]{2,1,0:T(8,128)(2,1)}, u32[]{:S(2)}, u32[]{:S(2)}) %collective-permute-start) | collective-permute-done | bytes 2097184 | tf_op jit(solution)/shard_map/ppermute | solution.py:94
  17.1 2.1 %broadcast_select_fusion.1 = (bf16[2,1024,512]{2,1,0:T(8,128)(2,1)S(1)}, bf16[2,1024,512]{2,1,0:T(8,128)(2,1)S(1)}) fusion(bf16[2,1024,512]{2,1,0:T(8,128)(2,1)} %collective-permute-done, pred[]{:T(512)S(6)} %eq.43, bf16[1,1024,512]{2,1,0:T(8,128)(2,1)} %copy-done.2, bf16[1,1024,512]{2,1,0:T(8,128)(2,1)S(1)} %get-tuple-element.10), kind=kLoop, calls=%fused_computation.32 | loop fusion | flops 3145728 | bytes 8388609 | tf_op jit(solution)/shard_map/jit(_where)/select_n | solution.py:95
  19.2 0.6 fusion.13
  20.5 4.9 %convolution_convert_fusion = bf16[2048,1024]{1,0:T(8,128)(2,1)S(1)} fusion(bf16[1024,2048]{1,0:T(8,128)(2,1)S(1)} %pad_maximum_fusion, bf16[1,1024,1024]{2,1,0:T(8,128)(2,1)S(1)} %copy-done), kind=kOutput, calls=%fused_computation.9 | convolution fusion | flops 4297064448 | bytes 10485760 | tf_op jit(solution)/shard_map/dot_general | solution.py:135
  25.8 10.4 %fusion.6 = bf16[128,8,2048]{2,1,0:T(8,128)(2,1)} fusion(bf16[1024,2,1024]{0,2,1:T(8,128)(2,1)S(1)} %bitcast.40, bf16[1,1024,2048]{2,1,0:T(8,128)(2,1)S(1)} %maximum_bitcast_fusion, bf16[1,1024,2048]{2,1,0:T(8,128)(2,1)S(1)} %bitcast.34), kind=kOutput, calls=%fused_computation.10 | convolution fusion | flops 8596226048 | bytes 16777216 | tf_op jit(solution)/shard_map/ypk,pyj->kj/dot_general | solution.py:147
  36.2 10.9 %all-to-all-start = ((bf16[128,8,2048]{2,1,0:T(8,128)(2,1)}), bf16[128,8,2048]{2,1,0:T(8,128)(2,1)}, u32[]{:S(2)}, u32[]{:S(2)}) async-start(bf16[128,8,2048]{2,1,0:T(8,128)(2,1)} %fusion.6), calls=%async_computation | async-start | bytes 8388608 | tf_op jit(solution)/shard_map/all_to_all | solution.py:149
  47.1 1.8 %collective-permute-start.1 = (f32[2,256]{1,0:T(2,128)S(1)}, f32[2,256]{1,0:T(2,128)S(1)}, u32[]{:S(2)}, u32[]{:S(2)}) collective-permute-start(f32[2,256]{1,0:T(2,128)S(1)} %copy-done.3), channel_id=1, source_target_pairs={{0,1},{1,2},{2,3},{3,0},{4,5},{5,6},{6,7},{7,4},{8,9},{9,10},{10,1... | collective-permute-start | bytes 6152 | tf_op jit(solution)/shard_map/ppermute | solution.py:173
  49.0 0.7 collective-permute-start.2
  50.4 21.0 %collective-permute-done.2 = f32[2,256]{1,0:T(2,128)S(1)} collective-permute-done((f32[2,256]{1,0:T(2,128)S(1)}, f32[2,256]{1,0:T(2,128)S(1)}, u32[]{:S(2)}, u32[]{:S(2)}) %collective-permute-start.2) | collective-permute-done | bytes 2080 | tf_op jit(solution)/shard_map/ppermute | solution.py:173
  71.5 0.8 multiply_reduce_fusion
  72.2 27.4 %all-to-all-done.x_ref = bf16[128,8,2048]{2,1,0:T(8,128)(2,1)} async-done(((bf16[128,8,2048]{2,1,0:T(8,128)(2,1)}), bf16[128,8,2048]{2,1,0:T(8,128)(2,1)}, u32[]{:S(2)}, u32[]{:S(2)}) %all-to-all-start) | async-done | bytes 4194336 | tf_op jit(solution)/shard_map/all_to_all | solution.py:149
  99.6 15.3 %shard_map.59 = f32[16,8,1024]{2,1,0:T(8,128)} custom-call(s32[16]{0:T(128)S(1)} %copy-done.1, bf16[128,8,2048]{2,1,0:T(8,128)(2,1)} %all-to-all-done.x_ref), custom_call_target="tpu_custom_call" | custom-call | tf_op jit(solution)/shard_map/pallas_call | solution.py:63
  114.9 1.1 reduce_sum.36
  116.4 0.8 copy.34
  117.1 5.8 %all-to-all-start.1 = ((f32[128,2,17]{2,1,0:T(2,128)}), f32[128,2,17]{2,1,0:T(2,128)S(1)}, u32[]{:S(2)}, u32[]{:S(2)}) async-start(f32[128,2,17]{2,1,0:T(2,128)} %copy.34), calls=%async_computation.1 | async-start | bytes 262144 | tf_op jit(solution)/shard_map/all_to_all | solution.py:165
  122.9 10.2 %all-to-all-done.1 = f32[128,2,17]{2,1,0:T(2,128)S(1)} async-done(((f32[128,2,17]{2,1,0:T(2,128)}), f32[128,2,17]{2,1,0:T(2,128)S(1)}, u32[]{:S(2)}, u32[]{:S(2)}) %all-to-all-start.1) | async-done | bytes 17440 | tf_op jit(solution)/shard_map/all_to_all | solution.py:165
  133.5 0.7 broadcast_in_dim.20.tgt_ref
  134.2 0.7 broadcast_in_dim.38.step_ref
  134.9 13.4 %shard_map.60 = f32[2,1,1024]{2,1,0:T(1,128)} custom-call(f32[2,16,1024]{2,1,0:T(8,128)} %get-tuple-element.9.k_ref, f32[2,16,128]{2,1,0:T(8,128)} %broadcast_in_dim.20.tgt_ref, f32[2,1,1024]{2,1,0:T(1,128)} %broadcast_in_dim.38.step_ref), custom_call_target="tpu_custom_call" | custom-call | tf_op jit(solution)/shard_map/pallas_call | solution.py:124
  148.2 0.7 copy.46
  148.9 0.6 slice.33
  (32 shorter events, 2.6 us)
Async XLA Ops:
  0.6 19.9 %copy-start = (bf16[1,1024,1024]{2,1,0:T(8,128)(2,1)S(1)}, bf16[1,1024,1024]{2,1,0:T(8,128)(2,1)}, u32[]{:S(2)}) copy-start(bf16[1,1024,1024]{2,1,0:T(8,128)(2,1)} %param.4) | copy-start | bytes 6291460
  9.9 1.6 %copy-start.2 = (bf16[1,1024,512]{2,1,0:T(8,128)(2,1)}, bf16[1,1024,512]{2,1,0:T(8,128)(2,1)S(1)}, u32[]{:S(2)}) copy-start(bf16[1,1024,512]{2,1,0:T(8,128)(2,1)S(1)} %get-tuple-element.11) | copy-start | bytes 3145732
  11.6 5.5 %collective-permute-start = (bf16[2,1024,512]{2,1,0:T(8,128)(2,1)}, bf16[2,1024,512]{2,1,0:T(8,128)(2,1)}, u32[]{:S(2)}, u32[]{:S(2)}) collective-permute-start(bf16[2,1024,512]{2,1,0:T(8,128)(2,1)} %pad_maximum_fusion.2), channel_id=1, source_target_pairs={{0,1},{1,0},{2,3},{3,2},{4,5},{5,4},{6,7},{7,6},{8,9},{9,8},{10,11... | collective-permute-start | bytes 6291464 | tf_op jit(solution)/shard_map/ppermute | solution.py:94
  36.2 11.0 %copy-start.3 = (f32[2,256]{1,0:T(2,128)S(1)}, f32[2,256]{1,0:T(2,128)}, u32[]{:S(2)}) copy-start(f32[2,256]{1,0:T(2,128)} %param.7) | copy-start | bytes 6148
  36.2 13.5 %copy-start.4 = (s32[8,1]{0,1:T(1,128)S(1)}, s32[8,1]{0,1:T(1,128)}, u32[]{:S(2)}) copy-start(s32[8,1]{0,1:T(1,128)} %param.6) | copy-start | bytes 100
  36.2 13.8 %copy-start.1 = (s32[16]{0:T(128)S(1)}, s32[16]{0:T(128)}, u32[]{:S(2)}) copy-start(s32[16]{0:T(128)} %lags_ref.1) | copy-start | bytes 196
  36.2 63.4 %all-to-all-start = ((bf16[128,8,2048]{2,1,0:T(8,128)(2,1)}), bf16[128,8,2048]{2,1,0:T(8,128)(2,1)}, u32[]{:S(2)}, u32[]{:S(2)}) async-start(bf16[128,8,2048]{2,1,0:T(8,128)(2,1)} %fusion.6), calls=%async_computation | async-start | bytes 8388608 | tf_op jit(solution)/shard_map/all_to_all | solution.py:149
  47.1 3.3 %collective-permute-start.1 = (f32[2,256]{1,0:T(2,128)S(1)}, f32[2,256]{1,0:T(2,128)S(1)}, u32[]{:S(2)}, u32[]{:S(2)}) collective-permute-start(f32[2,256]{1,0:T(2,128)S(1)} %copy-done.3), channel_id=1, source_target_pairs={{0,1},{1,2},{2,3},{3,0},{4,5},{5,6},{6,7},{7,4},{8,9},{9,10},{10,1... | collective-permute-start | bytes 6152 | tf_op jit(solution)/shard_map/ppermute | solution.py:173
  49.0 22.5 %collective-permute-start.2 = (f32[2,256]{1,0:T(2,128)S(1)}, f32[2,256]{1,0:T(2,128)S(1)}, u32[]{:S(2)}, u32[]{:S(2)}) collective-permute-start(f32[2,256]{1,0:T(2,128)S(1)} %copy-done.3), channel_id=1, source_target_pairs={{0,2},{1,3},{2,0},{3,1},{4,6},{5,7},{6,4},{7,5},{8,10},{9,11},{10,... | collective-permute-start | bytes 6152 | tf_op jit(solution)/shard_map/ppermute | solution.py:173
  49.7 21.8 %collective-permute-start.3 = (f32[2,256]{1,0:T(2,128)S(1)}, f32[2,256]{1,0:T(2,128)S(1)}, u32[]{:S(2)}, u32[]{:S(2)}) collective-permute-start(f32[2,256]{1,0:T(2,128)S(1)} %copy-done.3), channel_id=1, source_target_pairs={{0,3},{1,0},{2,1},{3,2},{4,7},{5,4},{6,5},{7,6},{8,11},{9,8},{10,9... | collective-permute-start | bytes 6152 | tf_op jit(solution)/shard_map/ppermute | solution.py:173
  117.1 16.0 %all-to-all-start.1 = ((f32[128,2,17]{2,1,0:T(2,128)}), f32[128,2,17]{2,1,0:T(2,128)S(1)}, u32[]{:S(2)}, u32[]{:S(2)}) async-start(f32[128,2,17]{2,1,0:T(2,128)} %copy.34), calls=%async_computation.1 | async-start | bytes 262144 | tf_op jit(solution)/shard_map/all_to_all | solution.py:165

commit v9 on v7

--- a/solution.py
+++ b/solution.py
@@ -81,26 +81,57 @@
 
 
 def fit_kernel(k_ref, tgt_ref, step_ref, w_ref):
-    panel = k_ref[...]
-    tgt = tgt_ref[...][:, :, 0:1]
-    step = step_ref[...]
+    bands, lags, bins = k_ref.shape
+    halves = lags // 8
+    tiles = bins // 128
 
-    def body(i, w):
-        predicted = jnp.sum(panel * w, axis=2, keepdims=True)
-        residual = predicted - tgt
-        gradient = jnp.sum(panel * residual, axis=1, keepdims=True)
-        return jnp.maximum(w - step * gradient, 0.0)
+    def lane_total(x):
+        shift = 64
+        while shift >= 1:
+            x = x + pltpu.roll(x, shift, 1)
+            shift //= 2
+        return x
 
-    w_ref[...] = lax.fori_loop(0, ITERS, body, jnp.zeros(step.shape, jnp.float32), unroll=4)
+    def sublane_total(x):
+        shift = 4
+        while shift >= 1:
+            x = x + pltpu.roll(x, shift, 0)
+            shift //= 2
+        return x
+
+    def body(it, w):
+        new_w = []
+        for b in range(bands):
+            residual = []
+            for h in range(halves):
+                acc = None
+                for i in range(tiles):
+                    term = k_ref[b, h * 8:(h + 1) * 8, i * 128:(i + 1) * 128] * w[b * tiles + i]
+                    acc = term if acc is None else acc + term
+                residual.append(lane_total(acc) - tgt_ref[b, h * 8:(h + 1) * 8, :])
+            step = step_ref[b]
+            for i in range(tiles):
+                g = None
+                for h in range(halves):
+                    term = k_ref[b, h * 8:(h + 1) * 8, i * 128:(i + 1) * 128] * residual[h]
+                    g = term if g is None else g + term
+                new_w.append(jnp.maximum(w[b * tiles + i] - step * sublane_total(g), 0.0))
+        return tuple(new_w)
+
+    init = tuple(jnp.zeros((8, 128), jnp.float32) for _ in range(bands * tiles))
+    w = lax.fori_loop(0, ITERS, body, init)
+    for b in range(bands):
+        for i in range(tiles):
+            w_ref[b, :, i * 128:(i + 1) * 128] = w[b * tiles + i]
 
 
 def fit_bands(kernel, target, step_size):
     bands, lags, bins = kernel.shape
     tgt = jnp.broadcast_to(target[:, :, None], (bands, lags, 128))
-    step = jnp.broadcast_to(step_size[:, None, None], (bands, 1, bins))
+    step = jnp.broadcast_to(step_size[:, None, None], (bands, 8, 128))
     out = pl.pallas_call(
         fit_kernel,
-        out_shape=jax.ShapeDtypeStruct((bands, 1, bins), jnp.float32),
+        out_shape=jax.ShapeDtypeStruct((bands, 8, bins), jnp.float32),
     )(kernel, tgt, step)
     return out[:, 0, :]
 

time: 150 us -> 171 us (1.14)
  Pallas kernels: 29 us -> 49.5 us
    pallas_call x1, Pallas kernels: 13.4 us -> 34.8 us  [fit_bands(): pl.pallas_call(fit_kernel, out_shape=jax.ShapeDtypeStruct((bands, 8, bins...]
where the time goes in v9:
time: 171 us
  waiting for transfers between devices  59 us (35%)
  Pallas kernels  49.5 us (29%)
  other arithmetic  21.8 us (13%)
  starting transfers between devices  20.3 us (12%)
  matrix products  15.4 us (9%)
  local copies, waits for them, and re-layouts  3.92 us (2%)
    pallas_call x1, Pallas kernels, fit_bands(): pl.pallas_call(fit_kernel, out_shape=jax.ShapeDtypeStruct((bands, 8, bins...  34.8 us
    all_to_all x1, waiting for transfers between devices, on_device(): gathered = lax.all_to_all(spectrum, ('tm', 'qband'), 0, 0, tiled=True)  27.3 us
    ppermute x3, waiting for transfers between devices, on_device(): lax.ppermute(decay_rates, 'qband', [(j, (j + s) % ring) for j in range(ri...  21.5 us
    another operation x1, other arithmetic  18.3 us
    pallas_call x1, Pallas kernels, structure_block(): pl.pallas_call(structure_kernel, out_shape=jax.ShapeDtypeStruct((nlag, ro...  14.7 us
    all_to_all x1, starting transfers between devices, on_device(): gathered = lax.all_to_all(spectrum, ('tm', 'qband'), 0, 0, tiled=True)  11.9 us
    dot_general x1, matrix products, on_device(): jnp.einsum('ypk,pyj->kj', row_transform, mixing, preferred_element_type=j...  10.4 us
    all_to_all x1, waiting for transfers between devices, on_device(): received = lax.all_to_all(per_dest, ('tm', 'qband'), 0, 0, tiled=True)  10.2 us
  transfers between devices with their start and end apart: 5, of which 4 were waited for; matrix products, arithmetic and copies ran while one was open for 1% of the time, Pallas kernels for 0%

profile of v9, /device:TPU:1, one launch (start us, length us, event | category | flops | bytes accessed | tf_op | source)
XLA Modules:
  0.0 170.7 jit_solution(8220295057267702655)
XLA Ops:
  0.6 18.3 %multiply_convert_fusion = (bf16[1024,1024]{1,0:T(8,128)(2,1)S(1)}, bf16[1024,1024]{1,0:T(8,128)(2,1)S(1)}) fusion(), kind=kLoop, calls=%fused_computation.14 | loop fusion | flops 26214400 | bytes 4194304 | tf_op jit(solution)/shard_map/convert.1
  19.0 0.4 pad_maximum_fusion
  19.4 0.3 slice_negate_fusion
  19.7 4.9 %convolution_convert_fusion = bf16[2048,1024]{1,0:T(8,128)(2,1)S(1)} fusion(bf16[1024,2048]{1,0:T(8,128)(2,1)S(1)} %pad_maximum_fusion, bf16[1,1024,1024]{2,1,0:T(8,128)(2,1)S(1)} %copy-done), kind=kOutput, calls=%fused_computation.20 | convolution fusion | flops 4297064448 | bytes 10485760 | tf_op jit(solution)/shard_map/dot_general | solution.py:143
  24.6 0.4 maximum_bitcast_fusion
  25.0 10.4 %fusion.12 = bf16[128,8,2048]{2,1,0:T(8,128)(2,1)} fusion(bf16[1024,2,1024]{0,2,1:T(8,128)(2,1)S(1)} %bitcast.36, bf16[1,1024,2048]{2,1,0:T(8,128)(2,1)S(1)} %maximum_bitcast_fusion, bf16[1,1024,2048]{2,1,0:T(8,128)(2,1)S(1)} %bitcast.30), kind=kOutput, calls=%fused_computation.21 | convolution fusion | flops 8596226048 | bytes 16777216 | tf_op jit(solution)/shard_map/ypk,pyj->kj/dot_general | solution.py:155
  35.4 11.9 %all-to-all-start = ((bf16[128,8,2048]{2,1,0:T(8,128)(2,1)}), bf16[128,8,2048]{2,1,0:T(8,128)(2,1)}, u32[]{:S(2)}, u32[]{:S(2)}) async-start(bf16[128,8,2048]{2,1,0:T(8,128)(2,1)} %fusion.12), calls=%async_computation | async-start | bytes 8388608 | tf_op jit(solution)/shard_map/all_to_all | solution.py:157
  47.3 1.8 %collective-permute-start = (f32[2,256]{1,0:T(2,128)S(1)}, f32[2,256]{1,0:T(2,128)S(1)}, u32[]{:S(2)}, u32[]{:S(2)}) collective-permute-start(f32[2,256]{1,0:T(2,128)S(1)} %copy-done.2), channel_id=1, source_target_pairs={{0,1},{1,2},{2,3},{3,0},{4,5},{5,6},{6,7},{7,4},{8,9},{9,10},{10,1... | collective-permute-start | bytes 6152 | tf_op jit(solution)/shard_map/ppermute | solution.py:181
  49.2 0.7 collective-permute-start.1
  50.2 0.4 collective-permute-done
  50.6 21.0 %collective-permute-done.1 = f32[2,256]{1,0:T(2,128)S(1)} collective-permute-done((f32[2,256]{1,0:T(2,128)S(1)}, f32[2,256]{1,0:T(2,128)S(1)}, u32[]{:S(2)}, u32[]{:S(2)}) %collective-permute-start.1) | collective-permute-done | bytes 2080 | tf_op jit(solution)/shard_map/ppermute | solution.py:181
  71.7 0.8 multiply_reduce_fusion
  72.4 27.3 %all-to-all-done.x_ref = bf16[128,8,2048]{2,1,0:T(8,128)(2,1)} async-done(((bf16[128,8,2048]{2,1,0:T(8,128)(2,1)}), bf16[128,8,2048]{2,1,0:T(8,128)(2,1)}, u32[]{:S(2)}, u32[]{:S(2)}) %all-to-all-start) | async-done | bytes 4194336 | tf_op jit(solution)/shard_map/all_to_all | solution.py:157
  99.8 14.7 %shard_map.59 = f32[16,8,1024]{2,1,0:T(8,128)} custom-call(s32[16]{0:T(128)S(1)} %copy-done.1, bf16[128,8,2048]{2,1,0:T(8,128)(2,1)} %all-to-all-done.x_ref), custom_call_target="tpu_custom_call" | custom-call | tf_op jit(solution)/shard_map/pallas_call | solution.py:63
  114.5 1.1 reduce_sum.36
  115.7 0.2 convolution_bitcast_fusion
  116.0 0.7 copy.34
  116.8 5.8 %all-to-all-start.1 = ((f32[128,2,17]{2,1,0:T(2,128)}), f32[128,2,17]{2,1,0:T(2,128)S(1)}, u32[]{:S(2)}, u32[]{:S(2)}) async-start(f32[128,2,17]{2,1,0:T(2,128)} %copy.34), calls=%async_computation.1 | async-start | bytes 262144 | tf_op jit(solution)/shard_map/all_to_all | solution.py:173
  122.6 10.2 %all-to-all-done.1 = f32[128,2,17]{2,1,0:T(2,128)S(1)} async-done(((f32[128,2,17]{2,1,0:T(2,128)}), f32[128,2,17]{2,1,0:T(2,128)S(1)}, u32[]{:S(2)}, u32[]{:S(2)}) %all-to-all-start.1) | async-done | bytes 17440 | tf_op jit(solution)/shard_map/all_to_all | solution.py:173
  133.2 0.7 broadcast_in_dim.20.tgt_ref
  133.8 0.7 broadcast_in_dim.38.step_ref
  134.5 34.8 %shard_map.60 = f32[2,8,1024]{2,1,0:T(8,128)} custom-call(f32[2,16,1024]{2,1,0:T(8,128)} %get-tuple-element.5.k_ref, f32[2,16,128]{2,1,0:T(8,128)} %broadcast_in_dim.20.tgt_ref, f32[2,8,128]{2,1,0:T(8,128)} %broadcast_in_dim.38.step_ref), custom_call_target="tpu_custom_call" | custom-call | tf_op jit(solution)/shard_map/pallas_call | solution.py:132
  169.3 0.8 slice.27
  170.1 0.6 slice.28
  (25 shorter events, 0.8 us)
Async XLA Ops:
  0.6 19.1 %copy-start = (bf16[1,1024,1024]{2,1,0:T(8,128)(2,1)S(1)}, bf16[1,1024,1024]{2,1,0:T(8,128)(2,1)}, u32[]{:S(2)}) copy-start(bf16[1,1024,1024]{2,1,0:T(8,128)(2,1)} %param.4) | copy-start | bytes 6291460
  35.4 12.0 %copy-start.2 = (f32[2,256]{1,0:T(2,128)S(1)}, f32[2,256]{1,0:T(2,128)}, u32[]{:S(2)}) copy-start(f32[2,256]{1,0:T(2,128)} %param.7) | copy-start | bytes 6148
  35.4 14.5 %copy-start.3 = (s32[8,1]{0,1:T(1,128)S(1)}, s32[8,1]{0,1:T(1,128)}, u32[]{:S(2)}) copy-start(s32[8,1]{0,1:T(1,128)} %param.6) | copy-start | bytes 100
  35.4 14.8 %copy-start.1 = (s32[16]{0:T(128)S(1)}, s32[16]{0:T(128)}, u32[]{:S(2)}) copy-start(s32[16]{0:T(128)} %lags_ref.1) | copy-start | bytes 196
  35.4 64.4 %all-to-all-start = ((bf16[128,8,2048]{2,1,0:T(8,128)(2,1)}), bf16[128,8,2048]{2,1,0:T(8,128)(2,1)}, u32[]{:S(2)}, u32[]{:S(2)}) async-start(bf16[128,8,2048]{2,1,0:T(8,128)(2,1)} %fusion.12), calls=%async_computation | async-start | bytes 8388608 | tf_op jit(solution)/shard_map/all_to_all | solution.py:157
  47.3 3.3 %collective-permute-start = (f32[2,256]{1,0:T(2,128)S(1)}, f32[2,256]{1,0:T(2,128)S(1)}, u32[]{:S(2)}, u32[]{:S(2)}) collective-permute-start(f32[2,256]{1,0:T(2,128)S(1)} %copy-done.2), channel_id=1, source_target_pairs={{0,1},{1,2},{2,3},{3,0},{4,5},{5,6},{6,7},{7,4},{8,9},{9,10},{10,1... | collective-permute-start | bytes 6152 | tf_op jit(solution)/shard_map/ppermute | solution.py:181
  49.2 22.5 %collective-permute-start.1 = (f32[2,256]{1,0:T(2,128)S(1)}, f32[2,256]{1,0:T(2,128)S(1)}, u32[]{:S(2)}, u32[]{:S(2)}) collective-permute-start(f32[2,256]{1,0:T(2,128)S(1)} %copy-done.2), channel_id=1, source_target_pairs={{0,2},{1,3},{2,0},{3,1},{4,6},{5,7},{6,4},{7,5},{8,10},{9,11},{10,... | collective-permute-start | bytes 6152 | tf_op jit(solution)/shard_map/ppermute | solution.py:181
  49.9 21.8 %collective-permute-start.2 = (f32[2,256]{1,0:T(2,128)S(1)}, f32[2,256]{1,0:T(2,128)S(1)}, u32[]{:S(2)}, u32[]{:S(2)}) collective-permute-start(f32[2,256]{1,0:T(2,128)S(1)} %copy-done.2), channel_id=1, source_target_pairs={{0,3},{1,0},{2,1},{3,2},{4,7},{5,4},{6,5},{7,6},{8,11},{9,8},{10,9... | collective-permute-start | bytes 6152 | tf_op jit(solution)/shard_map/ppermute | solution.py:181
  116.8 16.0 %all-to-all-start.1 = ((f32[128,2,17]{2,1,0:T(2,128)}), f32[128,2,17]{2,1,0:T(2,128)S(1)}, u32[]{:S(2)}, u32[]{:S(2)}) async-start(f32[128,2,17]{2,1,0:T(2,128)} %copy.34), calls=%async_computation.1 | async-start | bytes 262144 | tf_op jit(solution)/shard_map/all_to_all | solution.py:173

commit v10 on v7

--- a/solution.py
+++ b/solution.py
@@ -91,7 +91,7 @@
         gradient = jnp.sum(panel * residual, axis=1, keepdims=True)
         return jnp.maximum(w - step * gradient, 0.0)
 
-    w_ref[...] = lax.fori_loop(0, ITERS, body, jnp.zeros(step.shape, jnp.float32), unroll=4)
+    w_ref[...] = lax.fori_loop(0, ITERS, body, jnp.zeros(step.shape, jnp.float32), unroll=16)
 
 
 def fit_bands(kernel, target, step_size):
@@ -128,17 +128,15 @@
     structure = jnp.concatenate(pieces_out, axis=2)
 
     bands_dev = decay_rates.shape[0]
-    bands_total = bands_dev * lax.axis_size("tm")
+    groups = lax.axis_size("tm")
+    dest_band = (jnp.arange(devices, dtype=jnp.int32) // (devices // groups))[:, None] * bands_dev + jnp.arange(
+        bands_dev, dtype=jnp.int32
+    )[None, :]
+    dest_hot = (band_index[:, 0][None, None, :] == dest_band[:, :, None]).astype(jnp.float32)
+    dest_counts = jnp.sum(dest_hot, axis=2, keepdims=True)
     row_sums = jnp.sum(structure, axis=2)
-    band_ids = jnp.arange(bands_total, dtype=jnp.int32)
-    one_hot = (band_index[:, 0][None, :] == band_ids[:, None]).astype(jnp.float32)
-    partial_totals = jnp.dot(one_hot, row_sums.T, precision=lax.Precision.HIGHEST)
-    partial_counts = jnp.sum(one_hot, axis=1, keepdims=True)
-    partial = jnp.concatenate([partial_totals, partial_counts], axis=1)
-    per_dest = jnp.broadcast_to(
-        partial.reshape(bands_total // bands_dev, 1, bands_dev, -1),
-        (bands_total // bands_dev, devices // (bands_total // bands_dev), bands_dev, partial.shape[1]),
-    ).reshape(devices, bands_dev, partial.shape[1])
+    dest_totals = jnp.einsum("dbr,lr->dbl", dest_hot, row_sums, precision=lax.Precision.HIGHEST)
+    per_dest = jnp.concatenate([dest_totals, dest_counts], axis=2)
     received = lax.all_to_all(per_dest, ("tm", "qband"), 0, 0, tiled=True)
     own = jnp.sum(received, axis=0)
     nlag = lag_list.shape[0]

time: 150 us -> 150 us (level)
  no operation moved by 1% of the time
where the time goes in v10:
time: 150 us; the launch traced here: 149 us
  waiting for transfers between devices  59.2 us (39%)
  Pallas kernels  28.6 us (19%)
  other arithmetic  21.9 us (15%)
  starting transfers between devices  20.3 us (14%)
  matrix products  15.4 us (10%)
  local copies, waits for them, and re-layouts  3.39 us (2%)
    all_to_all x1, waiting for transfers between devices, on_device(): gathered = lax.all_to_all(spectrum, ('tm', 'qband'), 0, 0, tiled=True)  27.4 us
    ppermute x3, waiting for transfers between devices, on_device(): lax.ppermute(decay_rates, 'qband', [(j, (j + s) % ring) for j in range(ri...  21.7 us
    another operation x1, other arithmetic  18.3 us
    pallas_call x1, Pallas kernels, structure_block(): pl.pallas_call(structure_kernel, out_shape=jax.ShapeDtypeStruct((nlag, ro...  15.7 us
    pallas_call x1, Pallas kernels, fit_bands(): pl.pallas_call(fit_kernel, out_shape=jax.ShapeDtypeStruct((bands, 1, bins...  12.9 us
    all_to_all x1, starting transfers between devices, on_device(): gathered = lax.all_to_all(spectrum, ('tm', 'qband'), 0, 0, tiled=True)  11.9 us
    dot_general x1, matrix products, on_device(): jnp.einsum('ypk,pyj->kj', row_transform, mixing, preferred_element_type=j...  10.4 us
    all_to_all x1, waiting for transfers between devices, on_device(): received = lax.all_to_all(per_dest, ('tm', 'qband'), 0, 0, tiled=True)  10.2 us
  transfers between devices with their start and end apart: 5, of which 4 were waited for; matrix products, arithmetic and copies ran while one was open for 1% of the time, Pallas kernels for 0%

profile of v10, /device:TPU:1, one launch (start us, length us, event | category | flops | bytes accessed | tf_op | source)
XLA Modules:
  0.0 149.5 jit_solution(9982789595769667012)
XLA Ops:
  0.6 18.3 %multiply_convert_fusion = (bf16[1024,1024]{1,0:T(8,128)(2,1)S(1)}, bf16[1024,1024]{1,0:T(8,128)(2,1)S(1)}) fusion(), kind=kLoop, calls=%fused_computation.14 | loop fusion | flops 26214400 | bytes 4194304 | tf_op jit(solution)/shard_map/convert.1
  19.0 0.4 pad_maximum_fusion
  19.4 0.3 slice_negate_fusion
  19.7 4.9 %convolution_convert_fusion = bf16[2048,1024]{1,0:T(8,128)(2,1)S(1)} fusion(bf16[1024,2048]{1,0:T(8,128)(2,1)S(1)} %pad_maximum_fusion, bf16[1,1024,1024]{2,1,0:T(8,128)(2,1)S(1)} %copy-done), kind=kOutput, calls=%fused_computation.20 | convolution fusion | flops 4297064448 | bytes 10485760 | tf_op jit(solution)/shard_map/dot_general | solution.py:112
  24.6 0.4 maximum_bitcast_fusion
  25.0 10.4 %fusion.12 = bf16[128,8,2048]{2,1,0:T(8,128)(2,1)} fusion(bf16[1024,2,1024]{0,2,1:T(8,128)(2,1)S(1)} %bitcast.30, bf16[1,1024,2048]{2,1,0:T(8,128)(2,1)S(1)} %maximum_bitcast_fusion, bf16[1,1024,2048]{2,1,0:T(8,128)(2,1)S(1)} %bitcast.25), kind=kOutput, calls=%fused_computation.21 | convolution fusion | flops 8596226048 | bytes 16777216 | tf_op jit(solution)/shard_map/ypk,pyj->kj/dot_general | solution.py:124
  35.4 11.9 %all-to-all-start = ((bf16[128,8,2048]{2,1,0:T(8,128)(2,1)}), bf16[128,8,2048]{2,1,0:T(8,128)(2,1)}, u32[]{:S(2)}, u32[]{:S(2)}) async-start(bf16[128,8,2048]{2,1,0:T(8,128)(2,1)} %fusion.12), calls=%async_computation | async-start | bytes 8388608 | tf_op jit(solution)/shard_map/all_to_all | solution.py:126
  47.3 1.8 %collective-permute-start = (f32[2,256]{1,0:T(2,128)S(1)}, f32[2,256]{1,0:T(2,128)S(1)}, u32[]{:S(2)}, u32[]{:S(2)}) collective-permute-start(f32[2,256]{1,0:T(2,128)S(1)} %copy-done.2), channel_id=1, source_target_pairs={{0,1},{1,2},{2,3},{3,0},{4,5},{5,6},{6,7},{7,4},{8,9},{9,10},{10,1... | collective-permute-start | bytes 6152 | tf_op jit(solution)/shard_map/ppermute | solution.py:148
  49.2 0.7 collective-permute-start.1
  50.0 0.6 collective-permute-done
  50.6 21.0 %collective-permute-done.1 = f32[2,256]{1,0:T(2,128)S(1)} collective-permute-done((f32[2,256]{1,0:T(2,128)S(1)}, f32[2,256]{1,0:T(2,128)S(1)}, u32[]{:S(2)}, u32[]{:S(2)}) %collective-permute-start.1) | collective-permute-done | bytes 2080 | tf_op jit(solution)/shard_map/ppermute | solution.py:148
  71.7 0.8 multiply_reduce_fusion
  72.4 27.4 %all-to-all-done.x_ref = bf16[128,8,2048]{2,1,0:T(8,128)(2,1)} async-done(((bf16[128,8,2048]{2,1,0:T(8,128)(2,1)}), bf16[128,8,2048]{2,1,0:T(8,128)(2,1)}, u32[]{:S(2)}, u32[]{:S(2)}) %all-to-all-start) | async-done | bytes 4194336 | tf_op jit(solution)/shard_map/all_to_all | solution.py:126
  99.8 15.7 %shard_map.59 = f32[16,8,1024]{2,1,0:T(8,128)} custom-call(s32[16]{0:T(128)S(1)} %copy-done.1, bf16[128,8,2048]{2,1,0:T(8,128)(2,1)} %all-to-all-done.x_ref), custom_call_target="tpu_custom_call" | custom-call | tf_op jit(solution)/shard_map/pallas_call | solution.py:63
  115.5 1.1 reduce_sum.36
  116.6 0.2 fusion.16
  116.8 0.8 copy.11
  117.6 5.8 %all-to-all-start.1 = ((f32[128,2,17]{2,1,0:T(2,128)}), f32[128,2,17]{2,1,0:T(2,128)S(1)}, u32[]{:S(2)}, u32[]{:S(2)}) async-start(f32[128,2,17]{2,1,0:T(2,128)} %copy.11), calls=%async_computation.1 | async-start | bytes 262144 | tf_op jit(solution)/shard_map/all_to_all | solution.py:140
  123.4 10.2 %all-to-all-done.1 = f32[128,2,17]{2,1,0:T(2,128)S(1)} async-done(((f32[128,2,17]{2,1,0:T(2,128)}), f32[128,2,17]{2,1,0:T(2,128)S(1)}, u32[]{:S(2)}, u32[]{:S(2)}) %all-to-all-start.1) | async-done | bytes 17440 | tf_op jit(solution)/shard_map/all_to_all | solution.py:140
  134.0 0.7 broadcast_in_dim.17.tgt_ref
  134.7 0.7 broadcast_in_dim.18.step_ref
  135.3 12.9 %shard_map.60 = f32[2,1,1024]{2,1,0:T(1,128)} custom-call(f32[2,16,1024]{2,1,0:T(8,128)} %get-tuple-element.5.k_ref, f32[2,16,128]{2,1,0:T(8,128)} %broadcast_in_dim.17.tgt_ref, f32[2,1,1024]{2,1,0:T(1,128)} %broadcast_in_dim.18.step_ref), custom_call_target="tpu_custom_call" | custom-call | tf_op jit(solution)/shard_map/pallas_call | solution.py:101
  148.2 0.7 copy.20
  148.9 0.6 slice.23
  (20 shorter events, 0.6 us)
Async XLA Ops:
  0.6 19.1 %copy-start = (bf16[1,1024,1024]{2,1,0:T(8,128)(2,1)S(1)}, bf16[1,1024,1024]{2,1,0:T(8,128)(2,1)}, u32[]{:S(2)}) copy-start(bf16[1,1024,1024]{2,1,0:T(8,128)(2,1)} %param.4) | copy-start | bytes 6291460
  35.4 12.0 %copy-start.2 = (f32[2,256]{1,0:T(2,128)S(1)}, f32[2,256]{1,0:T(2,128)}, u32[]{:S(2)}) copy-start(f32[2,256]{1,0:T(2,128)} %param.7) | copy-start | bytes 6148
  35.4 14.5 %copy-start.3 = (s32[8,1]{0,1:T(1,128)S(1)}, s32[8,1]{0,1:T(1,128)}, u32[]{:S(2)}) copy-start(s32[8,1]{0,1:T(1,128)} %param.6) | copy-start | bytes 100
  35.4 14.6 %copy-start.1 = (s32[16]{0:T(128)S(1)}, s32[16]{0:T(128)}, u32[]{:S(2)}) copy-start(s32[16]{0:T(128)} %lags_ref.1) | copy-start | bytes 196
  35.4 64.4 %all-to-all-start = ((bf16[128,8,2048]{2,1,0:T(8,128)(2,1)}), bf16[128,8,2048]{2,1,0:T(8,128)(2,1)}, u32[]{:S(2)}, u32[]{:S(2)}) async-start(bf16[128,8,2048]{2,1,0:T(8,128)(2,1)} %fusion.12), calls=%async_computation | async-start | bytes 8388608 | tf_op jit(solution)/shard_map/all_to_all | solution.py:126
  47.3 3.3 %collective-permute-start = (f32[2,256]{1,0:T(2,128)S(1)}, f32[2,256]{1,0:T(2,128)S(1)}, u32[]{:S(2)}, u32[]{:S(2)}) collective-permute-start(f32[2,256]{1,0:T(2,128)S(1)} %copy-done.2), channel_id=1, source_target_pairs={{0,1},{1,2},{2,3},{3,0},{4,5},{5,6},{6,7},{7,4},{8,9},{9,10},{10,1... | collective-permute-start | bytes 6152 | tf_op jit(solution)/shard_map/ppermute | solution.py:148
  49.2 22.5 %collective-permute-start.1 = (f32[2,256]{1,0:T(2,128)S(1)}, f32[2,256]{1,0:T(2,128)S(1)}, u32[]{:S(2)}, u32[]{:S(2)}) collective-permute-start(f32[2,256]{1,0:T(2,128)S(1)} %copy-done.2), channel_id=1, source_target_pairs={{0,2},{1,3},{2,0},{3,1},{4,6},{5,7},{6,4},{7,5},{8,10},{9,11},{10,... | collective-permute-start | bytes 6152 | tf_op jit(solution)/shard_map/ppermute | solution.py:148
  49.9 21.8 %collective-permute-start.2 = (f32[2,256]{1,0:T(2,128)S(1)}, f32[2,256]{1,0:T(2,128)S(1)}, u32[]{:S(2)}, u32[]{:S(2)}) collective-permute-start(f32[2,256]{1,0:T(2,128)S(1)} %copy-done.2), channel_id=1, source_target_pairs={{0,3},{1,0},{2,1},{3,2},{4,7},{5,4},{6,5},{7,6},{8,11},{9,8},{10,9... | collective-permute-start | bytes 6152 | tf_op jit(solution)/shard_map/ppermute | solution.py:148
  117.6 16.0 %all-to-all-start.1 = ((f32[128,2,17]{2,1,0:T(2,128)}), f32[128,2,17]{2,1,0:T(2,128)S(1)}, u32[]{:S(2)}, u32[]{:S(2)}) async-start(f32[128,2,17]{2,1,0:T(2,128)} %copy.11), calls=%async_computation.1 | async-start | bytes 262144 | tf_op jit(solution)/shard_map/all_to_all | solution.py:140

commit v11 on v10

--- a/solution.py
+++ b/solution.py
@@ -80,10 +80,11 @@
     return (1.0 - jnp.exp(-decay_rates[:, None, :] * lag_values[None, :, None])) / BINS
 
 
-def fit_kernel(k_ref, tgt_ref, step_ref, w_ref):
+def fit_kernel(k_ref, tgt_ref, w_ref):
     panel = k_ref[...]
     tgt = tgt_ref[...][:, :, 0:1]
-    step = step_ref[...]
+    norm = jnp.sum(jnp.sum(panel * panel, axis=2, keepdims=True), axis=1, keepdims=True)
+    step = 1.0 / norm
 
     def body(i, w):
         predicted = jnp.sum(panel * w, axis=2, keepdims=True)
@@ -91,18 +92,20 @@
         gradient = jnp.sum(panel * residual, axis=1, keepdims=True)
         return jnp.maximum(w - step * gradient, 0.0)
 
-    w_ref[...] = lax.fori_loop(0, ITERS, body, jnp.zeros(step.shape, jnp.float32), unroll=16)
+    shape = (panel.shape[0], 1, panel.shape[2])
+    w = lax.fori_loop(0, ITERS, body, jnp.zeros(shape, jnp.float32), unroll=16)
+    columns = w_ref.shape[1]
+    for b in range(panel.shape[0]):
+        w_ref[b:b + 1, :] = w[b, :, 0:columns]
 
 
-def fit_bands(kernel, target, step_size):
+def fit_bands(kernel, target, columns):
     bands, lags, bins = kernel.shape
     tgt = jnp.broadcast_to(target[:, :, None], (bands, lags, 128))
-    step = jnp.broadcast_to(step_size[:, None, None], (bands, 1, bins))
-    out = pl.pallas_call(
+    return pl.pallas_call(
         fit_kernel,
-        out_shape=jax.ShapeDtypeStruct((bands, 1, bins), jnp.float32),
-    )(kernel, tgt, step)
-    return out[:, 0, :]
+        out_shape=jax.ShapeDtypeStruct((bands, columns), jnp.float32),
+    )(kernel, tgt)
 
 
 def on_device(frames, lag_list, band_index, decay_rates):
@@ -149,8 +152,7 @@
     ]
     all_rates = jnp.concatenate(pieces, axis=1)
     kernel = kernel_panel(all_rates, lag_list)
-    step_size = 1.0 / jnp.sum(kernel * kernel, axis=(1, 2))
-    weights = fit_bands(kernel, target, step_size)[:, :columns]
+    weights = fit_bands(kernel, target, columns)
     return (structure, weights)
 
 

time: 150 us -> 147 us (0.980)
  local copies, waits for them, and re-layouts: 3.39 us -> 1.46 us
where the time goes in v11:
time: 147 us
  waiting for transfers between devices  59.2 us (40%)
  Pallas kernels  27.6 us (19%)
  other arithmetic  21.9 us (15%)
  starting transfers between devices  20.3 us (14%)
  matrix products  15.6 us (11%)
    all_to_all x1, waiting for transfers between devices, on_device(): gathered = lax.all_to_all(spectrum, ('tm', 'qband'), 0, 0, tiled=True)  28.1 us
    ppermute x3, waiting for transfers between devices, on_device(): lax.ppermute(decay_rates, 'qband', [(j, (j + s) % ring) for j in range(ri...  21.7 us
    another operation x1, other arithmetic  18.3 us
    pallas_call x1, Pallas kernels, structure_block(): pl.pallas_call(structure_kernel, out_shape=jax.ShapeDtypeStruct((nlag, ro...  15.2 us
    pallas_call x1, Pallas kernels, fit_bands(): pl.pallas_call(fit_kernel, out_shape=jax.ShapeDtypeStruct((bands, columns...  12.5 us
    all_to_all x1, starting transfers between devices, on_device(): gathered = lax.all_to_all(spectrum, ('tm', 'qband'), 0, 0, tiled=True)  12 us
    dot_general x1, matrix products, on_device(): jnp.einsum('ypk,pyj->kj', row_transform, mixing, preferred_element_type=j...  10.4 us
    all_to_all x1, waiting for transfers between devices, on_device(): received = lax.all_to_all(per_dest, ('tm', 'qband'), 0, 0, tiled=True)  9.46 us
  transfers between devices with their start and end apart: 5, of which 4 were waited for; matrix products, arithmetic and copies ran while one was open for 1% of the time, Pallas kernels for 0%

profile of v11, /device:TPU:1, one launch (start us, length us, event | category | flops | bytes accessed | tf_op | source)
XLA Modules:
  0.0 146.8 jit_solution(8951513721171290259)
XLA Ops:
  0.6 18.3 %multiply_convert_fusion = (bf16[1024,1024]{1,0:T(8,128)(2,1)S(1)}, bf16[1024,1024]{1,0:T(8,128)(2,1)S(1)}) fusion(), kind=kLoop, calls=%fused_computation.14 | loop fusion | flops 26214400 | bytes 4194304 | tf_op jit(solution)/shard_map/convert.1
  19.0 0.4 pad_maximum_fusion
  19.4 0.3 slice_negate_fusion
  19.7 5.0 %convolution_convert_fusion = bf16[2048,1024]{1,0:T(8,128)(2,1)S(1)} fusion(bf16[1024,2048]{1,0:T(8,128)(2,1)S(1)} %pad_maximum_fusion, bf16[1,1024,1024]{2,1,0:T(8,128)(2,1)S(1)} %copy-done), kind=kOutput, calls=%fused_computation.20 | convolution fusion | flops 4297064448 | bytes 10485760 | tf_op jit(solution)/shard_map/dot_general | solution.py:115
  24.7 0.4 maximum_bitcast_fusion
  25.2 10.4 %fusion.12 = bf16[128,8,2048]{2,1,0:T(8,128)(2,1)} fusion(bf16[1024,2,1024]{0,2,1:T(8,128)(2,1)S(1)} %bitcast.26, bf16[1,1024,2048]{2,1,0:T(8,128)(2,1)S(1)} %maximum_bitcast_fusion, bf16[1,1024,2048]{2,1,0:T(8,128)(2,1)S(1)} %bitcast.22), kind=kOutput, calls=%fused_computation.21 | convolution fusion | flops 8596226048 | bytes 16777216 | tf_op jit(solution)/shard_map/ypk,pyj->kj/dot_general | solution.py:127
  35.6 12.0 %all-to-all-start = ((bf16[128,8,2048]{2,1,0:T(8,128)(2,1)}), bf16[128,8,2048]{2,1,0:T(8,128)(2,1)}, u32[]{:S(2)}, u32[]{:S(2)}) async-start(bf16[128,8,2048]{2,1,0:T(8,128)(2,1)} %fusion.12), calls=%async_computation | async-start | bytes 8388608 | tf_op jit(solution)/shard_map/all_to_all | solution.py:129
  47.6 1.8 %collective-permute-start = (f32[2,256]{1,0:T(2,128)S(1)}, f32[2,256]{1,0:T(2,128)S(1)}, u32[]{:S(2)}, u32[]{:S(2)}) collective-permute-start(f32[2,256]{1,0:T(2,128)S(1)} %copy-done.2), channel_id=1, source_target_pairs={{0,1},{1,2},{2,3},{3,0},{4,5},{5,6},{6,7},{7,4},{8,9},{9,10},{10,1... | collective-permute-start | bytes 6152 | tf_op jit(solution)/shard_map/ppermute | solution.py:151
  49.4 0.7 collective-permute-start.1
  50.1 0.1 fusion.18
  50.2 0.6 collective-permute-done
  50.8 21.0 %collective-permute-done.1 = f32[2,256]{1,0:T(2,128)S(1)} collective-permute-done((f32[2,256]{1,0:T(2,128)S(1)}, f32[2,256]{1,0:T(2,128)S(1)}, u32[]{:S(2)}, u32[]{:S(2)}) %collective-permute-start.1) | collective-permute-done | bytes 2080 | tf_op jit(solution)/shard_map/ppermute | solution.py:151
  71.9 28.1 %all-to-all-done.x_ref = bf16[128,8,2048]{2,1,0:T(8,128)(2,1)} async-done(((bf16[128,8,2048]{2,1,0:T(8,128)(2,1)}), bf16[128,8,2048]{2,1,0:T(8,128)(2,1)}, u32[]{:S(2)}, u32[]{:S(2)}) %all-to-all-start) | async-done | bytes 4194336 | tf_op jit(solution)/shard_map/all_to_all | solution.py:129
  100.0 15.2 %shard_map.59 = f32[16,8,1024]{2,1,0:T(8,128)} custom-call(s32[16]{0:T(128)S(1)} %copy-done.1, bf16[128,8,2048]{2,1,0:T(8,128)(2,1)} %all-to-all-done.x_ref), custom_call_target="tpu_custom_call" | custom-call | tf_op jit(solution)/shard_map/pallas_call | solution.py:63
  115.2 1.1 reduce_sum.27
  116.3 0.2 fusion.16
  116.5 0.8 copy.11
  117.3 5.8 %all-to-all-start.1 = ((f32[128,2,17]{2,1,0:T(2,128)}), f32[128,2,17]{2,1,0:T(2,128)S(1)}, u32[]{:S(2)}, u32[]{:S(2)}) async-start(f32[128,2,17]{2,1,0:T(2,128)} %copy.11), calls=%async_computation.1 | async-start | bytes 262144 | tf_op jit(solution)/shard_map/all_to_all | solution.py:143
  123.1 0.7 subtract_multiply_fusion.k_ref
  123.8 9.5 %all-to-all-done.1 = f32[128,2,17]{2,1,0:T(2,128)S(1)} async-done(((f32[128,2,17]{2,1,0:T(2,128)}), f32[128,2,17]{2,1,0:T(2,128)S(1)}, u32[]{:S(2)}, u32[]{:S(2)}) %all-to-all-start.1) | async-done | bytes 17440 | tf_op jit(solution)/shard_map/all_to_all | solution.py:143
  133.3 0.1 reduce_sum.29
  133.4 0.2 multiply_reduce_fusion
  133.7 0.7 broadcast_in_dim.15.tgt_ref
  134.4 12.5 %shard_map.60 = f32[2,256]{1,0:T(2,128)} custom-call(f32[2,16,1024]{2,1,0:T(8,128)} %subtract_multiply_fusion.k_ref, f32[2,16,128]{2,1,0:T(8,128)} %broadcast_in_dim.15.tgt_ref), custom_call_target="tpu_custom_call" | custom-call | tf_op jit(solution)/shard_map/pallas_call | solution.py:105
  (16 shorter events, 0.1 us)
Async XLA Ops:
  0.6 19.1 %copy-start = (bf16[1,1024,1024]{2,1,0:T(8,128)(2,1)S(1)}, bf16[1,1024,1024]{2,1,0:T(8,128)(2,1)}, u32[]{:S(2)}) copy-start(bf16[1,1024,1024]{2,1,0:T(8,128)(2,1)} %param.4) | copy-start | bytes 6291460
  35.6 12.0 %copy-start.2 = (f32[2,256]{1,0:T(2,128)S(1)}, f32[2,256]{1,0:T(2,128)}, u32[]{:S(2)}) copy-start(f32[2,256]{1,0:T(2,128)} %param.7) | copy-start | bytes 6148
  35.6 14.6 %copy-start.3 = (s32[8,1]{0,1:T(1,128)S(1)}, s32[8,1]{0,1:T(1,128)}, u32[]{:S(2)}) copy-start(s32[8,1]{0,1:T(1,128)} %param.6) | copy-start | bytes 100
  35.6 14.6 %copy-start.1 = (s32[16]{0:T(128)S(1)}, s32[16]{0:T(128)}, u32[]{:S(2)}) copy-start(s32[16]{0:T(128)} %lags_ref.1) | copy-start | bytes 196
  35.6 64.4 %all-to-all-start = ((bf16[128,8,2048]{2,1,0:T(8,128)(2,1)}), bf16[128,8,2048]{2,1,0:T(8,128)(2,1)}, u32[]{:S(2)}, u32[]{:S(2)}) async-start(bf16[128,8,2048]{2,1,0:T(8,128)(2,1)} %fusion.12), calls=%async_computation | async-start | bytes 8388608 | tf_op jit(solution)/shard_map/all_to_all | solution.py:129
  47.6 3.3 %collective-permute-start = (f32[2,256]{1,0:T(2,128)S(1)}, f32[2,256]{1,0:T(2,128)S(1)}, u32[]{:S(2)}, u32[]{:S(2)}) collective-permute-start(f32[2,256]{1,0:T(2,128)S(1)} %copy-done.2), channel_id=1, source_target_pairs={{0,1},{1,2},{2,3},{3,0},{4,5},{5,6},{6,7},{7,4},{8,9},{9,10},{10,1... | collective-permute-start | bytes 6152 | tf_op jit(solution)/shard_map/ppermute | solution.py:151
  49.4 22.5 %collective-permute-start.1 = (f32[2,256]{1,0:T(2,128)S(1)}, f32[2,256]{1,0:T(2,128)S(1)}, u32[]{:S(2)}, u32[]{:S(2)}) collective-permute-start(f32[2,256]{1,0:T(2,128)S(1)} %copy-done.2), channel_id=1, source_target_pairs={{0,2},{1,3},{2,0},{3,1},{4,6},{5,7},{6,4},{7,5},{8,10},{9,11},{10,... | collective-permute-start | bytes 6152 | tf_op jit(solution)/shard_map/ppermute | solution.py:151
  50.1 21.8 %collective-permute-start.2 = (f32[2,256]{1,0:T(2,128)S(1)}, f32[2,256]{1,0:T(2,128)S(1)}, u32[]{:S(2)}, u32[]{:S(2)}) collective-permute-start(f32[2,256]{1,0:T(2,128)S(1)} %copy-done.2), channel_id=1, source_target_pairs={{0,3},{1,0},{2,1},{3,2},{4,7},{5,4},{6,5},{7,6},{8,11},{9,8},{10,9... | collective-permute-start | bytes 6152 | tf_op jit(solution)/shard_map/ppermute | solution.py:151
  117.3 16.0 %all-to-all-start.1 = ((f32[128,2,17]{2,1,0:T(2,128)}), f32[128,2,17]{2,1,0:T(2,128)S(1)}, u32[]{:S(2)}, u32[]{:S(2)}) async-start(f32[128,2,17]{2,1,0:T(2,128)} %copy.11), calls=%async_computation.1 | async-start | bytes 262144 | tf_op jit(solution)/shard_map/all_to_all | solution.py:143

commit v12 on v11

--- a/solution.py
+++ b/solution.py
@@ -93,7 +93,7 @@
         return jnp.maximum(w - step * gradient, 0.0)
 
     shape = (panel.shape[0], 1, panel.shape[2])
-    w = lax.fori_loop(0, ITERS, body, jnp.zeros(shape, jnp.float32), unroll=16)
+    w = lax.fori_loop(0, ITERS, body, jnp.zeros(shape, jnp.float32), unroll=64)
     columns = w_ref.shape[1]
     for b in range(panel.shape[0]):
         w_ref[b:b + 1, :] = w[b, :, 0:columns]

time: 147 us -> 147 us (level)
  no operation moved by 1% of the time
where the time goes in v12:
time: 147 us
  waiting for transfers between devices  59.2 us (40%)
  Pallas kernels  27.9 us (19%)
  other arithmetic  21.9 us (15%)
  starting transfers between devices  20.3 us (14%)
  matrix products  15.6 us (11%)
    all_to_all x1, waiting for transfers between devices, on_device(): gathered = lax.all_to_all(spectrum, ('tm', 'qband'), 0, 0, tiled=True)  28.1 us
    ppermute x3, waiting for transfers between devices, on_device(): lax.ppermute(decay_rates, 'qband', [(j, (j + s) % ring) for j in range(ri...  21.7 us
    another operation x1, other arithmetic  18.3 us
    pallas_call x1, Pallas kernels, structure_block(): pl.pallas_call(structure_kernel, out_shape=jax.ShapeDtypeStruct((nlag, ro...  15.7 us
    pallas_call x1, Pallas kernels, fit_bands(): pl.pallas_call(fit_kernel, out_shape=jax.ShapeDtypeStruct((bands, columns...  12.3 us
    all_to_all x1, starting transfers between devices, on_device(): gathered = lax.all_to_all(spectrum, ('tm', 'qband'), 0, 0, tiled=True)  11.9 us
    dot_general x1, matrix products, on_device(): jnp.einsum('ypk,pyj->kj', row_transform, mixing, preferred_element_type=j...  10.4 us
    all_to_all x1, waiting for transfers between devices, on_device(): received = lax.all_to_all(per_dest, ('tm', 'qband'), 0, 0, tiled=True)  9.45 us
  transfers between devices with their start and end apart: 5, of which 4 were waited for; matrix products, arithmetic and copies ran while one was open for 1% of the time, Pallas kernels for 0%

profile of v12, /device:TPU:1, one launch (start us, length us, event | category | flops | bytes accessed | tf_op | source)
XLA Modules:
  0.0 147.1 jit_solution(9794243376019418752)
XLA Ops:
  0.6 18.3 %multiply_convert_fusion = (bf16[1024,1024]{1,0:T(8,128)(2,1)S(1)}, bf16[1024,1024]{1,0:T(8,128)(2,1)S(1)}) fusion(), kind=kLoop, calls=%fused_computation.14 | loop fusion | flops 26214400 | bytes 4194304 | tf_op jit(solution)/shard_map/convert.1
  19.0 0.4 pad_maximum_fusion
  19.4 0.3 slice_negate_fusion
  19.7 5.0 %convolution_convert_fusion = bf16[2048,1024]{1,0:T(8,128)(2,1)S(1)} fusion(bf16[1024,2048]{1,0:T(8,128)(2,1)S(1)} %pad_maximum_fusion, bf16[1,1024,1024]{2,1,0:T(8,128)(2,1)S(1)} %copy-done), kind=kOutput, calls=%fused_computation.20 | convolution fusion | flops 4297064448 | bytes 10485760 | tf_op jit(solution)/shard_map/dot_general | solution.py:115
  24.7 0.4 maximum_bitcast_fusion
  25.2 10.4 %fusion.12 = bf16[128,8,2048]{2,1,0:T(8,128)(2,1)} fusion(bf16[1024,2,1024]{0,2,1:T(8,128)(2,1)S(1)} %bitcast.26, bf16[1,1024,2048]{2,1,0:T(8,128)(2,1)S(1)} %maximum_bitcast_fusion, bf16[1,1024,2048]{2,1,0:T(8,128)(2,1)S(1)} %bitcast.22), kind=kOutput, calls=%fused_computation.21 | convolution fusion | flops 8596226048 | bytes 16777216 | tf_op jit(solution)/shard_map/ypk,pyj->kj/dot_general | solution.py:127
  35.6 11.9 %all-to-all-start = ((bf16[128,8,2048]{2,1,0:T(8,128)(2,1)}), bf16[128,8,2048]{2,1,0:T(8,128)(2,1)}, u32[]{:S(2)}, u32[]{:S(2)}) async-start(bf16[128,8,2048]{2,1,0:T(8,128)(2,1)} %fusion.12), calls=%async_computation | async-start | bytes 8388608 | tf_op jit(solution)/shard_map/all_to_all | solution.py:129
  47.6 1.8 %collective-permute-start = (f32[2,256]{1,0:T(2,128)S(1)}, f32[2,256]{1,0:T(2,128)S(1)}, u32[]{:S(2)}, u32[]{:S(2)}) collective-permute-start(f32[2,256]{1,0:T(2,128)S(1)} %copy-done.2), channel_id=1, source_target_pairs={{0,1},{1,2},{2,3},{3,0},{4,5},{5,6},{6,7},{7,4},{8,9},{9,10},{10,1... | collective-permute-start | bytes 6152 | tf_op jit(solution)/shard_map/ppermute | solution.py:151
  49.4 0.7 collective-permute-start.1
  50.1 0.1 fusion.18
  50.2 0.6 collective-permute-done
  50.8 21.0 %collective-permute-done.1 = f32[2,256]{1,0:T(2,128)S(1)} collective-permute-done((f32[2,256]{1,0:T(2,128)S(1)}, f32[2,256]{1,0:T(2,128)S(1)}, u32[]{:S(2)}, u32[]{:S(2)}) %collective-permute-start.1) | collective-permute-done | bytes 2080 | tf_op jit(solution)/shard_map/ppermute | solution.py:151
  71.9 28.1 %all-to-all-done.x_ref = bf16[128,8,2048]{2,1,0:T(8,128)(2,1)} async-done(((bf16[128,8,2048]{2,1,0:T(8,128)(2,1)}), bf16[128,8,2048]{2,1,0:T(8,128)(2,1)}, u32[]{:S(2)}, u32[]{:S(2)}) %all-to-all-start) | async-done | bytes 4194336 | tf_op jit(solution)/shard_map/all_to_all | solution.py:129
  100.0 15.7 %shard_map.59 = f32[16,8,1024]{2,1,0:T(8,128)} custom-call(s32[16]{0:T(128)S(1)} %copy-done.1, bf16[128,8,2048]{2,1,0:T(8,128)(2,1)} %all-to-all-done.x_ref), custom_call_target="tpu_custom_call" | custom-call | tf_op jit(solution)/shard_map/pallas_call | solution.py:63
  115.7 1.1 reduce_sum.27
  116.8 0.2 fusion.16
  117.0 0.8 copy.11
  117.8 5.8 %all-to-all-start.1 = ((f32[128,2,17]{2,1,0:T(2,128)}), f32[128,2,17]{2,1,0:T(2,128)S(1)}, u32[]{:S(2)}, u32[]{:S(2)}) async-start(f32[128,2,17]{2,1,0:T(2,128)} %copy.11), calls=%async_computation.1 | async-start | bytes 262144 | tf_op jit(solution)/shard_map/all_to_all | solution.py:143
  123.6 0.7 subtract_multiply_fusion.k_ref
  124.3 9.5 %all-to-all-done.1 = f32[128,2,17]{2,1,0:T(2,128)S(1)} async-done(((f32[128,2,17]{2,1,0:T(2,128)}), f32[128,2,17]{2,1,0:T(2,128)S(1)}, u32[]{:S(2)}, u32[]{:S(2)}) %all-to-all-start.1) | async-done | bytes 17440 | tf_op jit(solution)/shard_map/all_to_all | solution.py:143
  133.8 0.1 reduce_sum.29
  133.9 0.2 multiply_reduce_fusion
  134.2 0.7 broadcast_in_dim.15.tgt_ref
  134.9 12.3 %shard_map.60 = f32[2,256]{1,0:T(2,128)} custom-call(f32[2,16,1024]{2,1,0:T(8,128)} %subtract_multiply_fusion.k_ref, f32[2,16,128]{2,1,0:T(8,128)} %broadcast_in_dim.15.tgt_ref), custom_call_target="tpu_custom_call" | custom-call | tf_op jit(solution)/shard_map/pallas_call | solution.py:105
  (16 shorter events, 0.1 us)
Async XLA Ops:
  0.6 19.1 %copy-start = (bf16[1,1024,1024]{2,1,0:T(8,128)(2,1)S(1)}, bf16[1,1024,1024]{2,1,0:T(8,128)(2,1)}, u32[]{:S(2)}) copy-start(bf16[1,1024,1024]{2,1,0:T(8,128)(2,1)} %param.4) | copy-start | bytes 6291460
  35.6 11.9 %copy-start.2 = (f32[2,256]{1,0:T(2,128)S(1)}, f32[2,256]{1,0:T(2,128)}, u32[]{:S(2)}) copy-start(f32[2,256]{1,0:T(2,128)} %param.7) | copy-start | bytes 6148
  35.6 14.5 %copy-start.3 = (s32[8,1]{0,1:T(1,128)S(1)}, s32[8,1]{0,1:T(1,128)}, u32[]{:S(2)}) copy-start(s32[8,1]{0,1:T(1,128)} %param.6) | copy-start | bytes 100
  35.6 14.6 %copy-start.1 = (s32[16]{0:T(128)S(1)}, s32[16]{0:T(128)}, u32[]{:S(2)}) copy-start(s32[16]{0:T(128)} %lags_ref.1) | copy-start | bytes 196
  35.6 64.4 %all-to-all-start = ((bf16[128,8,2048]{2,1,0:T(8,128)(2,1)}), bf16[128,8,2048]{2,1,0:T(8,128)(2,1)}, u32[]{:S(2)}, u32[]{:S(2)}) async-start(bf16[128,8,2048]{2,1,0:T(8,128)(2,1)} %fusion.12), calls=%async_computation | async-start | bytes 8388608 | tf_op jit(solution)/shard_map/all_to_all | solution.py:129
  47.6 3.3 %collective-permute-start = (f32[2,256]{1,0:T(2,128)S(1)}, f32[2,256]{1,0:T(2,128)S(1)}, u32[]{:S(2)}, u32[]{:S(2)}) collective-permute-start(f32[2,256]{1,0:T(2,128)S(1)} %copy-done.2), channel_id=1, source_target_pairs={{0,1},{1,2},{2,3},{3,0},{4,5},{5,6},{6,7},{7,4},{8,9},{9,10},{10,1... | collective-permute-start | bytes 6152 | tf_op jit(solution)/shard_map/ppermute | solution.py:151
  49.4 22.5 %collective-permute-start.1 = (f32[2,256]{1,0:T(2,128)S(1)}, f32[2,256]{1,0:T(2,128)S(1)}, u32[]{:S(2)}, u32[]{:S(2)}) collective-permute-start(f32[2,256]{1,0:T(2,128)S(1)} %copy-done.2), channel_id=1, source_target_pairs={{0,2},{1,3},{2,0},{3,1},{4,6},{5,7},{6,4},{7,5},{8,10},{9,11},{10,... | collective-permute-start | bytes 6152 | tf_op jit(solution)/shard_map/ppermute | solution.py:151
  50.1 21.8 %collective-permute-start.2 = (f32[2,256]{1,0:T(2,128)S(1)}, f32[2,256]{1,0:T(2,128)S(1)}, u32[]{:S(2)}, u32[]{:S(2)}) collective-permute-start(f32[2,256]{1,0:T(2,128)S(1)} %copy-done.2), channel_id=1, source_target_pairs={{0,3},{1,0},{2,1},{3,2},{4,7},{5,4},{6,5},{7,6},{8,11},{9,8},{10,9... | collective-permute-start | bytes 6152 | tf_op jit(solution)/shard_map/ppermute | solution.py:151
  117.8 16.0 %all-to-all-start.1 = ((f32[128,2,17]{2,1,0:T(2,128)}), f32[128,2,17]{2,1,0:T(2,128)S(1)}, u32[]{:S(2)}, u32[]{:S(2)}) async-start(f32[128,2,17]{2,1,0:T(2,128)} %copy.11), calls=%async_computation.1 | async-start | bytes 262144 | tf_op jit(solution)/shard_map/all_to_all | solution.py:143

commit v13 on v11

--- a/solution.py
+++ b/solution.py
@@ -35,26 +35,42 @@
 
     lax.fori_loop(0, frames_all, convert, 0)
 
-    def one_lag(l, carry):
-        lag = lags_ref[l]
-        count = frames_all - lag
+    def one_pair(p, carry):
+        lag_a = lags_ref[2 * p]
+        lag_b = lags_ref[2 * p + 1]
+        count_a = frames_all - lag_a
+        count_b = frames_all - lag_b
+        common = jnp.minimum(count_a, count_b)
 
-        def step(t, acc):
-            d = x32_ref[t + lag] - x32_ref[t]
-            return acc + d * d
+        def step_pair(t, accs):
+            acc_a, acc_b = accs
+            base = x32_ref[t]
+            d_a = x32_ref[t + lag_a] - base
+            d_b = x32_ref[t + lag_b] - base
+            return acc_a + d_a * d_a, acc_b + d_b * d_b
 
-        def step_block(i, acc):
+        def block_pair(i, accs):
             for u in range(UNROLL):
-                acc = step(i * UNROLL + u, acc)
-            return acc
+                accs = step_pair(i * UNROLL + u, accs)
+            return accs
 
-        blocks = count // UNROLL
-        acc = lax.fori_loop(0, blocks, step_block, jnp.zeros(x32_ref.shape[1:], jnp.float32))
-        acc = lax.fori_loop(blocks * UNROLL, count, step, acc)
-        out_ref[l] = (acc[:, :pixels] + acc[:, pixels:]) / count.astype(jnp.float32)
+        def step_one(lag):
+            def step(t, acc):
+                d = x32_ref[t + lag] - x32_ref[t]
+                return acc + d * d
+            return step
+
+        zeros = jnp.zeros(x32_ref.shape[1:], jnp.float32)
+        blocks = common // UNROLL
+        acc_a, acc_b = lax.fori_loop(0, blocks, block_pair, (zeros, zeros))
+        acc_a, acc_b = lax.fori_loop(blocks * UNROLL, common, step_pair, (acc_a, acc_b))
+        acc_a = lax.fori_loop(common, count_a, step_one(lag_a), acc_a)
+        acc_b = lax.fori_loop(common, count_b, step_one(lag_b), acc_b)
+        out_ref[2 * p] = (acc_a[:, :pixels] + acc_a[:, pixels:]) / count_a.astype(jnp.float32)
+        out_ref[2 * p + 1] = (acc_b[:, :pixels] + acc_b[:, pixels:]) / count_b.astype(jnp.float32)
         return carry
 
-    lax.fori_loop(0, lags_ref.shape[0], one_lag, 0)
+    lax.fori_loop(0, lags_ref.shape[0] // 2, one_pair, 0)
 
 
 def structure_block(spectrum_block, lag_list):

time: 147 us -> 153 us (1.041)
  Pallas kernels: 27.6 us -> 34 us
    pallas_call x1, Pallas kernels: 15.2 us -> 21.5 us  [structure_block(): pl.pallas_call(structure_kernel, out_shape=jax.ShapeDtypeStruct((nlag, ro...]
where the time goes in v13:
time: 153 us
  waiting for transfers between devices  59.2 us (39%)
  Pallas kernels  34 us (22%)
  other arithmetic  21.9 us (14%)
  starting transfers between devices  20.3 us (13%)
  matrix products  15.6 us (10%)
    all_to_all x1, waiting for transfers between devices, on_device(): gathered = lax.all_to_all(spectrum, ('tm', 'qband'), 0, 0, tiled=True)  28.1 us
    ppermute x3, waiting for transfers between devices, on_device(): lax.ppermute(decay_rates, 'qband', [(j, (j + s) % ring) for j in range(ri...  21.7 us
    pallas_call x1, Pallas kernels, structure_block(): pl.pallas_call(structure_kernel, out_shape=jax.ShapeDtypeStruct((nlag, ro...  21.5 us
    another operation x1, other arithmetic  18.3 us
    pallas_call x1, Pallas kernels, fit_bands(): pl.pallas_call(fit_kernel, out_shape=jax.ShapeDtypeStruct((bands, columns...  12.5 us
    all_to_all x1, starting transfers between devices, on_device(): gathered = lax.all_to_all(spectrum, ('tm', 'qband'), 0, 0, tiled=True)  12 us
    dot_general x1, matrix products, on_device(): jnp.einsum('ypk,pyj->kj', row_transform, mixing, preferred_element_type=j...  10.4 us
    all_to_all x1, waiting for transfers between devices, on_device(): received = lax.all_to_all(per_dest, ('tm', 'qband'), 0, 0, tiled=True)  9.46 us
  transfers between devices with their start and end apart: 5, of which 4 were waited for; matrix products, arithmetic and copies ran while one was open for 1% of the time, Pallas kernels for 0%

profile of v13, /device:TPU:1, one launch (start us, length us, event | category | flops | bytes accessed | tf_op | source)
XLA Modules:
  0.0 153.2 jit_solution(551795237734787295)
XLA Ops:
  0.6 18.3 %multiply_convert_fusion = (bf16[1024,1024]{1,0:T(8,128)(2,1)S(1)}, bf16[1024,1024]{1,0:T(8,128)(2,1)S(1)}) fusion(), kind=kLoop, calls=%fused_computation.14 | loop fusion | flops 26214400 | bytes 4194304 | tf_op jit(solution)/shard_map/convert.1
  19.0 0.4 pad_maximum_fusion
  19.4 0.3 slice_negate_fusion
  19.7 5.0 %convolution_convert_fusion = bf16[2048,1024]{1,0:T(8,128)(2,1)S(1)} fusion(bf16[1024,2048]{1,0:T(8,128)(2,1)S(1)} %pad_maximum_fusion, bf16[1,1024,1024]{2,1,0:T(8,128)(2,1)S(1)} %copy-done), kind=kOutput, calls=%fused_computation.20 | convolution fusion | flops 4297064448 | bytes 10485760 | tf_op jit(solution)/shard_map/dot_general | solution.py:131
  24.7 0.4 maximum_bitcast_fusion
  25.2 10.4 %fusion.12 = bf16[128,8,2048]{2,1,0:T(8,128)(2,1)} fusion(bf16[1024,2,1024]{0,2,1:T(8,128)(2,1)S(1)} %bitcast.26, bf16[1,1024,2048]{2,1,0:T(8,128)(2,1)S(1)} %maximum_bitcast_fusion, bf16[1,1024,2048]{2,1,0:T(8,128)(2,1)S(1)} %bitcast.22), kind=kOutput, calls=%fused_computation.21 | convolution fusion | flops 8596226048 | bytes 16777216 | tf_op jit(solution)/shard_map/ypk,pyj->kj/dot_general | solution.py:143
  35.6 12.0 %all-to-all-start = ((bf16[128,8,2048]{2,1,0:T(8,128)(2,1)}), bf16[128,8,2048]{2,1,0:T(8,128)(2,1)}, u32[]{:S(2)}, u32[]{:S(2)}) async-start(bf16[128,8,2048]{2,1,0:T(8,128)(2,1)} %fusion.12), calls=%async_computation | async-start | bytes 8388608 | tf_op jit(solution)/shard_map/all_to_all | solution.py:145
  47.6 1.8 %collective-permute-start = (f32[2,256]{1,0:T(2,128)S(1)}, f32[2,256]{1,0:T(2,128)S(1)}, u32[]{:S(2)}, u32[]{:S(2)}) collective-permute-start(f32[2,256]{1,0:T(2,128)S(1)} %copy-done.2), channel_id=1, source_target_pairs={{0,1},{1,2},{2,3},{3,0},{4,5},{5,6},{6,7},{7,4},{8,9},{9,10},{10,1... | collective-permute-start | bytes 6152 | tf_op jit(solution)/shard_map/ppermute | solution.py:167
  49.4 0.7 collective-permute-start.1
  50.1 0.1 fusion.18
  50.2 0.6 collective-permute-done
  50.8 21.0 %collective-permute-done.1 = f32[2,256]{1,0:T(2,128)S(1)} collective-permute-done((f32[2,256]{1,0:T(2,128)S(1)}, f32[2,256]{1,0:T(2,128)S(1)}, u32[]{:S(2)}, u32[]{:S(2)}) %collective-permute-start.1) | collective-permute-done | bytes 2080 | tf_op jit(solution)/shard_map/ppermute | solution.py:167
  71.9 28.1 %all-to-all-done.x_ref = bf16[128,8,2048]{2,1,0:T(8,128)(2,1)} async-done(((bf16[128,8,2048]{2,1,0:T(8,128)(2,1)}), bf16[128,8,2048]{2,1,0:T(8,128)(2,1)}, u32[]{:S(2)}, u32[]{:S(2)}) %all-to-all-start) | async-done | bytes 4194336 | tf_op jit(solution)/shard_map/all_to_all | solution.py:145
  100.0 21.5 %shard_map.59 = f32[16,8,1024]{2,1,0:T(8,128)} custom-call(s32[16]{0:T(128)S(1)} %copy-done.1, bf16[128,8,2048]{2,1,0:T(8,128)(2,1)} %all-to-all-done.x_ref), custom_call_target="tpu_custom_call" | custom-call | tf_op jit(solution)/shard_map/pallas_call | solution.py:79
  121.5 1.1 reduce_sum.27
  122.7 0.2 fusion.16
  122.9 0.8 copy.11
  123.6 5.8 %all-to-all-start.1 = ((f32[128,2,17]{2,1,0:T(2,128)}), f32[128,2,17]{2,1,0:T(2,128)S(1)}, u32[]{:S(2)}, u32[]{:S(2)}) async-start(f32[128,2,17]{2,1,0:T(2,128)} %copy.11), calls=%async_computation.1 | async-start | bytes 262144 | tf_op jit(solution)/shard_map/all_to_all | solution.py:159
  129.4 0.7 subtract_multiply_fusion.k_ref
  130.2 9.5 %all-to-all-done.1 = f32[128,2,17]{2,1,0:T(2,128)S(1)} async-done(((f32[128,2,17]{2,1,0:T(2,128)}), f32[128,2,17]{2,1,0:T(2,128)S(1)}, u32[]{:S(2)}, u32[]{:S(2)}) %all-to-all-start.1) | async-done | bytes 17440 | tf_op jit(solution)/shard_map/all_to_all | solution.py:159
  139.6 0.1 reduce_sum.29
  139.8 0.2 multiply_reduce_fusion
  140.0 0.7 broadcast_in_dim.15.tgt_ref
  140.7 12.5 %shard_map.60 = f32[2,256]{1,0:T(2,128)} custom-call(f32[2,16,1024]{2,1,0:T(8,128)} %subtract_multiply_fusion.k_ref, f32[2,16,128]{2,1,0:T(8,128)} %broadcast_in_dim.15.tgt_ref), custom_call_target="tpu_custom_call" | custom-call | tf_op jit(solution)/shard_map/pallas_call | solution.py:121
  (16 shorter events, 0.1 us)
Async XLA Ops:
  0.6 19.1 %copy-start = (bf16[1,1024,1024]{2,1,0:T(8,128)(2,1)S(1)}, bf16[1,1024,1024]{2,1,0:T(8,128)(2,1)}, u32[]{:S(2)}) copy-start(bf16[1,1024,1024]{2,1,0:T(8,128)(2,1)} %param.4) | copy-start | bytes 6291460
  35.6 12.0 %copy-start.2 = (f32[2,256]{1,0:T(2,128)S(1)}, f32[2,256]{1,0:T(2,128)}, u32[]{:S(2)}) copy-start(f32[2,256]{1,0:T(2,128)} %param.7) | copy-start | bytes 6148
  35.6 14.6 %copy-start.3 = (s32[8,1]{0,1:T(1,128)S(1)}, s32[8,1]{0,1:T(1,128)}, u32[]{:S(2)}) copy-start(s32[8,1]{0,1:T(1,128)} %param.6) | copy-start | bytes 100
  35.6 14.6 %copy-start.1 = (s32[16]{0:T(128)S(1)}, s32[16]{0:T(128)}, u32[]{:S(2)}) copy-start(s32[16]{0:T(128)} %lags_ref.1) | copy-start | bytes 196
  35.6 64.4 %all-to-all-start = ((bf16[128,8,2048]{2,1,0:T(8,128)(2,1)}), bf16[128,8,2048]{2,1,0:T(8,128)(2,1)}, u32[]{:S(2)}, u32[]{:S(2)}) async-start(bf16[128,8,2048]{2,1,0:T(8,128)(2,1)} %fusion.12), calls=%async_computation | async-start | bytes 8388608 | tf_op jit(solution)/shard_map/all_to_all | solution.py:145
  47.6 3.3 %collective-permute-start = (f32[2,256]{1,0:T(2,128)S(1)}, f32[2,256]{1,0:T(2,128)S(1)}, u32[]{:S(2)}, u32[]{:S(2)}) collective-permute-start(f32[2,256]{1,0:T(2,128)S(1)} %copy-done.2), channel_id=1, source_target_pairs={{0,1},{1,2},{2,3},{3,0},{4,5},{5,6},{6,7},{7,4},{8,9},{9,10},{10,1... | collective-permute-start | bytes 6152 | tf_op jit(solution)/shard_map/ppermute | solution.py:167
  49.4 22.5 %collective-permute-start.1 = (f32[2,256]{1,0:T(2,128)S(1)}, f32[2,256]{1,0:T(2,128)S(1)}, u32[]{:S(2)}, u32[]{:S(2)}) collective-permute-start(f32[2,256]{1,0:T(2,128)S(1)} %copy-done.2), channel_id=1, source_target_pairs={{0,2},{1,3},{2,0},{3,1},{4,6},{5,7},{6,4},{7,5},{8,10},{9,11},{10,... | collective-permute-start | bytes 6152 | tf_op jit(solution)/shard_map/ppermute | solution.py:167
  50.1 21.8 %collective-permute-start.2 = (f32[2,256]{1,0:T(2,128)S(1)}, f32[2,256]{1,0:T(2,128)S(1)}, u32[]{:S(2)}, u32[]{:S(2)}) collective-permute-start(f32[2,256]{1,0:T(2,128)S(1)} %copy-done.2), channel_id=1, source_target_pairs={{0,3},{1,0},{2,1},{3,2},{4,7},{5,4},{6,5},{7,6},{8,11},{9,8},{10,9... | collective-permute-start | bytes 6152 | tf_op jit(solution)/shard_map/ppermute | solution.py:167
  123.6 16.0 %all-to-all-start.1 = ((f32[128,2,17]{2,1,0:T(2,128)}), f32[128,2,17]{2,1,0:T(2,128)S(1)}, u32[]{:S(2)}, u32[]{:S(2)}) async-start(f32[128,2,17]{2,1,0:T(2,128)} %copy.11), calls=%async_computation.1 | async-start | bytes 262144 | tf_op jit(solution)/shard_map/all_to_all | solution.py:159

commit v14 on v11

--- a/solution.py
+++ b/solution.py
@@ -25,7 +25,7 @@
     ).astype(jnp.bfloat16)
 
 
-def structure_kernel(lags_ref, x_ref, out_ref, x32_ref):
+def structure_kernel(lags_ref, x_ref, out_ref, rows_ref, x32_ref):
     frames_all = x_ref.shape[0]
     pixels = out_ref.shape[2]
 
@@ -51,7 +51,12 @@
         blocks = count // UNROLL
         acc = lax.fori_loop(0, blocks, step_block, jnp.zeros(x32_ref.shape[1:], jnp.float32))
         acc = lax.fori_loop(blocks * UNROLL, count, step, acc)
-        out_ref[l] = (acc[:, :pixels] + acc[:, pixels:]) / count.astype(jnp.float32)
+        value = (acc[:, :pixels] + acc[:, pixels:]) / count.astype(jnp.float32)
+        out_ref[l] = value
+        part = value[:, 0:128]
+        for i in range(1, pixels // 128):
+            part = part + value[:, i * 128:(i + 1) * 128]
+        rows_ref[l] = part
         return carry
 
     lax.fori_loop(0, lags_ref.shape[0], one_lag, 0)
@@ -62,12 +67,15 @@
     nlag = lag_list.shape[0]
     return pl.pallas_call(
         structure_kernel,
-        out_shape=jax.ShapeDtypeStruct((nlag, rows, width // 2), jnp.float32),
+        out_shape=(
+            jax.ShapeDtypeStruct((nlag, rows, width // 2), jnp.float32),
+            jax.ShapeDtypeStruct((nlag, rows, 128), jnp.float32),
+        ),
         in_specs=[
             pl.BlockSpec(memory_space=pltpu.SMEM),
             pl.BlockSpec(memory_space=pltpu.VMEM),
         ],
-        out_specs=pl.BlockSpec(memory_space=pltpu.VMEM),
+        out_specs=(pl.BlockSpec(memory_space=pltpu.VMEM), pl.BlockSpec(memory_space=pltpu.VMEM)),
         scratch_shapes=[
             pltpu.VMEM((frames_all, rows, width), jnp.float32),
         ],
@@ -118,6 +126,7 @@
     sin_part = table[:, pixels:]
     width = pixels // CHUNKS
     pieces_out = []
+    partials = []
     for k in range(CHUNKS):
         cols = slice(k * width, (k + 1) * width)
         mixing = jnp.stack([
@@ -127,7 +136,9 @@
         spectrum = jnp.einsum("ypk,pyj->kj", row_transform, mixing, preferred_element_type=jnp.float32)
         spectrum = spectrum.astype(jnp.bfloat16).reshape(devices, pixels // devices, 2 * width)
         gathered = lax.all_to_all(spectrum, ("tm", "qband"), 0, 0, tiled=True)
-        pieces_out.append(structure_block(gathered, lag_list))
+        piece, partial = structure_block(gathered, lag_list)
+        pieces_out.append(piece)
+        partials.append(partial)
     structure = jnp.concatenate(pieces_out, axis=2)
 
     bands_dev = decay_rates.shape[0]
@@ -137,7 +148,7 @@
     )[None, :]
     dest_hot = (band_index[:, 0][None, None, :] == dest_band[:, :, None]).astype(jnp.float32)
     dest_counts = jnp.sum(dest_hot, axis=2, keepdims=True)
-    row_sums = jnp.sum(structure, axis=2)
+    row_sums = jnp.sum(jnp.concatenate(partials, axis=2), axis=2)
     dest_totals = jnp.einsum("dbr,lr->dbl", dest_hot, row_sums, precision=lax.Precision.HIGHEST)
     per_dest = jnp.concatenate([dest_totals, dest_counts], axis=2)
     received = lax.all_to_all(per_dest, ("tm", "qband"), 0, 0, tiled=True)

time: 147 us -> 146 us (level)
  no operation moved by 1% of the time
where the time goes in v14:
time: 146 us
  waiting for transfers between devices  59.2 us (41%)
  Pallas kernels  28 us (19%)
  other arithmetic  20.8 us (14%)
  starting transfers between devices  20.3 us (14%)
  matrix products  15.4 us (11%)
  local copies, waits for them, and re-layouts  1.47 us (1%)
    all_to_all x1, waiting for transfers between devices, on_device(): gathered = lax.all_to_all(spectrum, ('tm', 'qband'), 0, 0, tiled=True)  28.1 us
    ppermute x3, waiting for transfers between devices, on_device(): lax.ppermute(decay_rates, 'qband', [(j, (j + s) % ring) for j in range(ri...  21.7 us
    another operation x1, other arithmetic  18.3 us
    pallas_call x1, Pallas kernels, structure_block(): pl.pallas_call(structure_kernel, out_shape=(jax.ShapeDtypeStruct((nlag, r...  15.5 us
    pallas_call x1, Pallas kernels, fit_bands(): pl.pallas_call(fit_kernel, out_shape=jax.ShapeDtypeStruct((bands, columns...  12.5 us
    all_to_all x1, starting transfers between devices, on_device(): gathered = lax.all_to_all(spectrum, ('tm', 'qband'), 0, 0, tiled=True)  11.9 us
    dot_general x1, matrix products, on_device(): jnp.einsum('ypk,pyj->kj', row_transform, mixing, preferred_element_type=j...  10.4 us
    all_to_all x1, waiting for transfers between devices, on_device(): received = lax.all_to_all(per_dest, ('tm', 'qband'), 0, 0, tiled=True)  9.44 us
  transfers between devices with their start and end apart: 5, of which 4 were waited for; matrix products, arithmetic and copies ran while one was open for 1% of the time, Pallas kernels for 0%

profile of v14, /device:TPU:1, one launch (start us, length us, event | category | flops | bytes accessed | tf_op | source)
XLA Modules:
  0.0 145.9 jit_solution(7082122624415641778)
XLA Ops:
  0.6 18.3 %multiply_convert_fusion = (bf16[1024,1024]{1,0:T(8,128)(2,1)S(1)}, bf16[1024,1024]{1,0:T(8,128)(2,1)S(1)}) fusion(), kind=kLoop, calls=%fused_computation.14 | loop fusion | flops 26214400 | bytes 4194304 | tf_op jit(solution)/shard_map/convert.1
  19.0 0.4 pad_maximum_fusion
  19.4 0.3 slice_negate_fusion
  19.7 4.9 %convolution_convert_fusion = bf16[2048,1024]{1,0:T(8,128)(2,1)S(1)} fusion(bf16[1024,2048]{1,0:T(8,128)(2,1)S(1)} %pad_maximum_fusion, bf16[1,1024,1024]{2,1,0:T(8,128)(2,1)S(1)} %copy-done), kind=kOutput, calls=%fused_computation.20 | convolution fusion | flops 4297064448 | bytes 10485760 | tf_op jit(solution)/shard_map/dot_general | solution.py:123
  24.6 0.4 maximum_bitcast_fusion
  25.0 10.4 %fusion.12 = bf16[128,8,2048]{2,1,0:T(8,128)(2,1)} fusion(bf16[1024,2,1024]{0,2,1:T(8,128)(2,1)S(1)} %bitcast.26, bf16[1,1024,2048]{2,1,0:T(8,128)(2,1)S(1)} %maximum_bitcast_fusion, bf16[1,1024,2048]{2,1,0:T(8,128)(2,1)S(1)} %bitcast.22), kind=kOutput, calls=%fused_computation.21 | convolution fusion | flops 8596226048 | bytes 16777216 | tf_op jit(solution)/shard_map/ypk,pyj->kj/dot_general | solution.py:136
  35.4 11.9 %all-to-all-start = ((bf16[128,8,2048]{2,1,0:T(8,128)(2,1)}), bf16[128,8,2048]{2,1,0:T(8,128)(2,1)}, u32[]{:S(2)}, u32[]{:S(2)}) async-start(bf16[128,8,2048]{2,1,0:T(8,128)(2,1)} %fusion.12), calls=%async_computation | async-start | bytes 8388608 | tf_op jit(solution)/shard_map/all_to_all | solution.py:138
  47.3 1.8 %collective-permute-start = (f32[2,256]{1,0:T(2,128)S(1)}, f32[2,256]{1,0:T(2,128)S(1)}, u32[]{:S(2)}, u32[]{:S(2)}) collective-permute-start(f32[2,256]{1,0:T(2,128)S(1)} %copy-done.2), channel_id=1, source_target_pairs={{0,1},{1,2},{2,3},{3,0},{4,5},{5,6},{6,7},{7,4},{8,9},{9,10},{10,1... | collective-permute-start | bytes 6152 | tf_op jit(solution)/shard_map/ppermute | solution.py:162
  49.2 0.7 collective-permute-start.1
  49.9 0.1 fusion.18
  50.0 0.6 collective-permute-done
  50.6 21.0 %collective-permute-done.1 = f32[2,256]{1,0:T(2,128)S(1)} collective-permute-done((f32[2,256]{1,0:T(2,128)S(1)}, f32[2,256]{1,0:T(2,128)S(1)}, u32[]{:S(2)}, u32[]{:S(2)}) %collective-permute-start.1) | collective-permute-done | bytes 2080 | tf_op jit(solution)/shard_map/ppermute | solution.py:162
  71.7 28.1 %all-to-all-done.x_ref = bf16[128,8,2048]{2,1,0:T(8,128)(2,1)} async-done(((bf16[128,8,2048]{2,1,0:T(8,128)(2,1)}), bf16[128,8,2048]{2,1,0:T(8,128)(2,1)}, u32[]{:S(2)}, u32[]{:S(2)}) %all-to-all-start) | async-done | bytes 4194336 | tf_op jit(solution)/shard_map/all_to_all | solution.py:138
  99.8 15.5 %shard_map.59 = (f32[16,8,1024]{2,1,0:T(8,128)}, f32[16,8,128]{2,1,0:T(8,128)S(1)}) custom-call(s32[16]{0:T(128)S(1)} %copy-done.1, bf16[128,8,2048]{2,1,0:T(8,128)(2,1)} %all-to-all-done.x_ref), custom_call_target="tpu_custom_call" | custom-call | tf_op jit(solution)/shard_map/pallas_call | solution.py:68
  115.3 0.1 reduce_sum.27
  115.4 0.2 fusion.16
  115.6 0.8 copy.11
  116.4 5.8 %all-to-all-start.1 = ((f32[128,2,17]{2,1,0:T(2,128)}), f32[128,2,17]{2,1,0:T(2,128)S(1)}, u32[]{:S(2)}, u32[]{:S(2)}) async-start(f32[128,2,17]{2,1,0:T(2,128)} %copy.11), calls=%async_computation.1 | async-start | bytes 262144 | tf_op jit(solution)/shard_map/all_to_all | solution.py:154
  122.2 0.7 subtract_multiply_fusion.k_ref
  122.9 9.4 %all-to-all-done.1 = f32[128,2,17]{2,1,0:T(2,128)S(1)} async-done(((f32[128,2,17]{2,1,0:T(2,128)}), f32[128,2,17]{2,1,0:T(2,128)S(1)}, u32[]{:S(2)}, u32[]{:S(2)}) %all-to-all-start.1) | async-done | bytes 17440 | tf_op jit(solution)/shard_map/all_to_all | solution.py:154
  132.4 0.1 reduce_sum.29
  132.5 0.2 multiply_reduce_fusion
  132.8 0.7 broadcast_in_dim.15.tgt_ref
  133.5 12.5 %shard_map.60 = f32[2,256]{1,0:T(2,128)} custom-call(f32[2,16,1024]{2,1,0:T(8,128)} %subtract_multiply_fusion.k_ref, f32[2,16,128]{2,1,0:T(8,128)} %broadcast_in_dim.15.tgt_ref), custom_call_target="tpu_custom_call" | custom-call | tf_op jit(solution)/shard_map/pallas_call | solution.py:113
  (16 shorter events, 0.1 us)
Async XLA Ops:
  0.6 19.1 %copy-start = (bf16[1,1024,1024]{2,1,0:T(8,128)(2,1)S(1)}, bf16[1,1024,1024]{2,1,0:T(8,128)(2,1)}, u32[]{:S(2)}) copy-start(bf16[1,1024,1024]{2,1,0:T(8,128)(2,1)} %param.4) | copy-start | bytes 6291460
  35.4 12.0 %copy-start.2 = (f32[2,256]{1,0:T(2,128)S(1)}, f32[2,256]{1,0:T(2,128)}, u32[]{:S(2)}) copy-start(f32[2,256]{1,0:T(2,128)} %param.7) | copy-start | bytes 6148
  35.4 14.5 %copy-start.3 = (s32[8,1]{0,1:T(1,128)S(1)}, s32[8,1]{0,1:T(1,128)}, u32[]{:S(2)}) copy-start(s32[8,1]{0,1:T(1,128)} %param.6) | copy-start | bytes 100
  35.4 14.6 %copy-start.1 = (s32[16]{0:T(128)S(1)}, s32[16]{0:T(128)}, u32[]{:S(2)}) copy-start(s32[16]{0:T(128)} %lags_ref.1) | copy-start | bytes 196
  35.4 64.4 %all-to-all-start = ((bf16[128,8,2048]{2,1,0:T(8,128)(2,1)}), bf16[128,8,2048]{2,1,0:T(8,128)(2,1)}, u32[]{:S(2)}, u32[]{:S(2)}) async-start(bf16[128,8,2048]{2,1,0:T(8,128)(2,1)} %fusion.12), calls=%async_computation | async-start | bytes 8388608 | tf_op jit(solution)/shard_map/all_to_all | solution.py:138
  47.3 3.3 %collective-permute-start = (f32[2,256]{1,0:T(2,128)S(1)}, f32[2,256]{1,0:T(2,128)S(1)}, u32[]{:S(2)}, u32[]{:S(2)}) collective-permute-start(f32[2,256]{1,0:T(2,128)S(1)} %copy-done.2), channel_id=1, source_target_pairs={{0,1},{1,2},{2,3},{3,0},{4,5},{5,6},{6,7},{7,4},{8,9},{9,10},{10,1... | collective-permute-start | bytes 6152 | tf_op jit(solution)/shard_map/ppermute | solution.py:162
  49.2 22.5 %collective-permute-start.1 = (f32[2,256]{1,0:T(2,128)S(1)}, f32[2,256]{1,0:T(2,128)S(1)}, u32[]{:S(2)}, u32[]{:S(2)}) collective-permute-start(f32[2,256]{1,0:T(2,128)S(1)} %copy-done.2), channel_id=1, source_target_pairs={{0,2},{1,3},{2,0},{3,1},{4,6},{5,7},{6,4},{7,5},{8,10},{9,11},{10,... | collective-permute-start | bytes 6152 | tf_op jit(solution)/shard_map/ppermute | solution.py:162
  49.9 21.8 %collective-permute-start.2 = (f32[2,256]{1,0:T(2,128)S(1)}, f32[2,256]{1,0:T(2,128)S(1)}, u32[]{:S(2)}, u32[]{:S(2)}) collective-permute-start(f32[2,256]{1,0:T(2,128)S(1)} %copy-done.2), channel_id=1, source_target_pairs={{0,3},{1,0},{2,1},{3,2},{4,7},{5,4},{6,5},{7,6},{8,11},{9,8},{10,9... | collective-permute-start | bytes 6152 | tf_op jit(solution)/shard_map/ppermute | solution.py:162
  116.4 16.0 %all-to-all-start.1 = ((f32[128,2,17]{2,1,0:T(2,128)}), f32[128,2,17]{2,1,0:T(2,128)S(1)}, u32[]{:S(2)}, u32[]{:S(2)}) async-start(f32[128,2,17]{2,1,0:T(2,128)} %copy.11), calls=%async_computation.1 | async-start | bytes 262144 | tf_op jit(solution)/shard_map/all_to_all | solution.py:154

commit v15 on v14

--- a/solution.py
+++ b/solution.py
@@ -109,7 +109,7 @@
 
 def fit_bands(kernel, target, columns):
     bands, lags, bins = kernel.shape
-    tgt = jnp.broadcast_to(target[:, :, None], (bands, lags, 128))
+    tgt = target[:, :, None]
     return pl.pallas_call(
         fit_kernel,
         out_shape=jax.ShapeDtypeStruct((bands, columns), jnp.float32),

time: 146 us -> 147 us (level)
  no operation moved by 1% of the time
where the time goes in v15:
time: 147 us; the launch traced here: 146 us
  waiting for transfers between devices  59.2 us (40%)
  Pallas kernels  28.5 us (19%)
  other arithmetic  20.8 us (14%)
  starting transfers between devices  20.3 us (14%)
  matrix products  15.4 us (10%)
  local copies, waits for them, and re-layouts  1.49 us (1%)
    all_to_all x1, waiting for transfers between devices, on_device(): gathered = lax.all_to_all(spectrum, ('tm', 'qband'), 0, 0, tiled=True)  28.1 us
    ppermute x3, waiting for transfers between devices, on_device(): lax.ppermute(decay_rates, 'qband', [(j, (j + s) % ring) for j in range(ri...  21.7 us
    another operation x1, other arithmetic  18.3 us
    pallas_call x1, Pallas kernels, structure_block(): pl.pallas_call(structure_kernel, out_shape=(jax.ShapeDtypeStruct((nlag, r...  16 us
    pallas_call x1, Pallas kernels, fit_bands(): pl.pallas_call(fit_kernel, out_shape=jax.ShapeDtypeStruct((bands, columns...  12.5 us
    all_to_all x1, starting transfers between devices, on_device(): gathered = lax.all_to_all(spectrum, ('tm', 'qband'), 0, 0, tiled=True)  11.9 us
    dot_general x1, matrix products, on_device(): jnp.einsum('ypk,pyj->kj', row_transform, mixing, preferred_element_type=j...  10.4 us
    all_to_all x1, waiting for transfers between devices, on_device(): received = lax.all_to_all(per_dest, ('tm', 'qband'), 0, 0, tiled=True)  9.44 us
  transfers between devices with their start and end apart: 5, of which 4 were waited for; matrix products, arithmetic and copies ran while one was open for 1% of the time, Pallas kernels for 0%

profile of v15, /device:TPU:1, one launch (start us, length us, event | category | flops | bytes accessed | tf_op | source)
XLA Modules:
  0.0 146.4 jit_solution(5479836599754026898)
XLA Ops:
  0.6 18.3 %multiply_convert_fusion = (bf16[1024,1024]{1,0:T(8,128)(2,1)S(1)}, bf16[1024,1024]{1,0:T(8,128)(2,1)S(1)}) fusion(), kind=kLoop, calls=%fused_computation.14 | loop fusion | flops 26214400 | bytes 4194304 | tf_op jit(solution)/shard_map/convert.1
  19.0 0.4 pad_maximum_fusion
  19.4 0.3 slice_negate_fusion
  19.7 4.9 %convolution_convert_fusion = bf16[2048,1024]{1,0:T(8,128)(2,1)S(1)} fusion(bf16[1024,2048]{1,0:T(8,128)(2,1)S(1)} %pad_maximum_fusion, bf16[1,1024,1024]{2,1,0:T(8,128)(2,1)S(1)} %copy-done), kind=kOutput, calls=%fused_computation.20 | convolution fusion | flops 4297064448 | bytes 10485760 | tf_op jit(solution)/shard_map/dot_general | solution.py:123
  24.6 0.4 maximum_bitcast_fusion
  25.0 10.4 %fusion.12 = bf16[128,8,2048]{2,1,0:T(8,128)(2,1)} fusion(bf16[1024,2,1024]{0,2,1:T(8,128)(2,1)S(1)} %bitcast.28, bf16[1,1024,2048]{2,1,0:T(8,128)(2,1)S(1)} %maximum_bitcast_fusion, bf16[1,1024,2048]{2,1,0:T(8,128)(2,1)S(1)} %bitcast.24), kind=kOutput, calls=%fused_computation.21 | convolution fusion | flops 8596226048 | bytes 16777216 | tf_op jit(solution)/shard_map/ypk,pyj->kj/dot_general | solution.py:136
  35.4 11.9 %all-to-all-start = ((bf16[128,8,2048]{2,1,0:T(8,128)(2,1)}), bf16[128,8,2048]{2,1,0:T(8,128)(2,1)}, u32[]{:S(2)}, u32[]{:S(2)}) async-start(bf16[128,8,2048]{2,1,0:T(8,128)(2,1)} %fusion.12), calls=%async_computation | async-start | bytes 8388608 | tf_op jit(solution)/shard_map/all_to_all | solution.py:138
  47.3 1.8 %collective-permute-start = (f32[2,256]{1,0:T(2,128)S(1)}, f32[2,256]{1,0:T(2,128)S(1)}, u32[]{:S(2)}, u32[]{:S(2)}) collective-permute-start(f32[2,256]{1,0:T(2,128)S(1)} %copy-done.2), channel_id=1, source_target_pairs={{0,1},{1,2},{2,3},{3,0},{4,5},{5,6},{6,7},{7,4},{8,9},{9,10},{10,1... | collective-permute-start | bytes 6152 | tf_op jit(solution)/shard_map/ppermute | solution.py:162
  49.2 0.7 collective-permute-start.1
  49.9 0.1 fusion.18
  50.0 0.6 collective-permute-done
  50.6 21.0 %collective-permute-done.1 = f32[2,256]{1,0:T(2,128)S(1)} collective-permute-done((f32[2,256]{1,0:T(2,128)S(1)}, f32[2,256]{1,0:T(2,128)S(1)}, u32[]{:S(2)}, u32[]{:S(2)}) %collective-permute-start.1) | collective-permute-done | bytes 2080 | tf_op jit(solution)/shard_map/ppermute | solution.py:162
  71.7 28.1 %all-to-all-done.x_ref = bf16[128,8,2048]{2,1,0:T(8,128)(2,1)} async-done(((bf16[128,8,2048]{2,1,0:T(8,128)(2,1)}), bf16[128,8,2048]{2,1,0:T(8,128)(2,1)}, u32[]{:S(2)}, u32[]{:S(2)}) %all-to-all-start) | async-done | bytes 4194336 | tf_op jit(solution)/shard_map/all_to_all | solution.py:138
  99.8 16.0 %shard_map.59 = (f32[16,8,1024]{2,1,0:T(8,128)}, f32[16,8,128]{2,1,0:T(8,128)S(1)}) custom-call(s32[16]{0:T(128)S(1)} %copy-done.1, bf16[128,8,2048]{2,1,0:T(8,128)(2,1)} %all-to-all-done.x_ref), custom_call_target="tpu_custom_call" | custom-call | tf_op jit(solution)/shard_map/pallas_call | solution.py:68
  115.8 0.1 reduce_sum.27
  115.9 0.2 fusion.16
  116.1 0.8 copy.9
  116.8 5.8 %all-to-all-start.1 = ((f32[128,2,17]{2,1,0:T(2,128)}), f32[128,2,17]{2,1,0:T(2,128)S(1)}, u32[]{:S(2)}, u32[]{:S(2)}) async-start(f32[128,2,17]{2,1,0:T(2,128)} %copy.9), calls=%async_computation.1 | async-start | bytes 262144 | tf_op jit(solution)/shard_map/all_to_all | solution.py:154
  122.6 0.7 subtract_multiply_fusion.k_ref
  123.4 9.4 %all-to-all-done.1 = f32[128,2,17]{2,1,0:T(2,128)S(1)} async-done(((f32[128,2,17]{2,1,0:T(2,128)}), f32[128,2,17]{2,1,0:T(2,128)S(1)}, u32[]{:S(2)}, u32[]{:S(2)}) %all-to-all-start.1) | async-done | bytes 17440 | tf_op jit(solution)/shard_map/all_to_all | solution.py:154
  132.8 0.1 reduce_sum.29
  133.0 0.2 multiply_reduce_fusion
  133.2 0.7 copy.10.tgt_ref
  134.0 12.5 %shard_map.60 = f32[2,256]{1,0:T(2,128)} custom-call(f32[2,16,1024]{2,1,0:T(8,128)} %subtract_multiply_fusion.k_ref, f32[2,16,1]{2,1,0:T(8,128)} %copy.10.tgt_ref), custom_call_target="tpu_custom_call" | custom-call | tf_op jit(solution)/shard_map/pallas_call | solution.py:113
  (16 shorter events, 0.1 us)
Async XLA Ops:
  0.6 19.1 %copy-start = (bf16[1,1024,1024]{2,1,0:T(8,128)(2,1)S(1)}, bf16[1,1024,1024]{2,1,0:T(8,128)(2,1)}, u32[]{:S(2)}) copy-start(bf16[1,1024,1024]{2,1,0:T(8,128)(2,1)} %param.4) | copy-start | bytes 6291460
  35.4 12.0 %copy-start.2 = (f32[2,256]{1,0:T(2,128)S(1)}, f32[2,256]{1,0:T(2,128)}, u32[]{:S(2)}) copy-start(f32[2,256]{1,0:T(2,128)} %param.7) | copy-start | bytes 6148
  35.4 14.5 %copy-start.3 = (s32[8,1]{0,1:T(1,128)S(1)}, s32[8,1]{0,1:T(1,128)}, u32[]{:S(2)}) copy-start(s32[8,1]{0,1:T(1,128)} %param.6) | copy-start | bytes 100
  35.4 14.6 %copy-start.1 = (s32[16]{0:T(128)S(1)}, s32[16]{0:T(128)}, u32[]{:S(2)}) copy-start(s32[16]{0:T(128)} %lags_ref.1) | copy-start | bytes 196
  35.4 64.4 %all-to-all-start = ((bf16[128,8,2048]{2,1,0:T(8,128)(2,1)}), bf16[128,8,2048]{2,1,0:T(8,128)(2,1)}, u32[]{:S(2)}, u32[]{:S(2)}) async-start(bf16[128,8,2048]{2,1,0:T(8,128)(2,1)} %fusion.12), calls=%async_computation | async-start | bytes 8388608 | tf_op jit(solution)/shard_map/all_to_all | solution.py:138
  47.3 3.3 %collective-permute-start = (f32[2,256]{1,0:T(2,128)S(1)}, f32[2,256]{1,0:T(2,128)S(1)}, u32[]{:S(2)}, u32[]{:S(2)}) collective-permute-start(f32[2,256]{1,0:T(2,128)S(1)} %copy-done.2), channel_id=1, source_target_pairs={{0,1},{1,2},{2,3},{3,0},{4,5},{5,6},{6,7},{7,4},{8,9},{9,10},{10,1... | collective-permute-start | bytes 6152 | tf_op jit(solution)/shard_map/ppermute | solution.py:162
  49.2 22.5 %collective-permute-start.1 = (f32[2,256]{1,0:T(2,128)S(1)}, f32[2,256]{1,0:T(2,128)S(1)}, u32[]{:S(2)}, u32[]{:S(2)}) collective-permute-start(f32[2,256]{1,0:T(2,128)S(1)} %copy-done.2), channel_id=1, source_target_pairs={{0,2},{1,3},{2,0},{3,1},{4,6},{5,7},{6,4},{7,5},{8,10},{9,11},{10,... | collective-permute-start | bytes 6152 | tf_op jit(solution)/shard_map/ppermute | solution.py:162
  49.9 21.8 %collective-permute-start.2 = (f32[2,256]{1,0:T(2,128)S(1)}, f32[2,256]{1,0:T(2,128)S(1)}, u32[]{:S(2)}, u32[]{:S(2)}) collective-permute-start(f32[2,256]{1,0:T(2,128)S(1)} %copy-done.2), channel_id=1, source_target_pairs={{0,3},{1,0},{2,1},{3,2},{4,7},{5,4},{6,5},{7,6},{8,11},{9,8},{10,9... | collective-permute-start | bytes 6152 | tf_op jit(solution)/shard_map/ppermute | solution.py:162
  116.8 16.0 %all-to-all-start.1 = ((f32[128,2,17]{2,1,0:T(2,128)}), f32[128,2,17]{2,1,0:T(2,128)S(1)}, u32[]{:S(2)}, u32[]{:S(2)}) async-start(f32[128,2,17]{2,1,0:T(2,128)} %copy.9), calls=%async_computation.1 | async-start | bytes 262144 | tf_op jit(solution)/shard_map/all_to_all | solution.py:154

commit v16 on v15

--- a/solution.py
+++ b/solution.py
@@ -33,7 +33,7 @@
         x32_ref[t] = x_ref[t].astype(jnp.float32)
         return carry
 
-    lax.fori_loop(0, frames_all, convert, 0)
+    lax.fori_loop(0, frames_all, convert, 0, unroll=8)
 
     def one_lag(l, carry):
         lag = lags_ref[l]

time: 147 us -> 146 us (level)
  Pallas kernels: 28.5 us -> 27 us
    pallas_call x1, Pallas kernels: 16 us -> 14.5 us  [structure_block(): pl.pallas_call(structure_kernel, out_shape=(jax.ShapeDtypeStruct((nlag, r...]
where the time goes in v16:
time: 146 us; the launch traced here: 145 us
  waiting for transfers between devices  59.2 us (41%)
  Pallas kernels  27 us (18%)
  other arithmetic  20.8 us (14%)
  starting transfers between devices  20.3 us (14%)
  matrix products  15.4 us (11%)
  local copies, waits for them, and re-layouts  1.49 us (1%)
    all_to_all x1, waiting for transfers between devices, on_device(): gathered = lax.all_to_all(spectrum, ('tm', 'qband'), 0, 0, tiled=True)  28.1 us
    ppermute x3, waiting for transfers between devices, on_device(): lax.ppermute(decay_rates, 'qband', [(j, (j + s) % ring) for j in range(ri...  21.7 us
    another operation x1, other arithmetic  18.3 us
    pallas_call x1, Pallas kernels, structure_block(): pl.pallas_call(structure_kernel, out_shape=(jax.ShapeDtypeStruct((nlag, r...  14.5 us
    pallas_call x1, Pallas kernels, fit_bands(): pl.pallas_call(fit_kernel, out_shape=jax.ShapeDtypeStruct((bands, columns...  12.5 us
    all_to_all x1, starting transfers between devices, on_device(): gathered = lax.all_to_all(spectrum, ('tm', 'qband'), 0, 0, tiled=True)  11.9 us
    dot_general x1, matrix products, on_device(): jnp.einsum('ypk,pyj->kj', row_transform, mixing, preferred_element_type=j...  10.4 us
    all_to_all x1, waiting for transfers between devices, on_device(): received = lax.all_to_all(per_dest, ('tm', 'qband'), 0, 0, tiled=True)  9.44 us
  transfers between devices with their start and end apart: 5, of which 4 were waited for; matrix products, arithmetic and copies ran while one was open for 1% of the time, Pallas kernels for 0%

profile of v16, /device:TPU:1, one launch (start us, length us, event | category | flops | bytes accessed | tf_op | source)
XLA Modules:
  0.0 144.9 jit_solution(12500576522282773735)
XLA Ops:
  0.6 18.3 %multiply_convert_fusion = (bf16[1024,1024]{1,0:T(8,128)(2,1)S(1)}, bf16[1024,1024]{1,0:T(8,128)(2,1)S(1)}) fusion(), kind=kLoop, calls=%fused_computation.14 | loop fusion | flops 26214400 | bytes 4194304 | tf_op jit(solution)/shard_map/convert.1
  19.0 0.4 pad_maximum_fusion
  19.4 0.3 slice_negate_fusion
  19.7 4.9 %convolution_convert_fusion = bf16[2048,1024]{1,0:T(8,128)(2,1)S(1)} fusion(bf16[1024,2048]{1,0:T(8,128)(2,1)S(1)} %pad_maximum_fusion, bf16[1,1024,1024]{2,1,0:T(8,128)(2,1)S(1)} %copy-done), kind=kOutput, calls=%fused_computation.20 | convolution fusion | flops 4297064448 | bytes 10485760 | tf_op jit(solution)/shard_map/dot_general | solution.py:123
  24.6 0.4 maximum_bitcast_fusion
  25.0 10.4 %fusion.12 = bf16[128,8,2048]{2,1,0:T(8,128)(2,1)} fusion(bf16[1024,2,1024]{0,2,1:T(8,128)(2,1)S(1)} %bitcast.28, bf16[1,1024,2048]{2,1,0:T(8,128)(2,1)S(1)} %maximum_bitcast_fusion, bf16[1,1024,2048]{2,1,0:T(8,128)(2,1)S(1)} %bitcast.24), kind=kOutput, calls=%fused_computation.21 | convolution fusion | flops 8596226048 | bytes 16777216 | tf_op jit(solution)/shard_map/ypk,pyj->kj/dot_general | solution.py:136
  35.4 11.9 %all-to-all-start = ((bf16[128,8,2048]{2,1,0:T(8,128)(2,1)}), bf16[128,8,2048]{2,1,0:T(8,128)(2,1)}, u32[]{:S(2)}, u32[]{:S(2)}) async-start(bf16[128,8,2048]{2,1,0:T(8,128)(2,1)} %fusion.12), calls=%async_computation | async-start | bytes 8388608 | tf_op jit(solution)/shard_map/all_to_all | solution.py:138
  47.3 1.8 %collective-permute-start = (f32[2,256]{1,0:T(2,128)S(1)}, f32[2,256]{1,0:T(2,128)S(1)}, u32[]{:S(2)}, u32[]{:S(2)}) collective-permute-start(f32[2,256]{1,0:T(2,128)S(1)} %copy-done.2), channel_id=1, source_target_pairs={{0,1},{1,2},{2,3},{3,0},{4,5},{5,6},{6,7},{7,4},{8,9},{9,10},{10,1... | collective-permute-start | bytes 6152 | tf_op jit(solution)/shard_map/ppermute | solution.py:162
  49.2 0.7 collective-permute-start.1
  49.9 0.1 fusion.18
  50.0 0.6 collective-permute-done
  50.6 21.0 %collective-permute-done.1 = f32[2,256]{1,0:T(2,128)S(1)} collective-permute-done((f32[2,256]{1,0:T(2,128)S(1)}, f32[2,256]{1,0:T(2,128)S(1)}, u32[]{:S(2)}, u32[]{:S(2)}) %collective-permute-start.1) | collective-permute-done | bytes 2080 | tf_op jit(solution)/shard_map/ppermute | solution.py:162
  71.7 28.1 %all-to-all-done.x_ref = bf16[128,8,2048]{2,1,0:T(8,128)(2,1)} async-done(((bf16[128,8,2048]{2,1,0:T(8,128)(2,1)}), bf16[128,8,2048]{2,1,0:T(8,128)(2,1)}, u32[]{:S(2)}, u32[]{:S(2)}) %all-to-all-start) | async-done | bytes 4194336 | tf_op jit(solution)/shard_map/all_to_all | solution.py:138
  99.8 14.5 %shard_map.59 = (f32[16,8,1024]{2,1,0:T(8,128)}, f32[16,8,128]{2,1,0:T(8,128)S(1)}) custom-call(s32[16]{0:T(128)S(1)} %copy-done.1, bf16[128,8,2048]{2,1,0:T(8,128)(2,1)} %all-to-all-done.x_ref), custom_call_target="tpu_custom_call" | custom-call | tf_op jit(solution)/shard_map/pallas_call | solution.py:68
  114.3 0.1 reduce_sum.27
  114.4 0.2 fusion.16
  114.6 0.8 copy.9
  115.3 5.8 %all-to-all-start.1 = ((f32[128,2,17]{2,1,0:T(2,128)}), f32[128,2,17]{2,1,0:T(2,128)S(1)}, u32[]{:S(2)}, u32[]{:S(2)}) async-start(f32[128,2,17]{2,1,0:T(2,128)} %copy.9), calls=%async_computation.1 | async-start | bytes 262144 | tf_op jit(solution)/shard_map/all_to_all | solution.py:154
  121.1 0.7 subtract_multiply_fusion.k_ref
  121.9 9.4 %all-to-all-done.1 = f32[128,2,17]{2,1,0:T(2,128)S(1)} async-done(((f32[128,2,17]{2,1,0:T(2,128)}), f32[128,2,17]{2,1,0:T(2,128)S(1)}, u32[]{:S(2)}, u32[]{:S(2)}) %all-to-all-start.1) | async-done | bytes 17440 | tf_op jit(solution)/shard_map/all_to_all | solution.py:154
  131.3 0.1 reduce_sum.29
  131.5 0.2 multiply_reduce_fusion
  131.7 0.7 copy.10.tgt_ref
  132.4 12.5 %shard_map.60 = f32[2,256]{1,0:T(2,128)} custom-call(f32[2,16,1024]{2,1,0:T(8,128)} %subtract_multiply_fusion.k_ref, f32[2,16,1]{2,1,0:T(8,128)} %copy.10.tgt_ref), custom_call_target="tpu_custom_call" | custom-call | tf_op jit(solution)/shard_map/pallas_call | solution.py:113
  (16 shorter events, 0.1 us)
Async XLA Ops:
  0.6 19.1 %copy-start = (bf16[1,1024,1024]{2,1,0:T(8,128)(2,1)S(1)}, bf16[1,1024,1024]{2,1,0:T(8,128)(2,1)}, u32[]{:S(2)}) copy-start(bf16[1,1024,1024]{2,1,0:T(8,128)(2,1)} %param.4) | copy-start | bytes 6291460
  35.4 12.0 %copy-start.2 = (f32[2,256]{1,0:T(2,128)S(1)}, f32[2,256]{1,0:T(2,128)}, u32[]{:S(2)}) copy-start(f32[2,256]{1,0:T(2,128)} %param.7) | copy-start | bytes 6148
  35.4 14.5 %copy-start.3 = (s32[8,1]{0,1:T(1,128)S(1)}, s32[8,1]{0,1:T(1,128)}, u32[]{:S(2)}) copy-start(s32[8,1]{0,1:T(1,128)} %param.6) | copy-start | bytes 100
  35.4 14.6 %copy-start.1 = (s32[16]{0:T(128)S(1)}, s32[16]{0:T(128)}, u32[]{:S(2)}) copy-start(s32[16]{0:T(128)} %lags_ref.1) | copy-start | bytes 196
  35.4 64.4 %all-to-all-start = ((bf16[128,8,2048]{2,1,0:T(8,128)(2,1)}), bf16[128,8,2048]{2,1,0:T(8,128)(2,1)}, u32[]{:S(2)}, u32[]{:S(2)}) async-start(bf16[128,8,2048]{2,1,0:T(8,128)(2,1)} %fusion.12), calls=%async_computation | async-start | bytes 8388608 | tf_op jit(solution)/shard_map/all_to_all | solution.py:138
  47.3 3.3 %collective-permute-start = (f32[2,256]{1,0:T(2,128)S(1)}, f32[2,256]{1,0:T(2,128)S(1)}, u32[]{:S(2)}, u32[]{:S(2)}) collective-permute-start(f32[2,256]{1,0:T(2,128)S(1)} %copy-done.2), channel_id=1, source_target_pairs={{0,1},{1,2},{2,3},{3,0},{4,5},{5,6},{6,7},{7,4},{8,9},{9,10},{10,1... | collective-permute-start | bytes 6152 | tf_op jit(solution)/shard_map/ppermute | solution.py:162
  49.2 22.5 %collective-permute-start.1 = (f32[2,256]{1,0:T(2,128)S(1)}, f32[2,256]{1,0:T(2,128)S(1)}, u32[]{:S(2)}, u32[]{:S(2)}) collective-permute-start(f32[2,256]{1,0:T(2,128)S(1)} %copy-done.2), channel_id=1, source_target_pairs={{0,2},{1,3},{2,0},{3,1},{4,6},{5,7},{6,4},{7,5},{8,10},{9,11},{10,... | collective-permute-start | bytes 6152 | tf_op jit(solution)/shard_map/ppermute | solution.py:162
  49.9 21.8 %collective-permute-start.2 = (f32[2,256]{1,0:T(2,128)S(1)}, f32[2,256]{1,0:T(2,128)S(1)}, u32[]{:S(2)}, u32[]{:S(2)}) collective-permute-start(f32[2,256]{1,0:T(2,128)S(1)} %copy-done.2), channel_id=1, source_target_pairs={{0,3},{1,0},{2,1},{3,2},{4,7},{5,4},{6,5},{7,6},{8,11},{9,8},{10,9... | collective-permute-start | bytes 6152 | tf_op jit(solution)/shard_map/ppermute | solution.py:162
  115.3 16.0 %all-to-all-start.1 = ((f32[128,2,17]{2,1,0:T(2,128)}), f32[128,2,17]{2,1,0:T(2,128)S(1)}, u32[]{:S(2)}, u32[]{:S(2)}) async-start(f32[128,2,17]{2,1,0:T(2,128)} %copy.9), calls=%async_computation.1 | async-start | bytes 262144 | tf_op jit(solution)/shard_map/all_to_all | solution.py:154
